TPU v7x, 256 devices: a whole 4x4x8 slice. The times are simulated.
256 devices in a mesh: dp: 8 (over y, x_hi), expert: 8 (over z), tensor: 4 (over x_lo, core).
Axes of the slice: x: 4 (x_hi: 2, x_lo: 2; x = x_hi * 2 + x_lo), y: 4, z: 8, core: 2. Of those that a mesh axis runs over, the one named last changes fastest.
Arguments:
- tokens: bfloat16 [4096, 2048], P(('dp', 'expert', 'tensor')), may hold values from -6 to 6
- cotangent: bfloat16 [4096, 2048], P(('dp', 'expert', 'tensor')), may hold values from -3 to 3
- routes: int32 [4096, 2], P(('dp', 'expert', 'tensor')), may hold values from 0 to 7, all different within a row; in each aligned block of 16 rows (0 to 15, 16 to 31, ...) at most 5 rows name the same one
- weight_codes: int32 [4096, 2], P(('dp', 'expert', 'tensor')), may hold values from 16 to 256
- dense_gate: bfloat16 [2048, 8192], P('expert', ('dp', 'tensor')), may hold values from -0.125 to 0.125
- dense_up: bfloat16 [2048, 8192], P('expert', ('dp', 'tensor')), may hold values from -0.125 to 0.125
- dense_down_t: bfloat16 [2048, 8192], P('expert', ('dp', 'tensor')), may hold values from -0.0625 to 0.0625
Outputs:
- mixed: bfloat16 [4096, 2048], P(('dp', 'expert', 'tensor'))
- input_grad: bfloat16 [4096, 2048], P(('dp', 'expert', 'tensor'))
- grad_gate: bfloat16 [8, 2048, 8192], P('expert', None, ('dp', 'tensor'))
- grad_up: bfloat16 [8, 2048, 8192], P('expert', None, ('dp', 'tensor'))
- grad_down_t: bfloat16 [8, 2048, 8192], P('expert', None, ('dp', 'tensor'))
Inputs may be any that keep to these rules, and one draw needn't show every extreme that they name: `routes`: each row names two different experts; the rows of one device name each expert at most 5 times.
All inputs are finite; a program needn't handle non-finite values.
Results may differ from a plain program's by a relative error of at most 0.02.
Values may be sent and summed in bfloat16 or wider, within the bound.
No kernel may reach another device: no remote copies, remote signals or barrier semaphores. Data moves between devices by JAX's collectives and lax.ppermute only.
A program may use at most 128 MiB of HBM per device.

v0:
```python
import jax
import jax.numpy as jnp
from jax import lax
from jax.sharding import PartitionSpec as P


def silu_parts(gate_pre):
    sigmoid_val = jax.nn.sigmoid(gate_pre)
    return (gate_pre * sigmoid_val, sigmoid_val * (1.0 + gate_pre * (1.0 - sigmoid_val)))


def contract_rows(left_side, right_side):
    return lax.dot_general(
        left_side, right_side, (((0,), (0,)), ((), ())), preferred_element_type=jnp.float32
    )


def contract_cols(left_side, right_side):
    return lax.dot_general(
        left_side, right_side, (((1,), (1,)), ((), ())), preferred_element_type=jnp.float32
    )


def expert_rows(rows_x, rows_dy, rows_code, gate_cols, up_cols, down_cols):
    gate_pre = jnp.dot(rows_x, gate_cols, preferred_element_type=jnp.float32)
    up_pre = jnp.dot(rows_x, up_cols, preferred_element_type=jnp.float32)
    activation, act_slope = silu_parts(gate_pre)
    hidden = (activation * up_pre).astype(jnp.bfloat16)
    code_scale = rows_code.astype(jnp.float32) / 256.0
    scaled = (code_scale[:, None] * rows_dy.astype(jnp.float32)).astype(jnp.bfloat16)
    hidden_grad = jnp.dot(scaled, down_cols, preferred_element_type=jnp.float32)
    gate_grad = (hidden_grad * up_pre * act_slope).astype(jnp.bfloat16)
    up_grad = (hidden_grad * activation).astype(jnp.bfloat16)
    weight_grads = (
        contract_rows(rows_x, gate_grad),
        contract_rows(rows_x, up_grad),
        contract_rows(scaled, hidden),
    )
    return (hidden, gate_grad, up_grad, weight_grads)


def shards(tokens, cotangent, routes, weight_codes, dense_gate, dense_up, dense_down_t):
    gate_cols, up_cols, down_cols = (
        lax.all_gather(dense_gate, "expert", axis=0, tiled=True),
        lax.all_gather(dense_up, "expert", axis=0, tiled=True),
        lax.all_gather(dense_down_t, "expert", axis=0, tiled=True),
    )
    experts = lax.axis_size("expert")
    count_tok, model_width = tokens.shape
    capacity = 5 * count_tok // (2 * experts)
    slots_here = experts * capacity
    flat_route = routes.reshape(-1)
    flat_code = weight_codes.reshape(-1)
    onehot = (flat_route[:, None] == jnp.arange(experts, dtype=jnp.int32)[None, :]).astype(
        jnp.int32
    )
    earlier = jnp.cumsum(onehot, axis=0) - onehot
    slot_of = flat_route * capacity + jnp.sum(earlier * onehot, axis=1)
    placed = (slot_of[None, :] == jnp.arange(slots_here, dtype=jnp.int32)[:, None]).astype(
        jnp.int32
    )
    placed_tok = placed.reshape(slots_here, count_tok, 2).sum(axis=2)
    place_table = placed_tok.astype(jnp.bfloat16)
    send_x = jnp.dot(place_table, tokens, preferred_element_type=jnp.float32).astype(jnp.bfloat16)
    send_dy = jnp.dot(place_table, cotangent, preferred_element_type=jnp.float32).astype(
        jnp.bfloat16
    )
    send_code = jnp.sum(placed * flat_code[None, :], axis=1)
    parcel = (
        lax.all_to_all(
            send_x.reshape(experts, capacity, model_width),
            "expert",
            split_axis=0,
            concat_axis=0,
            tiled=True,
        ),
        lax.all_to_all(
            send_dy.reshape(experts, capacity, model_width),
            "expert",
            split_axis=0,
            concat_axis=0,
            tiled=True,
        ),
        lax.all_to_all(
            send_code.reshape(experts, capacity), "expert", split_axis=0, concat_axis=0, tiled=True
        ),
    )
    parcel = (
        lax.all_gather(parcel[0], ("dp", "tensor"), axis=0, tiled=True),
        lax.all_gather(parcel[1], ("dp", "tensor"), axis=0, tiled=True),
        lax.all_gather(parcel[2], ("dp", "tensor"), axis=0, tiled=True),
    )
    all_x = parcel[0].reshape(-1, model_width)
    all_dy = parcel[1].reshape(-1, model_width)
    all_code = parcel[2].reshape(-1)
    hidden, gate_grad, up_grad, weight_grads = expert_rows(
        all_x, all_dy, all_code, gate_cols, up_cols, down_cols
    )
    out_rows = lax.psum_scatter(
        contract_cols(hidden, down_cols).astype(jnp.bfloat16),
        ("dp", "tensor"),
        scatter_dimension=0,
        tiled=True,
    )
    grad_rows = lax.psum_scatter(
        (contract_cols(gate_grad, gate_cols) + contract_cols(up_grad, up_cols)).astype(
            jnp.bfloat16
        ),
        ("dp", "tensor"),
        scatter_dimension=0,
        tiled=True,
    )
    back_out, back_grad = (
        lax.all_to_all(
            out_rows.reshape(experts, capacity, model_width),
            "expert",
            split_axis=0,
            concat_axis=0,
            tiled=True,
        ),
        lax.all_to_all(
            grad_rows.reshape(experts, capacity, model_width),
            "expert",
            split_axis=0,
            concat_axis=0,
            tiled=True,
        ),
    )
    code_scale = flat_code.astype(jnp.float32) / 256.0
    weighted = (
        (placed.astype(jnp.float32) * code_scale[None, :])
        .reshape(slots_here, count_tok, 2)
        .sum(axis=2)
    )
    mixed = lax.dot_general(
        weighted,
        back_out.reshape(slots_here, model_width).astype(jnp.float32),
        (((0,), (0,)), ((), ())),
        precision=lax.Precision.HIGHEST,
        preferred_element_type=jnp.float32,
    ).astype(jnp.bfloat16)
    input_grad = contract_rows(place_table, back_grad.reshape(slots_here, model_width)).astype(
        jnp.bfloat16
    )
    grad_gate = weight_grads[0].astype(jnp.bfloat16)[None]
    grad_up = weight_grads[1].astype(jnp.bfloat16)[None]
    grad_down_t = weight_grads[2].astype(jnp.bfloat16)[None]
    return (mixed, input_grad, grad_gate, grad_up, grad_down_t)


def solution(mesh):
    placed = (
        P(("dp", "expert", "tensor"), None),
        P(("dp", "expert", "tensor"), None),
        P(("dp", "expert", "tensor"), None),
        P(("dp", "expert", "tensor"), None),
        P("expert", ("dp", "tensor")),
        P("expert", ("dp", "tensor")),
        P("expert", ("dp", "tensor")),
    )
    return jax.shard_map(
        shards,
        mesh=mesh,
        in_specs=placed,
        out_specs=(
            P(("dp", "expert", "tensor"), None),
            P(("dp", "expert", "tensor"), None),
            P("expert", None, ("dp", "tensor")),
            P("expert", None, ("dp", "tensor")),
            P("expert", None, ("dp", "tensor")),
        ),
        check_vma=False,
    )
```

profile of v0, /device:TPU:32, one launch (start us, length us, event | category | flops | bytes accessed | tf_op | source)
XLA Modules:
  0.0 477.7 jit_solution(12512945700379093156)
XLA Ops:
  7.2 0.8 copy.52
  8.2 0.2 select_reduce_fusion.1
  8.5 0.1 copy.53
  8.6 0.7 multiply_add_fusion
  9.3 0.2 convolution_convert_fusion.5
  9.6 18.8 %all_to_all.32 = bf16[8,5,2048]{2,1,0:T(8,128)(2,1)S(1)} all-to-all(bf16[8,5,2048]{2,1,0:T(8,128)(2,1)S(1)} %reshape.89), channel_id=1, replica_groups=mesh['dp'=8,'expert'=8,'tensor'=4] {'expert'}, dimensions={0} | all-to-all | bytes 327680 | tf_op jit(solution)/shard_map/all_to_all | solution.py:70
  28.4 0.8 copy.54
  29.3 1.1 convolution_convert_fusion.4
  30.4 12.9 %all_to_all.33 = bf16[8,5,2048]{2,1,0:T(8,128)(2,1)S(1)} all-to-all(bf16[8,5,2048]{2,1,0:T(8,128)(2,1)S(1)} %reshape.93), channel_id=1, replica_groups=mesh['dp'=8,'expert'=8,'tensor'=4] {'expert'}, dimensions={0} | all-to-all | bytes 327680 | tf_op jit(solution)/shard_map/all_to_all | solution.py:77
  43.4 0.8 copy.58
  44.2 0.7 all-gather.9.cloned.1.call-update
  45.0 0.5 all-gather.11.cloned.1.call-update
  45.5 0.5 all-gather.13.cloned.1.call-update
  46.1 0.8 copy.56
  47.0 0.1 select_reduce_fusion
  47.2 10.0 %all_to_all.34 = s32[8,1,5]{2,1,0:T(1,128)S(1)} all-to-all(s32[8,1,5]{2,1,0:T(1,128)S(1)} %bitcast.28), channel_id=1, replica_groups=mesh['dp'=8,'expert'=8,'tensor'=4] {'expert'}, dimensions={0} | all-to-all | bytes 320 | tf_op jit(solution)/shard_map/all_to_all | solution.py:84
  57.2 24.9 %all-gather = s32[256,1,5]{2,1,0:T(1,128)S(1)} all-gather(s32[8,1,5]{2,1,0:T(1,128)S(1)} %all_to_all.34), channel_id=2, replica_groups=mesh['dp'=8,'expert'=8,'tensor'=4] {'dp','tensor'}, dimensions={0}, use_global_device_ids=true | all-gather | bytes 5280 | tf_op jit(solution)/shard_map/all_gather | solution.py:91
  82.1 0.4 multiply_reduce_fusion
  82.5 0.2 div.22
  82.7 8.9 %copy.55 = bf16[256,5,2048]{2,1,0:T(8,128)(2,1)} copy(bf16[256,5,2048]{2,0,1:T(8,128)(2,1)} %all-gather.7.cloned.1.call-done) | data formatting | bytes 10485760 | tf_op jit(solution)/shard_map/all_gather | solution.py:89
  91.6 10.1 %reshape.90 = bf16[1280,2048]{1,0:T(8,128)(2,1)} reshape(bf16[256,5,2048]{2,1,0:T(8,128)(2,1)} %copy.55) | data formatting | bytes 10485760 | tf_op jit(solution)/shard_map/reshape | solution.py:93
  101.7 32.9 %all-gather.15.cloned.1.call-done = bf16[256,5,2048]{2,0,1:T(8,128)(2,1)} async-done(((bf16[8,5,2048]{2,0,1:T(8,128)(2,1)}), bf16[256,5,2048]{2,0,1:T(8,128)(2,1)}) %all-gather.15.cloned.1.call-update) | async-done | bytes 5242896 | tf_op jit(solution)/shard_map/all_gather | solution.py:90
  134.6 11.5 %copy.59 = f32[256,5,2048]{2,1,0:T(8,128)} copy(bf16[256,5,2048]{2,0,1:T(8,128)(2,1)} %all-gather.15.cloned.1.call-done) | data formatting | bytes 15728640 | tf_op jit(solution)/shard_map/convert_element_type | solution.py:30
  146.1 14.1 %reshape.96 = f32[1280,2048]{1,0:T(8,128)} reshape(f32[256,5,2048]{2,1,0:T(8,128)} %copy.59) | data formatting | bytes 20971520 | tf_op jit(solution)/shard_map/convert_element_type | solution.py:30
  160.2 13.6 %all-gather.9.cloned.1.call-done = bf16[2048,256]{1,0:T(8,128)(2,1)} async-done(((bf16[256,256]{1,0:T(8,128)(2,1)}), bf16[2048,256]{1,0:T(8,128)(2,1)}) %all-gather.9.cloned.1.call-update) | async-done | bytes 1048592 | tf_op jit(solution)/shard_map/all_gather | solution.py:44
  173.8 5.4 %fusion.11 = f32[1280,256]{1,0:T(8,128)} fusion(bf16[1280,2048]{1,0:T(8,128)(2,1)} %reshape.90, bf16[2048,256]{1,0:T(8,128)(2,1)} %all-gather.9.cloned.1.call-done), kind=kOutput, calls=%fused_computation.36 | convolution fusion | flops 1342177280 | bytes 7602176 | tf_op jit(solution)/shard_map/dot_general | solution.py:25
  179.2 33.5 %all-gather.11.cloned.1.call-done = bf16[2048,256]{1,0:T(8,128)(2,1)} async-done(((bf16[256,256]{1,0:T(8,128)(2,1)}), bf16[2048,256]{1,0:T(8,128)(2,1)}) %all-gather.11.cloned.1.call-update) | async-done | bytes 1048592 | tf_op jit(solution)/shard_map/all_gather | solution.py:45
  212.7 5.4 %fusion.12 = f32[1280,256]{1,0:T(8,128)} fusion(bf16[1280,2048]{1,0:T(8,128)(2,1)} %reshape.90, bf16[2048,256]{1,0:T(8,128)(2,1)} %all-gather.11.cloned.1.call-done), kind=kOutput, calls=%fused_computation.37 | convolution fusion | flops 1342177280 | bytes 7602176 | tf_op jit(solution)/shard_map/dot_general | solution.py:26
  218.1 33.5 %all-gather.13.cloned.1.call-done = bf16[2048,256]{1,0:T(8,128)(2,1)} async-done(((bf16[256,256]{1,0:T(8,128)(2,1)}), bf16[2048,256]{1,0:T(8,128)(2,1)}) %all-gather.13.cloned.1.call-update) | async-done | bytes 1048592 | tf_op jit(solution)/shard_map/all_gather | solution.py:46
  251.6 7.0 %multiply_convert_fusion.1 = (bf16[1280,256]{1,0:T(8,128)(2,1)S(1)}, bf16[1280,256]{1,0:T(8,128)(2,1)S(1)}, bf16[1280,256]{1,0:T(8,128)(2,1)S(1)}) fusion(f32[1280,256]{1,0:T(8,128)} %fusion.11, f32[1280,256]{1,0:T(8,128)} %fusion.12, bf16[2048,256]{1,0:T(8,128)(2,1)} %all-gather.13.cloned.1.call-done, f32[1280,2048]{1,0:T(8,128)} %reshape.96, ...), kind=kOutput, calls=%fused_computation.13 | convolution fusion | flops 1352335360 | bytes 16126976 | tf_op jit(solution)/shard_map/dot_general | solution.py:31
  258.6 1.6 fusion.13
  260.2 3.9 add_convert_fusion
  264.1 0.3 reduce-scatter.3.cloned.1.call-start
  264.4 0.9 copy-done.3
  265.3 3.9 convolution_convert_fusion
  269.2 0.7 copy-done.5
  270.0 6.8 %fusion.2 = bf16[1,2048,256]{2,1,0:T(8,128)(2,1)} fusion(bf16[1280,256]{1,0:T(8,128)(2,1)S(1)} %get-tuple-element.7, f32[1280,2048]{1,0:T(8,128)} %reshape.96, f32[1280]{0:T(1024)S(1)} %div.22), kind=kOutput, calls=%fused_computation.8 | convolution fusion | flops 1347944448 | bytes 12194816 | tf_op jit(solution)/shard_map/dot_general | solution.py:13
  276.8 78.9 %reduce-scatter.5.cloned.1.call-done = bf16[40,2048]{1,0:T(8,128)(2,1)} async-done(((bf16[1280,2048]{1,0:T(8,128)(2,1)}), bf16[40,2048]{1,0:T(8,128)(2,1)}) %reduce-scatter.5.cloned.1.call-update) | async-done | bytes 163856 | tf_op jit(solution)/shard_map/reduce_scatter | solution.py:105
  355.6 1.7 reshape.94
  357.3 7.5 %all-to-all-start.4 = ((bf16[8,5,2048]{2,1,0:T(8,128)(2,1)}), bf16[8,5,2048]{2,1,0:T(8,128)(2,1)S(1)}, u32[]{:S(2)}, u32[]{:S(2)}) async-start(bf16[8,5,2048]{2,1,0:T(8,128)(2,1)} %reshape.94), calls=%async_computation.6 | async-start | bytes 524288 | tf_op jit(solution)/shard_map/all_to_all | solution.py:121
  364.8 5.1 %fusion = bf16[1,2048,256]{2,1,0:T(8,128)(2,1)} fusion(bf16[1280,2048]{1,0:T(8,128)(2,1)} %reshape.90, bf16[1280,256]{1,0:T(8,128)(2,1)S(1)} %get-tuple-element.6), kind=kOutput, calls=%fused_computation.6 | convolution fusion | flops 1342701568 | bytes 6946816 | tf_op jit(solution)/shard_map/dot_general | solution.py:13
  369.9 81.9 %reduce-scatter.3.cloned.1.call-done = bf16[40,2048]{1,0:T(8,128)(2,1)} async-done(((bf16[1280,2048]{1,0:T(8,128)(2,1)}), bf16[40,2048]{1,0:T(8,128)(2,1)}) %reduce-scatter.3.cloned.1.call-update) | async-done | bytes 163856 | tf_op jit(solution)/shard_map/reduce_scatter | solution.py:99
  451.8 1.7 reshape.91
  453.5 7.5 %all-to-all-start.1 = ((bf16[8,5,2048]{2,1,0:T(8,128)(2,1)}), bf16[8,5,2048]{2,1,0:T(8,128)(2,1)S(1)}, u32[]{:S(2)}, u32[]{:S(2)}) async-start(bf16[8,5,2048]{2,1,0:T(8,128)(2,1)} %reshape.91), calls=%async_computation.2 | async-start | bytes 524288 | tf_op jit(solution)/shard_map/all_to_all | solution.py:114
  461.0 5.1 %fusion.1 = bf16[1,2048,256]{2,1,0:T(8,128)(2,1)} fusion(bf16[1280,2048]{1,0:T(8,128)(2,1)} %reshape.90, bf16[1280,256]{1,0:T(8,128)(2,1)S(1)} %get-tuple-element.5), kind=kOutput, calls=%fused_computation.7 | convolution fusion | flops 1342701568 | bytes 6946816 | tf_op jit(solution)/shard_map/dot_general | solution.py:13
  466.1 0.8 convolution_convert_fusion.6
  466.9 3.1 all-to-all-done.1
  470.1 0.8 convolution_convert_fusion.7
  (36 shorter events, 1.3 us)
Async XLA Ops:
  7.2 2.2 copy-start
  7.2 75.5 %all-gather.7.cloned.1.call-start = ((), (), s32[]{:S(2)}) async-start(), calls=%async_computation.7 | async-start | bytes 5406720 | tf_op jit(solution)/shard_map/all_gather | solution.py:89
  29.2 105.4 %all-gather.15.cloned.1.call-start = ((), (), s32[]{:S(2)}) async-start(), calls=%async_computation.12 | async-start | bytes 5406720 | tf_op jit(solution)/shard_map/all_gather | solution.py:90
  44.2 129.6 %all-gather.9.cloned.1.call-start = ((), (), s32[]{:S(2)}) async-start(), calls=%async_computation.8 | async-start | bytes 1179648 | tf_op jit(solution)/shard_map/all_gather | solution.py:44
  44.9 167.8 %all-gather.11.cloned.1.call-start = ((), (), s32[]{:S(2)}) async-start(), calls=%async_computation.9 | async-start | bytes 1179648 | tf_op jit(solution)/shard_map/all_gather | solution.py:45
  45.5 206.1 %all-gather.13.cloned.1.call-start = ((), (), s32[]{:S(2)}) async-start(), calls=%async_computation.10 | async-start | bytes 1179648 | tf_op jit(solution)/shard_map/all_gather | solution.py:46
  46.1 309.6 %reduce-scatter.5.cloned.1.call-start = ((), (), s32[]{:S(2)}) async-start(), calls=%async_computation.13 | async-start | bytes 5406720 | tf_op jit(solution)/shard_map/reduce_scatter | solution.py:105
  218.1 40.6 %copy-start.2 = (bf16[2048,256]{1,0:T(8,128)(2,1)S(1)}, bf16[2048,256]{1,0:T(8,128)(2,1)}, u32[]{:S(2)}) copy-start(bf16[2048,256]{1,0:T(8,128)(2,1)} %all-gather.9.cloned.1.call-done) | copy-start | bytes 3145732
  258.6 1.6 copy-start.4
  264.1 1.2 copy-start.3
  264.1 187.7 %reduce-scatter.3.cloned.1.call-start = ((), (), s32[]{:S(2)}) async-start(), calls=%async_computation.11 | async-start | bytes 5406720 | tf_op jit(solution)/shard_map/reduce_scatter | solution.py:99
  269.2 0.7 copy-start.5
  357.3 96.1 %all-to-all-start.4 = ((bf16[8,5,2048]{2,1,0:T(8,128)(2,1)}), bf16[8,5,2048]{2,1,0:T(8,128)(2,1)S(1)}, u32[]{:S(2)}, u32[]{:S(2)}) async-start(bf16[8,5,2048]{2,1,0:T(8,128)(2,1)} %reshape.94), calls=%async_computation.6 | async-start | bytes 524288 | tf_op jit(solution)/shard_map/all_to_all | solution.py:121
  453.5 16.5 %all-to-all-start.1 = ((bf16[8,5,2048]{2,1,0:T(8,128)(2,1)}), bf16[8,5,2048]{2,1,0:T(8,128)(2,1)S(1)}, u32[]{:S(2)}, u32[]{:S(2)}) async-start(bf16[8,5,2048]{2,1,0:T(8,128)(2,1)} %reshape.91), calls=%async_computation.2 | async-start | bytes 524288 | tf_op jit(solution)/shard_map/all_to_all | solution.py:114
  461.0 9.9 %copy-start.1 = (bf16[16,2048]{1,0:T(8,128)(2,1)S(1)}, bf16[16,2048]{1,0:T(8,128)(2,1)}, u32[]{:S(2)}) copy-start(bf16[16,2048]{1,0:T(8,128)(2,1)} %param.7) | copy-start | bytes 196612
Sparse Core Ops, SparseCore 0:
  29.4 49.9 all-gather.6
  82.5 52.0 all-gather.14
  136.4 37.3 all-gather.8
  175.4 37.1 all-gather.10
  214.3 37.1 all-gather.12
  264.2 91.3 reduce-scatter.4
  360.2 91.5 reduce-scatter.2
where the time goes:
time: 480 us; the launch traced here: 478 us
  waiting for transfers between devices  279 us (58%)
  blocking collectives  66.6 us (14%)
  local copies, waits for them, and re-layouts  53.6 us (11%)
  matrix products  47 us (10%)
  starting transfers between devices  15.4 us (3%)
  between operations  14.3 us (3%)
    reduce_scatter x1, waiting for transfers between devices, shards(): lax.psum_scatter(contract_cols(hidden, down_cols).astype(jnp.bfloat16), (...  81.9 us
    reduce_scatter x1, waiting for transfers between devices, shards(): lax.psum_scatter((contract_cols(gate_grad, gate_cols) + contract_cols(up_...  78.9 us
    all_gather x1, waiting for transfers between devices, shards(): lax.all_gather(dense_up, 'expert', axis=0, tiled=True)  33.5 us
    all_gather x1, waiting for transfers between devices, shards(): lax.all_gather(dense_down_t, 'expert', axis=0, tiled=True)  33.5 us
    all_gather x1, waiting for transfers between devices, shards(): lax.all_gather(parcel[1], ('dp', 'tensor'), axis=0, tiled=True)  32.9 us
    convert_element_type x2, local copies, waits for them, and re-layouts, expert_rows(): rows_dy.astype(jnp.float32)  25.6 us
    all_gather x1, blocking collectives, shards(): lax.all_gather(parcel[2], ('dp', 'tensor'), axis=0, tiled=True)  24.9 us
    all_to_all x1, blocking collectives, shards(): lax.all_to_all(send_x.reshape(experts, capacity, model_width), 'expert',...  18.8 us
  transfers between devices with their start and end apart: 9, of which 7 were waited for; matrix products, arithmetic and copies ran while one was open for 18% of the time, Pallas kernels for 0%

commit v1 on v0

v1 whole, which is shorter than its diff:
```python
import jax
import jax.numpy as jnp
from jax import lax
from jax.sharding import PartitionSpec as P

GROUP = ("dp", "tensor")


def silu_parts(gate_pre):
    sigmoid_val = jax.nn.sigmoid(gate_pre)
    return (gate_pre * sigmoid_val, sigmoid_val * (1.0 + gate_pre * (1.0 - sigmoid_val)))


def contract_rows(left_side, right_side):
    return lax.dot_general(
        left_side, right_side, (((0,), (0,)), ((), ())), preferred_element_type=jnp.float32
    )


def contract_cols(left_side, right_side):
    return lax.dot_general(
        left_side, right_side, (((1,), (1,)), ((), ())), preferred_element_type=jnp.float32
    )


def forward_parts(rows_x, gate_cols, up_cols):
    gate_pre = jnp.dot(rows_x, gate_cols, preferred_element_type=jnp.float32)
    up_pre = jnp.dot(rows_x, up_cols, preferred_element_type=jnp.float32)
    activation, act_slope = silu_parts(gate_pre)
    hidden = (activation * up_pre).astype(jnp.bfloat16)
    return up_pre, activation, act_slope, hidden


def grad_parts(scaled, down_cols, up_pre, activation, act_slope):
    hidden_grad = jnp.dot(scaled, down_cols, preferred_element_type=jnp.float32)
    gate_grad = (hidden_grad * up_pre * act_slope).astype(jnp.bfloat16)
    up_grad = (hidden_grad * activation).astype(jnp.bfloat16)
    return gate_grad, up_grad


def shards(tokens, cotangent, routes, weight_codes, dense_gate, dense_up, dense_down_t):
    experts = lax.axis_size("expert")
    count_tok, model_width = tokens.shape
    hid = dense_gate.shape[1]
    capacity = 5 * count_tok // (2 * experts)
    slots_here = experts * capacity

    stacked = jnp.concatenate([dense_gate, dense_up, dense_down_t], axis=1)
    full_cols = lax.all_gather(stacked, "expert", axis=0, tiled=True)
    gate_cols = full_cols[:, :hid]
    up_cols = full_cols[:, hid : 2 * hid]
    down_cols = full_cols[:, 2 * hid :]
    gate_up_cols = full_cols[:, : 2 * hid]

    code_cols = jnp.zeros((count_tok, 128), jnp.bfloat16)
    code_cols = code_cols.at[:, 0:2].set(weight_codes.astype(jnp.bfloat16))
    home = jnp.concatenate([tokens, cotangent, code_cols], axis=1)
    plane = lax.all_gather(home, GROUP, axis=0, tiled=True)
    plane_x = plane[:, :model_width]
    plane_dy = plane[:, model_width : 2 * model_width].astype(jnp.float32)
    plane_scale = plane[:, 2 * model_width : 2 * model_width + 2].astype(jnp.float32) / 256.0

    up_pre, activation, act_slope, hidden = forward_parts(plane_x, gate_cols, up_cols)
    out_term = contract_cols(hidden, down_cols).astype(jnp.bfloat16)
    grad_term = jnp.zeros(out_term.shape, jnp.float32)
    for which in range(2):
        scaled = (plane_scale[:, which : which + 1] * plane_dy).astype(jnp.bfloat16)
        gate_grad, up_grad = grad_parts(scaled, down_cols, up_pre, activation, act_slope)
        grad_term = grad_term + contract_cols(
            jnp.concatenate([gate_grad, up_grad], axis=1), gate_up_cols
        )
    terms = jnp.concatenate([out_term, grad_term.astype(jnp.bfloat16)], axis=1)
    summed = lax.psum_scatter(terms, GROUP, scatter_dimension=0, tiled=True)
    expert_out = summed[:, :model_width].astype(jnp.float32)
    code_scale = weight_codes.astype(jnp.float32) / 256.0
    mixed = (code_scale[:, 0:1] * expert_out + code_scale[:, 1:2] * expert_out).astype(
        jnp.bfloat16
    )
    input_grad = summed[:, model_width:]

    flat_route = routes.reshape(-1)
    flat_scale = weight_codes.reshape(-1).astype(jnp.float32) / 256.0
    onehot = (flat_route[:, None] == jnp.arange(experts, dtype=jnp.int32)[None, :]).astype(
        jnp.int32
    )
    earlier = jnp.cumsum(onehot, axis=0) - onehot
    slot_of = flat_route * capacity + jnp.sum(earlier * onehot, axis=1)
    placed = (slot_of[None, :] == jnp.arange(slots_here, dtype=jnp.int32)[:, None]).astype(
        jnp.bfloat16
    )
    flat_x = jnp.repeat(tokens, 2, axis=0)
    flat_scaled = (flat_scale[:, None] * jnp.repeat(cotangent, 2, axis=0).astype(jnp.float32)).astype(
        jnp.bfloat16
    )
    send_x = jnp.dot(placed, flat_x, preferred_element_type=jnp.float32).astype(jnp.bfloat16)
    send_s = jnp.dot(placed, flat_scaled, preferred_element_type=jnp.float32).astype(jnp.bfloat16)
    send = jnp.stack(
        [send_x.reshape(experts, capacity, model_width), send_s.reshape(experts, capacity, model_width)],
        axis=1,
    )
    got = lax.all_to_all(send, "expert", split_axis=0, concat_axis=0, tiled=True)
    got = jnp.transpose(got, (1, 0, 2, 3))
    rows = lax.all_gather(got, GROUP, axis=1, tiled=True)
    rows_x = rows[0].reshape(-1, model_width)
    rows_s = rows[1].reshape(-1, model_width)
    r_up, r_act, r_slope, r_hidden = forward_parts(rows_x, gate_cols, up_cols)
    r_gate, r_upg = grad_parts(rows_s, down_cols, r_up, r_act, r_slope)
    grad_gate = contract_rows(rows_x, r_gate).astype(jnp.bfloat16)[None]
    grad_up = contract_rows(rows_x, r_upg).astype(jnp.bfloat16)[None]
    grad_down_t = contract_rows(rows_s, r_hidden).astype(jnp.bfloat16)[None]
    return (mixed, input_grad, grad_gate, grad_up, grad_down_t)


def solution(mesh):
    rows = P(("dp", "expert", "tensor"), None)
    weights = P("expert", ("dp", "tensor"))
    grads = P("expert", None, ("dp", "tensor"))
    return jax.shard_map(
        shards,
        mesh=mesh,
        in_specs=(rows, rows, rows, rows, weights, weights, weights),
        out_specs=(rows, rows, grads, grads, grads),
        check_vma=False,
    )
```

time: 480 us -> 378 us (0.79)
  waiting for transfers between devices: 279 us -> 221 us
  blocking collectives: 66.6 us -> 16.8 us
  local copies, waits for them, and re-layouts: 53.6 us -> 82.6 us
  matrix products: 47 us -> 29.2 us
  starting transfers between devices: 15.4 us -> 0.16 us
  other arithmetic: 1.65 us -> 11.7 us
    reduce_scatter x2 -> x1, waiting for transfers between devices: 161 us -> 60.9 us  [shards(): summed = lax.psum_scatter(terms, GROUP, scatter_dimension=0, tiled=True)]
    slice x0 -> x3, local copies, waits for them, and re-layouts: none -> 55.4 us  [the longest x1 53.6 us: shards(): rows_s = rows[1].reshape(-1, model_width)]
    all_gather x5 -> x3, waiting for transfers between devices: 114 us -> 160 us  [the longest x1 62 us: shards(): rows = lax.all_gather(got, GROUP, axis=1, tiled=True)]
    all_to_all x3 -> x1, blocking collectives: 41.8 us -> 16.8 us  [shards(): lax.all_to_all(send, 'expert', split_axis=0, concat_axis=0, tiled=True)]
    all_gather x1 -> x0, blocking collectives: 24.9 us -> none  [shards(): lax.all_gather(parcel[2], ('dp', 'tensor'), axis=0, tiled=True)]
    convert_element_type x2 -> x1, local copies, waits for them, and re-layouts: 25.6 us -> 0.89 us  [shards(): jnp.repeat(cotangent, 2, axis=0).astype(jnp.float32)]
    another operation x0 -> x5, local copies, waits for them, and re-layouts: none -> 23.1 us  [the longest x1 10 us: shards(): rows_x = rows[0].reshape(-1, model_width)]
    all_to_all x2 -> x0, starting transfers between devices: 14.9 us -> none  [the longest x1 7.47 us: shards(): lax.all_to_all(out_rows.reshape(experts, capacity, model_width), 'expert'...]
  transfers between devices with their start and end apart: 9 -> 4, of which waited for: 7 -> 4; matrix products, arithmetic and copies ran while one was open for 18% -> 4% of each run, Pallas kernels for 0% -> 0%
where the time goes in v1:
time: 378 us; the launch traced here: 375 us
  waiting for transfers between devices  221 us (58%)
  local copies, waits for them, and re-layouts  82.6 us (22%)
  matrix products  29.2 us (8%)
  blocking collectives  16.8 us (4%)
  between operations  14 us (4%)
  other arithmetic  11.7 us (3%)
    all_gather x1, waiting for transfers between devices, shards(): rows = lax.all_gather(got, GROUP, axis=1, tiled=True)  62 us
    reduce_scatter x1, waiting for transfers between devices, shards(): summed = lax.psum_scatter(terms, GROUP, scatter_dimension=0, tiled=True)  60.9 us
    slice x1, local copies, waits for them, and re-layouts, shards(): rows_s = rows[1].reshape(-1, model_width)  53.6 us
    all_gather x1, waiting for transfers between devices, shards(): plane = lax.all_gather(home, GROUP, axis=0, tiled=True)  52.4 us
    all_gather x1, waiting for transfers between devices, shards(): full_cols = lax.all_gather(stacked, 'expert', axis=0, tiled=True)  45.2 us
    all_to_all x1, blocking collectives, shards(): lax.all_to_all(send, 'expert', split_axis=0, concat_axis=0, tiled=True)  16.8 us
    another operation x1, local copies, waits for them, and re-layouts, shards(): rows_x = rows[0].reshape(-1, model_width)  10 us
    another operation x1, local copies, waits for them, and re-layouts, shards(): rows_s = rows[1].reshape(-1, model_width)  10 us
  transfers between devices with their start and end apart: 4, of which 4 were waited for; matrix products, arithmetic and copies ran while one was open for 4% of the time, Pallas kernels for 0%

profile of v1, /device:TPU:32, one launch (start us, length us, event | category | flops | bytes accessed | tf_op | source)
XLA Modules:
  0.0 375.1 jit_solution(17290189949668021922)
XLA Ops:
  7.2 0.6 compare_reduce_fusion
  7.9 1.3 broadcast_select_fusion
  9.2 0.1 copy.28
  9.3 1.5 fusion.43
  10.9 1.8 pad_maximum_fusion.2
  12.8 52.4 %all-gather.4.cloned.1.call-done = bf16[512,4224]{1,0:T(8,128)(2,1)} async-done(((bf16[16,4224]{1,0:T(8,128)(2,1)}), bf16[512,4224]{1,0:T(8,128)(2,1)}) %all-gather.4.cloned.1.call-update) | async-done | bytes 4325392 | tf_op jit(solution)/shard_map/all_gather | solution.py:58
  65.1 0.9 convert_multiply_fusion.2
  66.1 0.3 slice_reduce_fusion.2
  66.4 45.2 %all-gather.6.cloned.1.call-done = bf16[2048,768]{1,0:T(8,128)(2,1)} async-done(((bf16[256,768]{1,0:T(8,128)(2,1)}), bf16[2048,768]{1,0:T(8,128)(2,1)}) %all-gather.6.cloned.1.call-update) | async-done | bytes 3145744 | tf_op jit(solution)/shard_map/all_gather | solution.py:49
  111.6 2.8 fusion.16
  114.4 0.1 copy-done.1
  114.5 2.5 fusion.18
  117.0 0.4 copy-done.5
  117.3 0.8 fusion.7
  118.2 0.8 convolution_convert_fusion
  119.0 1.0 multiply_convert_fusion.7
  120.0 1.3 fusion.12
  121.3 1.3 add_convert_fusion
  122.6 2.6 pad_maximum_fusion
  125.3 0.6 copy-done.6
  126.0 0.1 reshape.63
  126.1 0.1 copy.24
  126.2 0.1 div.27
  126.3 0.1 broadcast_in_dim.21
  126.4 0.9 convert_element_type.107
  127.4 0.2 select_reduce_fusion
  127.6 1.9 convolution_convert_fusion.4
  129.4 1.0 stack_reshape.7
  130.4 0.7 broadcast_in_dim.20
  131.2 1.0 reshape.64
  132.1 0.8 convolution_convert_fusion.5
  133.0 1.7 stack_reshape.6
  134.7 1.1 pad_maximum_fusion.1
  135.7 0.4 copy.25
  136.1 16.8 %all_to_all.5 = bf16[8,2,5,2048]{3,1,2,0:T(2,128)(2,1)} all-to-all(bf16[8,2,5,2048]{3,1,2,0:T(2,128)(2,1)S(1)} %copy.25), channel_id=1, replica_groups=mesh['dp'=8,'expert'=8,'tensor'=4] {'expert'}, dimensions={0} | all-to-all | bytes 655360 | tf_op jit(solution)/shard_map/all_to_all | solution.py:101
  153.0 60.9 %reduce-scatter.2.cloned.1.call-done = bf16[16,4096]{1,0:T(8,128)(2,1)} async-done(((bf16[512,4096]{1,0:T(8,128)(2,1)}), bf16[16,4096]{1,0:T(8,128)(2,1)}) %reduce-scatter.2.cloned.1.call-update) | async-done | bytes 131088 | tf_op jit(solution)/shard_map/reduce_scatter | solution.py:73
  213.9 1.5 slice.86
  215.3 1.5 multiply_convert_fusion.14
  216.9 62.0 %all-gather.8.cloned.1.call-done = bf16[2,256,5,2048]{3,0,2,1:T(2,128)(2,1)} async-done(((bf16[2,8,5,2048]{3,0,2,1:T(2,128)(2,1)}), bf16[2,256,5,2048]{3,0,2,1:T(2,128)(2,1)}) %all-gather.8.cloned.1.call-update) | async-done | bytes 10485776 | tf_op jit(solution)/shard_map/all_gather | solution.py:103
  278.9 53.6 %slice_reduce_fusion = (bf16[256,5,2048]{2,1,0:T(8,128)(2,1)}, bf16[256,5,2048]{2,1,0:T(8,128)(2,1)}) fusion(bf16[2,256,5,2048]{3,0,2,1:T(2,128)(2,1)} %all-gather.8.cloned.1.call-done), kind=kLoop, calls=%fused_computation | loop fusion | bytes 20971520 | tf_op jit(solution)/shard_map/slice | solution.py:105
  332.5 10.0 %reshape_squeeze.6 = bf16[1280,2048]{1,0:T(8,128)(2,1)} reshape(bf16[256,5,2048]{2,1,0:T(8,128)(2,1)} %get-tuple-element.18) | data formatting | bytes 10485760 | tf_op jit(solution)/shard_map/reshape;squeeze | solution.py:104
  342.5 10.0 %reshape_squeeze.7 = bf16[1280,2048]{1,0:T(8,128)(2,1)} reshape(bf16[256,5,2048]{2,1,0:T(8,128)(2,1)} %get-tuple-element.17) | data formatting | bytes 10485760 | tf_op jit(solution)/shard_map/reshape;squeeze | solution.py:105
  352.6 4.2 %fusion.24 = f32[1280,256]{1,0:T(8,128)S(1)} fusion(bf16[1280,2048]{1,0:T(8,128)(2,1)} %reshape_squeeze.6, bf16[2048,768]{1,0:T(8,128)(2,1)S(1)} %copy-done.1), kind=kOutput, calls=%fused_computation.38 | convolution fusion | flops 1342177280 | bytes 7602176 | tf_op jit(solution)/shard_map/dot_general | solution.py:27
  356.8 1.6 fusion.21
  358.4 2.9 fusion.4
  361.2 1.6 fusion.27
  362.8 2.9 fusion.3
  365.6 3.0 fusion.2
  (30 shorter events, 0.5 us)
Async XLA Ops:
  7.2 58.0 %all-gather.4.cloned.1.call-start = ((), (), s32[]{:S(2)}) async-start(), calls=%async_computation.2 | async-start | bytes 4460544 | tf_op jit(solution)/shard_map/all_gather | solution.py:58
  10.8 100.8 %all-gather.6.cloned.1.call-start = ((), (), s32[]{:S(2)}) async-start(), calls=%async_computation.3 | async-start | bytes 3538944 | tf_op jit(solution)/shard_map/all_gather | solution.py:49
  12.7 201.1 %reduce-scatter.2.cloned.1.call-start = ((), (), s32[]{:S(2)}) async-start(), calls=%async_computation.4 | async-start | bytes 4325376 | tf_op jit(solution)/shard_map/reduce_scatter | solution.py:73
  111.6 2.9 copy-start.1
  114.5 2.9 copy-start.5
  125.2 0.7 copy-start.6
  125.2 0.9 copy-start.4
  125.2 1.0 copy-start.2
  125.2 5.2 %copy-start.3 = (bf16[16,2048]{1,0:T(8,128)(2,1)S(1)}, bf16[16,2048]{1,0:T(8,128)(2,1)}, u32[]{:S(2)}) copy-start(bf16[16,2048]{1,0:T(8,128)(2,1)} %param.9) | copy-start | bytes 196612
  125.2 153.7 %all-gather.8.cloned.1.call-start = ((), (), s32[]{:S(2)}) async-start(), calls=%async_computation.5 | async-start | bytes 10813440 | tf_op jit(solution)/shard_map/all_gather | solution.py:103
  352.5 4.2 %copy-start = (bf16[1280,2048]{1,0:T(8,128)(2,1)S(1)}, bf16[1280,2048]{1,0:T(8,128)(2,1)}, u32[]{:S(2)}) copy-start(bf16[1280,2048]{1,0:T(8,128)(2,1)} %reshape_squeeze.6) | copy-start | bytes 15728644
  352.5 5.8 %slice-start = ((s8[5242880]{0:T(1024)(128)(4,1)}), s8[4194304]{0:T(1024)(128)(4,1)S(1)}, s32[]{:S(2)}) async-start(s8[5242880]{0:T(1024)(128)(4,1)} %bitcast.16), calls=%async_computation.6 | async-start | bytes 8388608
  356.8 1.6 slice-start.1
Sparse Core Ops, SparseCore 0:
  11.2 53.8 all-gather.3
  67.5 44.0 all-gather.5
  125.4 88.4 reduce-scatter.1
  216.6 62.2 all-gather.7

commit v2 on v1

--- a/solution.py
+++ b/solution.py
@@ -70,13 +70,6 @@
             jnp.concatenate([gate_grad, up_grad], axis=1), gate_up_cols
         )
     terms = jnp.concatenate([out_term, grad_term.astype(jnp.bfloat16)], axis=1)
-    summed = lax.psum_scatter(terms, GROUP, scatter_dimension=0, tiled=True)
-    expert_out = summed[:, :model_width].astype(jnp.float32)
-    code_scale = weight_codes.astype(jnp.float32) / 256.0
-    mixed = (code_scale[:, 0:1] * expert_out + code_scale[:, 1:2] * expert_out).astype(
-        jnp.bfloat16
-    )
-    input_grad = summed[:, model_width:]
 
     flat_route = routes.reshape(-1)
     flat_scale = weight_codes.reshape(-1).astype(jnp.float32) / 256.0
@@ -94,15 +87,19 @@
     )
     send_x = jnp.dot(placed, flat_x, preferred_element_type=jnp.float32).astype(jnp.bfloat16)
     send_s = jnp.dot(placed, flat_scaled, preferred_element_type=jnp.float32).astype(jnp.bfloat16)
-    send = jnp.stack(
-        [send_x.reshape(experts, capacity, model_width), send_s.reshape(experts, capacity, model_width)],
-        axis=1,
+    send = jnp.concatenate([send_x, send_s], axis=1)
+    got = lax.all_to_all(send, "expert", split_axis=0, concat_axis=0, tiled=True)
+    rows = lax.all_gather(got, GROUP, axis=0, tiled=True)
+    terms, rows = lax.optimization_barrier((terms, rows))
+    summed = lax.psum_scatter(terms, GROUP, scatter_dimension=0, tiled=True)
+    expert_out = summed[:, :model_width].astype(jnp.float32)
+    code_scale = weight_codes.astype(jnp.float32) / 256.0
+    mixed = (code_scale[:, 0:1] * expert_out + code_scale[:, 1:2] * expert_out).astype(
+        jnp.bfloat16
     )
-    got = lax.all_to_all(send, "expert", split_axis=0, concat_axis=0, tiled=True)
-    got = jnp.transpose(got, (1, 0, 2, 3))
-    rows = lax.all_gather(got, GROUP, axis=1, tiled=True)
-    rows_x = rows[0].reshape(-1, model_width)
-    rows_s = rows[1].reshape(-1, model_width)
+    input_grad = summed[:, model_width:]
+    rows_x = rows[:, :model_width]
+    rows_s = rows[:, model_width:]
     r_up, r_act, r_slope, r_hidden = forward_parts(rows_x, gate_cols, up_cols)
     r_gate, r_upg = grad_parts(rows_s, down_cols, r_up, r_act, r_slope)
     grad_gate = contract_rows(rows_x, r_gate).astype(jnp.bfloat16)[None]

time: 378 us -> 280 us (0.74)
  local copies, waits for them, and re-layouts: 82.6 us -> 7.38 us
  waiting for transfers between devices: 221 us -> 194 us
  blocking collectives: 16.8 us -> 24.4 us
    slice x1 -> x0, local copies, waits for them, and re-layouts: 53.6 us -> none  [shards(): rows_s = rows[1].reshape(-1, model_width)]
    all_gather x1, waiting for transfers between devices: 52.4 us -> 22.3 us  [shards(): plane = lax.all_gather(home, GROUP, axis=0, tiled=True)]
    another operation x5 -> x0, local copies, waits for them, and re-layouts: 23.1 us -> none  [the longest x1 10 us: shards(): rows_x = rows[0].reshape(-1, model_width)]
    reduce_scatter x1, waiting for transfers between devices: 60.9 us -> 75.4 us  [shards(): summed = lax.psum_scatter(terms, GROUP, scatter_dimension=0, tiled=True)]
    all_gather x1, waiting for transfers between devices: 62 us -> 51.4 us  [shards(): rows = lax.all_gather(got, GROUP, axis=0, tiled=True)]
    all_to_all x1, blocking collectives: 16.8 us -> 24.4 us  [shards(): lax.all_to_all(send, 'expert', split_axis=0, concat_axis=0, tiled=True)]
  transfers between devices with their start and end apart: 4 -> 4, of which waited for: 4 -> 4; matrix products, arithmetic and copies ran while one was open for 4% -> 13% of each run, Pallas kernels for 0% -> 0%
where the time goes in v2:
time: 280 us; the launch traced here: 279 us
  waiting for transfers between devices  194 us (69%)
  matrix products  27.5 us (10%)
  blocking collectives  24.4 us (9%)
  between operations  13.9 us (5%)
  other arithmetic  11.4 us (4%)
  local copies, waits for them, and re-layouts  7.38 us (3%)
    reduce_scatter x1, waiting for transfers between devices, shards(): summed = lax.psum_scatter(terms, GROUP, scatter_dimension=0, tiled=True)  75.4 us
    all_gather x1, waiting for transfers between devices, shards(): rows = lax.all_gather(got, GROUP, axis=0, tiled=True)  51.4 us
    all_gather x1, waiting for transfers between devices, shards(): full_cols = lax.all_gather(stacked, 'expert', axis=0, tiled=True)  45.2 us
    all_to_all x1, blocking collectives, shards(): lax.all_to_all(send, 'expert', split_axis=0, concat_axis=0, tiled=True)  24.4 us
    all_gather x1, waiting for transfers between devices, shards(): plane = lax.all_gather(home, GROUP, axis=0, tiled=True)  22.3 us
    dot_general x3, matrix products, contract_rows(): lax.dot_general(left_side, right_side, (((0,), (0,)), ((), ())), preferre...  8.86 us
    dot_general x2, matrix products, forward_parts(): gate_pre = jnp.dot(rows_x, gate_cols, preferred_element_type=jnp.float32)  6.82 us
  transfers between devices with their start and end apart: 4, of which 4 were waited for; matrix products, arithmetic and copies ran while one was open for 13% of the time, Pallas kernels for 0%

profile of v2, /device:TPU:32, one launch (start us, length us, event | category | flops | bytes accessed | tf_op | source)
XLA Modules:
  0.0 279.1 jit_solution(2618374725488988174)
XLA Ops:
  7.2 0.6 compare_reduce_fusion
  7.9 1.3 broadcast_select_fusion
  9.2 0.1 copy.18
  9.3 1.5 fusion.67
  10.8 0.0 all-gather.6.cloned.1.call-start
  10.9 1.8 pad_maximum_fusion.1
  12.8 0.9 broadcast_in_dim.21
  13.7 0.2 convert_element_type.105
  13.9 0.7 convert_multiply_fusion.3
  14.6 0.1 copy.17
  14.7 0.1 div.27
  14.8 0.8 copy.16
  15.5 0.1 reshape.65
  15.6 0.9 broadcast_in_dim.20
  16.5 0.1 reshape.66
  16.6 0.1 fusion.69
  16.7 0.1 reduce_window_sum.11
  16.7 0.2 select_reduce_fusion
  16.9 0.2 convolution_convert_fusion.2
  17.1 0.2 convolution_convert_fusion.1
  17.4 0.1 all_to_all.8
  17.5 24.4 %all_to_all.12 = bf16[8,5,4096]{2,1,0:T(8,128)(2,1)S(1)} all-to-all(bf16[8,5,4096]{2,1,0:T(8,128)(2,1)S(1)} %all_to_all.8), channel_id=1, replica_groups=mesh['dp'=8,'expert'=8,'tensor'=4] {'expert'}, dimensions={0} | all-to-all | bytes 655360 | tf_op jit(solution)/shard_map/all_to_all | solution.py:91
  41.9 0.9 all_to_all.10
  42.8 0.0 reduce-scatter.2.cloned.1.call-start
  42.9 22.3 %all-gather.4.cloned.1.call-done = bf16[512,4224]{1,0:T(8,128)(2,1)} async-done(((bf16[16,4224]{1,0:T(8,128)(2,1)}), bf16[512,4224]{1,0:T(8,128)(2,1)}) %all-gather.4.cloned.1.call-update) | async-done | bytes 4325392 | tf_op jit(solution)/shard_map/all_gather | solution.py:58
  65.1 0.9 convert_multiply_fusion.2
  66.1 0.3 slice_reduce_fusion
  66.4 45.2 %all-gather.6.cloned.1.call-done = bf16[2048,768]{1,0:T(8,128)(2,1)} async-done(((bf16[256,768]{1,0:T(8,128)(2,1)}), bf16[2048,768]{1,0:T(8,128)(2,1)}) %all-gather.6.cloned.1.call-update) | async-done | bytes 3145744 | tf_op jit(solution)/shard_map/all_gather | solution.py:49
  111.6 2.8 fusion.43
  114.4 0.1 copy-done
  114.5 2.6 fusion.45
  117.1 0.8 convolution_convert_fusion
  117.9 0.9 fusion.34
  118.8 1.2 multiply_convert_fusion.7
  120.0 1.3 fusion.39
  121.3 1.3 add_convert_fusion
  122.6 2.6 pad_maximum_fusion
  125.2 51.4 %all-gather.8.cloned.1.call-done = bf16[1280,4096]{1,0:T(8,128)(2,1)} async-done(((bf16[40,4096]{1,0:T(8,128)(2,1)}), bf16[1280,4096]{1,0:T(8,128)(2,1)}) %all-gather.8.cloned.1.call-update) | async-done | bytes 10485776 | tf_op jit(solution)/shard_map/all_gather | solution.py:92
  176.6 4.2 %fusion.10 = f32[1280,256]{1,0:T(8,128)S(1)} fusion(bf16[1280,4096]{1,0:T(8,128)(2,1)} %all-gather.8.cloned.1.call-done, bf16[2048,768]{1,0:T(8,128)(2,1)S(1)} %copy-done), kind=kOutput, calls=%fused_computation.14 | convolution fusion | flops 1342177280 | bytes 7602176 | tf_op jit(solution)/shard_map/dot_general | solution.py:27
  180.9 1.3 copy-done.1
  182.2 1.5 fusion.2
  183.7 1.6 fusion.12
  185.3 3.0 %fusion.26 = bf16[1,2048,256]{2,1,0:T(8,128)(2,1)} fusion(bf16[1280,4096]{1,0:T(8,128)(2,1)S(1)} %copy-done.1, f32[1280,256]{1,0:T(8,128)S(1)} %fusion.2, f32[1280,256]{1,0:T(8,128)S(1)} %fusion.10), kind=kOutput, calls=%fused_computation.23 | convolution fusion | flops 1344667648 | bytes 8912896 | tf_op jit(solution)/shard_map/dot_general | solution.py:15
  188.3 2.9 %fusion.23 = bf16[1,2048,256]{2,1,0:T(8,128)(2,1)} fusion(bf16[1280,4096]{1,0:T(8,128)(2,1)S(1)} %copy-done.1, f32[1280,256]{1,0:T(8,128)S(1)} %fusion.12, f32[1280,256]{1,0:T(8,128)S(1)} %fusion.10), kind=kOutput, calls=%fused_computation.22 | convolution fusion | flops 1344667648 | bytes 8912896 | tf_op jit(solution)/shard_map/dot_general | solution.py:15
  191.2 3.0 %fusion.29 = bf16[1,2048,256]{2,1,0:T(8,128)(2,1)} fusion(bf16[1280,4096]{1,0:T(8,128)(2,1)S(1)} %copy-done.1, f32[1280,256]{1,0:T(8,128)S(1)} %fusion.10, f32[1280,256]{1,0:T(8,128)S(1)} %fusion.2, f32[1280,256]{1,0:T(8,128)S(1)} %fusion.12), kind=kOutput, calls=%fused_computation.24 | convolution fusion | flops 1345978368 | bytes 10223616 | tf_op jit(solution)/shard_map/dot_general | solution.py:15
  194.1 75.4 %reduce-scatter.2.cloned.1.call-done = bf16[16,4096]{1,0:T(8,128)(2,1)} async-done(((bf16[512,4096]{1,0:T(8,128)(2,1)}), bf16[16,4096]{1,0:T(8,128)(2,1)}) %reduce-scatter.2.cloned.1.call-update) | async-done | bytes 131088 | tf_op jit(solution)/shard_map/reduce_scatter | solution.py:94
  269.6 1.5 slice.86
  271.1 1.5 multiply_convert_fusion.14
  (16 shorter events, 0.2 us)
Async XLA Ops:
  7.2 58.0 %all-gather.4.cloned.1.call-start = ((), (), s32[]{:S(2)}) async-start(), calls=%async_computation.2 | async-start | bytes 4460544 | tf_op jit(solution)/shard_map/all_gather | solution.py:58
  10.8 100.8 %all-gather.6.cloned.1.call-start = ((), (), s32[]{:S(2)}) async-start(), calls=%async_computation.3 | async-start | bytes 3538944 | tf_op jit(solution)/shard_map/all_gather | solution.py:49
  12.7 163.9 %all-gather.8.cloned.1.call-start = ((), (), s32[]{:S(2)}) async-start(), calls=%async_computation.4 | async-start | bytes 10813440 | tf_op jit(solution)/shard_map/all_gather | solution.py:92
  42.8 226.8 %reduce-scatter.2.cloned.1.call-start = ((), (), s32[]{:S(2)}) async-start(), calls=%async_computation.5 | async-start | bytes 4325376 | tf_op jit(solution)/shard_map/reduce_scatter | solution.py:94
  111.6 2.9 %copy-start = (bf16[2048,768]{1,0:T(8,128)(2,1)S(1)}, bf16[2048,768]{1,0:T(8,128)(2,1)}, u32[]{:S(2)}) copy-start(bf16[2048,768]{1,0:T(8,128)(2,1)} %all-gather.6.cloned.1.call-done) | copy-start | bytes 9437188
  111.6 6.3 %slice-start = ((s8[4325376]{0:T(1024)(128)(4,1)}), s8[4194304]{0:T(1024)(128)(4,1)S(1)}, s32[]{:S(2)}) async-start(s8[4325376]{0:T(1024)(128)(4,1)} %bitcast.9), calls=%async_computation.6 | async-start | bytes 8388608
  114.5 3.4 %slice-start.1 = ((s8[4325376]{0:T(1024)(128)(4,1)}), s8[131072]{0:T(1024)(128)(4,1)S(1)}, s32[]{:S(2)}) async-start(s8[4325376]{0:T(1024)(128)(4,1)} %bitcast.9), calls=%async_computation.7 | async-start | bytes 262144
  176.6 5.5 %copy-start.1 = (bf16[1280,4096]{1,0:T(8,128)(2,1)S(1)}, bf16[1280,4096]{1,0:T(8,128)(2,1)}, u32[]{:S(2)}) copy-start(bf16[1280,4096]{1,0:T(8,128)(2,1)} %all-gather.8.cloned.1.call-done) | copy-start | bytes 31457284
Sparse Core Ops, SparseCore 0:
  11.2 53.8 all-gather.3
  67.5 44.0 all-gather.5
  114.7 61.8 all-gather.7
  180.4 89.1 reduce-scatter.1

commit v3 on v2

--- a/solution.py
+++ b/solution.py
@@ -52,25 +52,6 @@
     down_cols = full_cols[:, 2 * hid :]
     gate_up_cols = full_cols[:, : 2 * hid]
 
-    code_cols = jnp.zeros((count_tok, 128), jnp.bfloat16)
-    code_cols = code_cols.at[:, 0:2].set(weight_codes.astype(jnp.bfloat16))
-    home = jnp.concatenate([tokens, cotangent, code_cols], axis=1)
-    plane = lax.all_gather(home, GROUP, axis=0, tiled=True)
-    plane_x = plane[:, :model_width]
-    plane_dy = plane[:, model_width : 2 * model_width].astype(jnp.float32)
-    plane_scale = plane[:, 2 * model_width : 2 * model_width + 2].astype(jnp.float32) / 256.0
-
-    up_pre, activation, act_slope, hidden = forward_parts(plane_x, gate_cols, up_cols)
-    out_term = contract_cols(hidden, down_cols).astype(jnp.bfloat16)
-    grad_term = jnp.zeros(out_term.shape, jnp.float32)
-    for which in range(2):
-        scaled = (plane_scale[:, which : which + 1] * plane_dy).astype(jnp.bfloat16)
-        gate_grad, up_grad = grad_parts(scaled, down_cols, up_pre, activation, act_slope)
-        grad_term = grad_term + contract_cols(
-            jnp.concatenate([gate_grad, up_grad], axis=1), gate_up_cols
-        )
-    terms = jnp.concatenate([out_term, grad_term.astype(jnp.bfloat16)], axis=1)
-
     flat_route = routes.reshape(-1)
     flat_scale = weight_codes.reshape(-1).astype(jnp.float32) / 256.0
     onehot = (flat_route[:, None] == jnp.arange(experts, dtype=jnp.int32)[None, :]).astype(
@@ -89,9 +70,39 @@
     send_s = jnp.dot(placed, flat_scaled, preferred_element_type=jnp.float32).astype(jnp.bfloat16)
     send = jnp.concatenate([send_x, send_s], axis=1)
     got = lax.all_to_all(send, "expert", split_axis=0, concat_axis=0, tiled=True)
-    rows = lax.all_gather(got, GROUP, axis=0, tiled=True)
-    terms, rows = lax.optimization_barrier((terms, rows))
-    summed = lax.psum_scatter(terms, GROUP, scatter_dimension=0, tiled=True)
+
+    code_rows = jnp.zeros((8, 2 * model_width), jnp.bfloat16)
+    code_rows = code_rows.at[0, : 2 * count_tok].set(weight_codes.reshape(-1).astype(jnp.bfloat16))
+    parcel = jnp.concatenate(
+        [got, jnp.concatenate([tokens, cotangent], axis=1), code_rows], axis=0
+    )
+    per_dev = parcel.shape[0]
+    full_cols, parcel = lax.optimization_barrier((full_cols, parcel))
+    gate_cols = full_cols[:, :hid]
+    up_cols = full_cols[:, hid : 2 * hid]
+    down_cols = full_cols[:, 2 * hid :]
+    gate_up_cols = full_cols[:, : 2 * hid]
+    gathered = lax.all_gather(parcel, ("tensor", "dp"), axis=0, tiled=True)
+    gathered = gathered.reshape(-1, per_dev, 2 * model_width)
+    rows = gathered[:, :slots_here].reshape(-1, 2 * model_width)
+    plane = gathered[:, slots_here : slots_here + count_tok].reshape(-1, 2 * model_width)
+    plane_codes = gathered[:, slots_here + count_tok, : 2 * count_tok].reshape(-1, 2)
+    plane_x = plane[:, :model_width]
+    plane_dy = plane[:, model_width:].astype(jnp.float32)
+    plane_scale = plane_codes.astype(jnp.float32) / 256.0
+
+    up_pre, activation, act_slope, hidden = forward_parts(plane_x, gate_cols, up_cols)
+    out_term = contract_cols(hidden, down_cols).astype(jnp.bfloat16)
+    grad_term = jnp.zeros(out_term.shape, jnp.float32)
+    for which in range(2):
+        scaled = (plane_scale[:, which : which + 1] * plane_dy).astype(jnp.bfloat16)
+        gate_grad, up_grad = grad_parts(scaled, down_cols, up_pre, activation, act_slope)
+        grad_term = grad_term + contract_cols(
+            jnp.concatenate([gate_grad, up_grad], axis=1), gate_up_cols
+        )
+    terms = jnp.concatenate([out_term, grad_term.astype(jnp.bfloat16)], axis=1)
+    part = lax.psum_scatter(terms, "tensor", scatter_dimension=0, tiled=True)
+    summed = lax.psum_scatter(part, "dp", scatter_dimension=0, tiled=True)
     expert_out = summed[:, :model_width].astype(jnp.float32)
     code_scale = weight_codes.astype(jnp.float32) / 256.0
     mixed = (code_scale[:, 0:1] * expert_out + code_scale[:, 1:2] * expert_out).astype(

time: 280 us -> 335 us (1.20)
  waiting for transfers between devices: 194 us -> 248 us
  blocking collectives: 24.4 us -> 0 us
  local copies, waits for them, and re-layouts: 7.38 us -> 24.6 us
  starting transfers between devices: 0.16 us -> 8.87 us
  matrix products: 27.5 us -> 31.4 us
  other arithmetic: 11.4 us -> 7.78 us
    all_gather x2 -> x1, waiting for transfers between devices: 73.7 us -> 108 us  [shards(): gathered = lax.all_gather(parcel, ('tensor', 'dp'), axis=0, tiled=True)]
    all_to_all x1 -> x0, blocking collectives: 24.4 us -> none  [shards(): lax.all_to_all(send, 'expert', split_axis=0, concat_axis=0, tiled=True)]
    all_gather x1, waiting for transfers between devices: 45.2 us -> 21.2 us  [shards(): full_cols = lax.all_gather(stacked, 'expert', axis=0, tiled=True)]
    reduce_scatter x1 -> x2, waiting for transfers between devices: 75.4 us -> 96.9 us  [the longest x1 69.4 us: shards(): summed = lax.psum_scatter(part, 'dp', scatter_dimension=0, tiled=True)]
    all_to_all x0 -> x1, waiting for transfers between devices: none -> 21.4 us  [shards(): lax.all_to_all(send, 'expert', split_axis=0, concat_axis=0, tiled=True)]
    slice x0 -> x3, local copies, waits for them, and re-layouts: none -> 13.1 us  [the longest x1 9.62 us: shards(): rows = gathered[:, :slots_here].reshape(-1, 2 * model_width)]
    all_to_all x0 -> x1, starting transfers between devices: none -> 8.57 us  [shards(): lax.all_to_all(send, 'expert', split_axis=0, concat_axis=0, tiled=True)]
    unnamed x10 -> x33, local copies, waits for them, and re-layouts: 2.25 us -> 5.93 us
  transfers between devices with their start and end apart: 4 -> 5, of which waited for: 4 -> 5; matrix products, arithmetic and copies ran while one was open for 13% -> 11% of each run, Pallas kernels for 0% -> 0%
where the time goes in v3:
time: 335 us; the launch traced here: 334 us
  waiting for transfers between devices  248 us (74%)
  matrix products  31.4 us (9%)
  local copies, waits for them, and re-layouts  24.6 us (7%)
  between operations  14.1 us (4%)
  starting transfers between devices  8.87 us (3%)
  other arithmetic  7.78 us (2%)
    all_gather x1, waiting for transfers between devices, shards(): gathered = lax.all_gather(parcel, ('tensor', 'dp'), axis=0, tiled=True)  108 us
    reduce_scatter x1, waiting for transfers between devices, shards(): summed = lax.psum_scatter(part, 'dp', scatter_dimension=0, tiled=True)  69.4 us
    reduce_scatter x1, waiting for transfers between devices, shards(): part = lax.psum_scatter(terms, 'tensor', scatter_dimension=0, tiled=True)  27.5 us
    all_to_all x1, waiting for transfers between devices, shards(): lax.all_to_all(send, 'expert', split_axis=0, concat_axis=0, tiled=True)  21.4 us
    all_gather x1, waiting for transfers between devices, shards(): full_cols = lax.all_gather(stacked, 'expert', axis=0, tiled=True)  21.2 us
    dot_general x3, matrix products, contract_rows(): lax.dot_general(left_side, right_side, (((0,), (0,)), ((), ())), preferre...  11 us
    slice x1, local copies, waits for them, and re-layouts, shards(): rows = gathered[:, :slots_here].reshape(-1, 2 * model_width)  9.62 us
    all_to_all x1, starting transfers between devices, shards(): lax.all_to_all(send, 'expert', split_axis=0, concat_axis=0, tiled=True)  8.57 us
  transfers between devices with their start and end apart: 5, of which 5 were waited for; matrix products, arithmetic and copies ran while one was open for 11% of the time, Pallas kernels for 0%

profile of v3, /device:TPU:32, one launch (start us, length us, event | category | flops | bytes accessed | tf_op | source)
XLA Modules:
  0.0 334.2 jit_solution(11498404752860518179)
XLA Ops:
  7.2 1.8 pad_maximum_fusion.1
  9.1 1.0 broadcast_in_dim.21
  10.0 0.2 convert_element_type.102
  10.2 0.7 convert_multiply_fusion.3
  10.9 0.1 copy.16
  11.0 0.1 div.26
  11.1 0.8 copy.15
  11.9 0.9 broadcast_in_dim.20
  13.1 0.2 select_reduce_fusion
  13.2 0.2 convolution_convert_fusion.2
  13.4 0.2 convolution_convert_fusion.1
  13.7 0.9 all_to_all.8
  14.6 8.6 %all-to-all-start = ((bf16[8,5,4096]{2,1,0:T(8,128)(2,1)}), bf16[8,5,4096]{2,1,0:T(8,128)(2,1)S(1)}, u32[]{:S(2)}, u32[]{:S(2)}) async-start(bf16[8,5,4096]{2,1,0:T(8,128)(2,1)} %all_to_all.8), calls=%async_computation | async-start | bytes 1048576 | tf_op jit(solution)/shard_map/all_to_all | solution.py:72
  23.2 0.1 copy.17
  23.3 0.1 convert_element_type.106
  23.4 21.4 %all-to-all-done = bf16[8,5,4096]{2,1,0:T(8,128)(2,1)S(1)} async-done(((bf16[8,5,4096]{2,1,0:T(8,128)(2,1)}), bf16[8,5,4096]{2,1,0:T(8,128)(2,1)S(1)}, u32[]{:S(2)}, u32[]{:S(2)}) %all-to-all-start) | async-done | bytes 327712 | tf_op jit(solution)/shard_map/all_to_all | solution.py:72
  44.9 0.1 all_to_all.10
  45.0 0.8 fusion.58
  45.9 21.2 %all-gather.3.cloned.1.call-done = bf16[2048,768]{1,0:T(8,128)(2,1)} async-done(((bf16[256,768]{1,0:T(8,128)(2,1)}), bf16[2048,768]{1,0:T(8,128)(2,1)}) %all-gather.3.cloned.1.call-update) | async-done | bytes 3145744 | tf_op jit(solution)/shard_map/all_gather | solution.py:49
  67.1 107.9 %all-gather.5.cloned.1.call-done = bf16[2048,4096]{1,0:T(8,128)(2,1)} async-done(((bf16[64,4096]{1,0:T(8,128)(2,1)}), bf16[2048,4096]{1,0:T(8,128)(2,1)}) %all-gather.5.cloned.1.call-update) | async-done | bytes 16777232 | tf_op jit(solution)/shard_map/all_gather | solution.py:85
  175.0 2.6 slice.84
  177.6 0.5 copy-done.3
  178.2 1.6 fusion.40
  179.8 1.6 fusion.42
  181.4 0.9 slice.86
  182.2 0.2 div.30
  182.4 0.3 slice_reduce_fusion
  182.7 2.4 fusion.34
  185.2 0.8 convolution_convert_fusion
  186.0 1.4 copy-done.2
  187.4 1.1 multiply_convert_fusion.7
  188.5 1.3 fusion.45
  189.8 1.3 add_convert_fusion
  191.1 2.6 pad_maximum_fusion
  193.7 0.2 reduce-scatter.5.cloned.1.call-start
  193.9 9.6 %slice.92 = bf16[32,40,4096]{2,1,0:T(8,128)(2,1)} slice(bf16[32,64,4096]{2,1,0:T(8,128)(2,1)} %bitcast.16), slice={[0:32], [0:40], [0:4096]} | slice | bytes 20971520 | tf_op jit(solution)/shard_map/slice | solution.py:87
  203.6 4.2 %fusion.10 = f32[1280,256]{1,0:T(8,128)S(1)} fusion(bf16[1280,4096]{1,0:T(8,128)(2,1)} %bitcast.17, bf16[2048,768]{1,0:T(8,128)(2,1)S(1)} %copy-done.3), kind=kOutput, calls=%fused_computation.14 | convolution fusion | flops 1342177280 | bytes 7602176 | tf_op jit(solution)/shard_map/dot_general | solution.py:27
  207.8 2.1 copy-done
  209.9 1.5 fusion.2
  211.4 1.1 copy-done.11
  212.5 2.7 fusion.26
  215.2 27.5 %reduce-scatter.3.cloned.1.call-done = bf16[128,4096]{1,0:T(8,128)(2,1)} async-done(((bf16[512,4096]{1,0:T(8,128)(2,1)}), bf16[128,4096]{1,0:T(8,128)(2,1)}) %reduce-scatter.3.cloned.1.call-update) | async-done | bytes 1048592 | tf_op jit(solution)/shard_map/reduce_scatter | solution.py:104
  242.8 4.2 %fusion.12 = f32[1280,256]{1,0:T(8,128)S(1)} fusion(bf16[1280,4096]{1,0:T(8,128)(2,1)} %bitcast.18, bf16[2048,768]{1,0:T(8,128)(2,1)S(1)} %copy-done.3), kind=kOutput, calls=%fused_computation.16 | convolution fusion | flops 1342177280 | bytes 7602176 | tf_op jit(solution)/shard_map/dot_general | solution.py:28
  247.0 5.4 %fusion.23 = bf16[1,2048,256]{2,1,0:T(8,128)(2,1)} fusion(bf16[1280,4096]{1,0:T(8,128)(2,1)} %bitcast.19, f32[1280,256]{1,0:T(8,128)S(1)} %fusion.12, f32[1280,256]{1,0:T(8,128)S(1)} %copy-done.10), kind=kOutput, calls=%fused_computation.22 | convolution fusion | flops 1344667648 | bytes 8912896 | tf_op jit(solution)/shard_map/dot_general | solution.py:15
  252.5 2.8 fusion.29
  255.3 69.4 %reduce-scatter.5.cloned.1.call-done = bf16[16,4096]{1,0:T(8,128)(2,1)} async-done(((bf16[128,4096]{1,0:T(8,128)(2,1)}), bf16[16,4096]{1,0:T(8,128)(2,1)}) %reduce-scatter.5.cloned.1.call-update) | async-done | bytes 131088 | tf_op jit(solution)/shard_map/reduce_scatter | solution.py:105
  324.7 1.5 slice.91
  326.2 1.5 multiply_convert_fusion.14
  (45 shorter events, 0.5 us)
Async XLA Ops:
  7.2 16.1 %copy-start.6 = (s32[16,2]{0,1:T(2,128)S(1)}, s32[16,2]{0,1:T(2,128)}, u32[]{:S(2)}) copy-start(s32[16,2]{0,1:T(2,128)} %param.12) | copy-start | bytes 388
  7.2 59.9 %all-gather.3.cloned.1.call-start = ((), (), s32[]{:S(2)}) async-start(), calls=%async_computation.3 | async-start | bytes 3538944 | tf_op jit(solution)/shard_map/all_gather | solution.py:49
  9.0 36.0 %copy-start.4 = (bf16[16,2048]{1,0:T(8,128)(2,1)S(1)}, bf16[16,2048]{1,0:T(8,128)(2,1)}, u32[]{:S(2)}) copy-start(bf16[16,2048]{1,0:T(8,128)(2,1)} %param.10) | copy-start | bytes 196612
  9.0 36.0 %copy-start.5 = (bf16[16,2048]{1,0:T(8,128)(2,1)S(1)}, bf16[16,2048]{1,0:T(8,128)(2,1)}, u32[]{:S(2)}) copy-start(bf16[16,2048]{1,0:T(8,128)(2,1)} %param.9) | copy-start | bytes 196612
  14.6 30.2 %all-to-all-start = ((bf16[8,5,4096]{2,1,0:T(8,128)(2,1)}), bf16[8,5,4096]{2,1,0:T(8,128)(2,1)S(1)}, u32[]{:S(2)}, u32[]{:S(2)}) async-start(bf16[8,5,4096]{2,1,0:T(8,128)(2,1)} %all_to_all.8), calls=%async_computation | async-start | bytes 1048576 | tf_op jit(solution)/shard_map/all_to_all | solution.py:72
  23.2 151.8 %all-gather.5.cloned.1.call-start = ((), (), s32[]{:S(2)}) async-start(), calls=%async_computation.4 | async-start | bytes 17301504 | tf_op jit(solution)/shard_map/all_gather | solution.py:85
  67.1 175.7 %reduce-scatter.3.cloned.1.call-start = ((), (), s32[]{:S(2)}) async-start(), calls=%async_computation.5 | async-start | bytes 5242880 | tf_op jit(solution)/shard_map/reduce_scatter | solution.py:104
  175.0 3.2 copy-start.3
  177.6 3.7 %copy-start.1 = (bf16[32,16,4096]{2,1,0:T(8,128)(2,1)}, bf16[32,16,4096]{2,1,0:T(8,128)(2,1)S(1)}, u32[]{:S(2)}) copy-start(bf16[32,16,4096]{2,1,0:T(8,128)(2,1)S(1)} %slice.84) | copy-start | bytes 12582916
  182.4 2.8 copy-start.7
  182.4 2.8 copy-start.8
  185.2 2.2 copy-start.2
  193.7 131.0 %reduce-scatter.5.cloned.1.call-start = ((), (), s32[]{:S(2)}) async-start(), calls=%async_computation.6 | async-start | bytes 1179648 | tf_op jit(solution)/shard_map/reduce_scatter | solution.py:105
  203.6 6.3 %copy-start = (bf16[32,40,4096]{2,1,0:T(8,128)(2,1)S(1)}, bf16[32,40,4096]{2,1,0:T(8,128)(2,1)}, u32[]{:S(2)}) copy-start(bf16[32,40,4096]{2,1,0:T(8,128)(2,1)} %slice.92) | copy-start | bytes 31457284
  209.9 1.5 copy-start.9
  211.4 1.1 copy-start.11
  242.8 4.2 %copy-start.10 = (f32[1280,256]{1,0:T(8,128)S(1)}, f32[1280,256]{1,0:T(8,128)}, u32[]{:S(2)}) copy-start(f32[1280,256]{1,0:T(8,128)} %copy-done.9) | copy-start | bytes 3932164
  242.8 9.6 %slice-start = ((s8[10485760]{0:T(1024)(128)(4,1)}), s8[4194304]{0:T(1024)(128)(4,1)S(1)}, s32[]{:S(2)}) async-start(s8[10485760]{0:T(1024)(128)(4,1)} %bitcast.22), calls=%async_computation.7 | async-start | bytes 8388608
  242.8 9.6 %slice-start.1 = ((s8[10485760]{0:T(1024)(128)(4,1)}), s8[4194304]{0:T(1024)(128)(4,1)S(1)}, s32[]{:S(2)}) async-start(s8[10485760]{0:T(1024)(128)(4,1)} %bitcast.22), calls=%async_computation.8 | async-start | bytes 8388608
  247.0 5.4 %slice-start.2 = ((s8[10485760]{0:T(1024)(128)(4,1)}), s8[2097152]{0:T(1024)(128)(4,1)S(1)}, s32[]{:S(2)}) async-start(s8[10485760]{0:T(1024)(128)(4,1)} %bitcast.22), calls=%async_computation.9 | async-start | bytes 4194304
  247.0 5.4 %copy-start.12 = (f32[1280,256]{1,0:T(8,128)S(1)}, f32[1280,256]{1,0:T(8,128)}, u32[]{:S(2)}) copy-start(f32[1280,256]{1,0:T(8,128)} %copy-done.11) | copy-start | bytes 3932164
Sparse Core Ops, SparseCore 0:
  10.4 56.6 all-gather.2
  69.4 105.5 all-gather.4
  193.8 48.8 reduce-scatter.2
  247.0 77.6 reduce-scatter.4

commit v4 on v2

--- a/solution.py
+++ b/solution.py
@@ -46,7 +46,9 @@
     slots_here = experts * capacity
 
     stacked = jnp.concatenate([dense_gate, dense_up, dense_down_t], axis=1)
-    full_cols = lax.all_gather(stacked, "expert", axis=0, tiled=True)
+    copies = jnp.broadcast_to(stacked[None], (experts,) + stacked.shape)
+    full_cols = lax.all_to_all(copies, "expert", split_axis=0, concat_axis=0, tiled=True)
+    full_cols = full_cols.reshape(-1, stacked.shape[1])
     gate_cols = full_cols[:, :hid]
     up_cols = full_cols[:, hid : 2 * hid]
     down_cols = full_cols[:, 2 * hid :]

time: 280 us -> 234 us (0.84)
  waiting for transfers between devices: 194 us -> 145 us
  starting transfers between devices: 0.16 us -> 5.09 us
    all_to_all x0 -> x1, waiting for transfers between devices: none -> 52.3 us  [shards(): lax.all_to_all(copies, 'expert', split_axis=0, concat_axis=0, tiled=True)]
    all_gather x1, waiting for transfers between devices: 51.4 us -> 0.01 us  [shards(): rows = lax.all_gather(got, GROUP, axis=0, tiled=True)]
    all_gather x1 -> x0, waiting for transfers between devices: 45.2 us -> none  [shards(): full_cols = lax.all_gather(stacked, 'expert', axis=0, tiled=True)]
    all_gather x1, waiting for transfers between devices: 22.3 us -> 17.2 us  [shards(): plane = lax.all_gather(home, GROUP, axis=0, tiled=True)]
    all_to_all x0 -> x1, starting transfers between devices: none -> 5.01 us  [shards(): lax.all_to_all(copies, 'expert', split_axis=0, concat_axis=0, tiled=True)]
  transfers between devices with their start and end apart: 4 -> 4, of which waited for: 4 -> 3; matrix products, arithmetic and copies ran while one was open for 13% -> 15% of each run, Pallas kernels for 0% -> 0%
where the time goes in v4:
time: 234 us; the launch traced here: 233 us
  waiting for transfers between devices  145 us (62%)
  matrix products  25.5 us (11%)
  blocking collectives  24.4 us (10%)
  between operations  13.9 us (6%)
  local copies, waits for them, and re-layouts  9.68 us (4%)
  other arithmetic  9.66 us (4%)
  starting transfers between devices  5.09 us (2%)
    reduce_scatter x1, waiting for transfers between devices, shards(): summed = lax.psum_scatter(terms, GROUP, scatter_dimension=0, tiled=True)  75.5 us
    all_to_all x1, waiting for transfers between devices, shards(): lax.all_to_all(copies, 'expert', split_axis=0, concat_axis=0, tiled=True)  52.3 us
    all_to_all x1, blocking collectives, shards(): lax.all_to_all(send, 'expert', split_axis=0, concat_axis=0, tiled=True)  24.4 us
    all_gather x1, waiting for transfers between devices, shards(): plane = lax.all_gather(home, GROUP, axis=0, tiled=True)  17.2 us
    dot_general x3, matrix products, contract_rows(): lax.dot_general(left_side, right_side, (((0,), (0,)), ((), ())), preferre...  8.86 us
    all_to_all x1, starting transfers between devices, shards(): lax.all_to_all(copies, 'expert', split_axis=0, concat_axis=0, tiled=True)  5.01 us
    dot_general x2, matrix products, forward_parts(): gate_pre = jnp.dot(rows_x, gate_cols, preferred_element_type=jnp.float32)  4.97 us
  transfers between devices with their start and end apart: 4, of which 3 were waited for; matrix products, arithmetic and copies ran while one was open for 15% of the time, Pallas kernels for 0%

profile of v4, /device:TPU:32, one launch (start us, length us, event | category | flops | bytes accessed | tf_op | source)
XLA Modules:
  0.0 233.3 jit_solution(5199747582437725239)
XLA Ops:
  7.2 0.0 all-gather.3.cloned.1.call-start
  7.2 0.6 compare_reduce_fusion
  7.9 1.3 broadcast_select_fusion
  9.2 0.1 copy.18
  9.3 1.6 fusion.67
  10.9 0.0 all-gather.5.cloned.1.call-start
  10.9 0.9 broadcast_in_dim.28
  11.9 0.2 convert_element_type.105
  12.1 0.7 convert_multiply_fusion.3
  12.8 0.1 copy.17
  12.9 0.1 div.27
  12.9 0.8 copy.16
  13.7 0.1 reshape.70
  13.8 0.9 broadcast_in_dim.13
  14.7 0.1 reshape.71
  14.8 0.1 fusion.69
  14.8 0.1 reduce_window_sum.11
  14.9 0.2 select_reduce_fusion
  15.1 0.2 convolution_convert_fusion.2
  15.3 0.2 convolution_convert_fusion.1
  15.6 0.1 all_to_all.12
  15.7 24.4 %all_to_all.17 = bf16[8,5,4096]{2,1,0:T(8,128)(2,1)S(1)} all-to-all(bf16[8,5,4096]{2,1,0:T(8,128)(2,1)S(1)} %all_to_all.12), channel_id=1, replica_groups=mesh['dp'=8,'expert'=8,'tensor'=4] {'expert'}, dimensions={0} | all-to-all | bytes 655360 | tf_op jit(solution)/shard_map/all_to_all | solution.py:93
  40.1 0.9 all_to_all.14
  41.1 1.8 broadcast_in_dim.12
  42.9 5.0 %all-to-all-start = ((bf16[8,256,768]{2,1,0:T(8,128)(2,1)}), bf16[8,256,768]{2,1,0:T(8,128)(2,1)S(1)}, u32[]{:S(2)}, u32[]{:S(2)}) async-start(bf16[8,256,768]{2,1,0:T(8,128)(2,1)} %broadcast_in_dim.12), calls=%async_computation | async-start | bytes 6291456 | tf_op jit(solution)/shard_map/all_to_all | solution.py:50
  47.9 17.2 %all-gather.3.cloned.1.call-done = bf16[512,4224]{1,0:T(8,128)(2,1)} async-done(((bf16[16,4224]{1,0:T(8,128)(2,1)}), bf16[512,4224]{1,0:T(8,128)(2,1)}) %all-gather.3.cloned.1.call-update) | async-done | bytes 4325392 | tf_op jit(solution)/shard_map/all_gather | solution.py:60
  65.1 0.9 convert_multiply_fusion.2
  66.1 0.3 slice_reduce_fusion
  66.4 52.3 %all-to-all-done = bf16[8,256,768]{2,1,0:T(8,128)(2,1)S(1)} async-done(((bf16[8,256,768]{2,1,0:T(8,128)(2,1)}), bf16[8,256,768]{2,1,0:T(8,128)(2,1)S(1)}, u32[]{:S(2)}, u32[]{:S(2)}) %all-to-all-start) | async-done | bytes 3145760 | tf_op jit(solution)/shard_map/all_to_all | solution.py:50
  118.6 2.7 %fusion.43 = f32[512,256]{0,1:T(8,128)S(1)} fusion(bf16[512,4224]{1,0:T(8,128)(2,1)} %all-gather.3.cloned.1.call-done, bf16[2048,768]{1,0:T(8,128)(2,1)S(1)} %bitcast.10), kind=kOutput, calls=%fused_computation.36 | convolution fusion | flops 536870912 | bytes 3670016 | tf_op jit(solution)/shard_map/dot_general | solution.py:28
  121.3 0.5 copy-done.3
  121.9 0.8 fusion.45
  122.7 0.8 convolution_convert_fusion
  123.4 0.9 fusion.34
  124.4 1.2 multiply_convert_fusion.7
  125.5 1.3 fusion.39
  126.8 1.3 add_convert_fusion
  128.2 2.6 %pad_maximum_fusion = bf16[512,4096]{1,0:T(8,128)(2,1)} fusion(bf16[512,2048]{1,0:T(8,128)(2,1)S(1)} %add_convert_fusion, bf16[512,2048]{1,0:T(8,128)(2,1)S(1)} %convolution_convert_fusion), kind=kLoop, calls=%fused_computation.8 | loop fusion | flops 8388608 | bytes 8388608 | tf_op jit(solution)/shard_map/concatenate | solution.py:74
  130.8 4.2 %fusion.10 = f32[1280,256]{1,0:T(8,128)S(1)} fusion(bf16[1280,4096]{1,0:T(8,128)(2,1)} %all-gather.5.cloned.1.call-done, bf16[2048,768]{1,0:T(8,128)(2,1)S(1)} %bitcast.17), kind=kOutput, calls=%fused_computation.14 | convolution fusion | flops 1342177280 | bytes 7602176 | tf_op jit(solution)/shard_map/dot_general | solution.py:27
  135.0 1.3 copy-done.4
  136.3 1.5 fusion.2
  137.9 1.6 fusion.12
  139.4 3.0 %fusion.26 = bf16[1,2048,256]{2,1,0:T(8,128)(2,1)} fusion(bf16[1280,4096]{1,0:T(8,128)(2,1)S(1)} %copy-done.4, f32[1280,256]{1,0:T(8,128)S(1)} %fusion.2, f32[1280,256]{1,0:T(8,128)S(1)} %fusion.10), kind=kOutput, calls=%fused_computation.23 | convolution fusion | flops 1344667648 | bytes 8912896 | tf_op jit(solution)/shard_map/dot_general | solution.py:15
  142.5 2.9 %fusion.23 = bf16[1,2048,256]{2,1,0:T(8,128)(2,1)} fusion(bf16[1280,4096]{1,0:T(8,128)(2,1)S(1)} %copy-done.4, f32[1280,256]{1,0:T(8,128)S(1)} %fusion.12, f32[1280,256]{1,0:T(8,128)S(1)} %fusion.10), kind=kOutput, calls=%fused_computation.22 | convolution fusion | flops 1344667648 | bytes 8912896 | tf_op jit(solution)/shard_map/dot_general | solution.py:15
  145.3 3.0 %fusion.29 = bf16[1,2048,256]{2,1,0:T(8,128)(2,1)} fusion(bf16[1280,4096]{1,0:T(8,128)(2,1)S(1)} %copy-done.4, f32[1280,256]{1,0:T(8,128)S(1)} %fusion.10, f32[1280,256]{1,0:T(8,128)S(1)} %fusion.2, f32[1280,256]{1,0:T(8,128)S(1)} %fusion.12), kind=kOutput, calls=%fused_computation.24 | convolution fusion | flops 1345978368 | bytes 10223616 | tf_op jit(solution)/shard_map/dot_general | solution.py:15
  148.3 75.5 %reduce-scatter.2.cloned.1.call-done = bf16[16,4096]{1,0:T(8,128)(2,1)} async-done(((bf16[512,4096]{1,0:T(8,128)(2,1)}), bf16[16,4096]{1,0:T(8,128)(2,1)}) %reduce-scatter.2.cloned.1.call-update) | async-done | bytes 131088 | tf_op jit(solution)/shard_map/reduce_scatter | solution.py:96
  223.7 1.5 slice.86
  225.2 1.5 multiply_convert_fusion.14
  (17 shorter events, 0.1 us)
Async XLA Ops:
  7.2 58.0 %all-gather.3.cloned.1.call-start = ((), (), s32[]{:S(2)}) async-start(), calls=%async_computation.3 | async-start | bytes 4460544 | tf_op jit(solution)/shard_map/all_gather | solution.py:60
  9.3 31.7 %copy-start = (bf16[256,256]{1,0:T(8,128)(2,1)S(1)}, bf16[256,256]{1,0:T(8,128)(2,1)}, u32[]{:S(2)}) copy-start(bf16[256,256]{1,0:T(8,128)(2,1)} %param.15) | copy-start | bytes 393220
  9.3 31.7 %copy-start.1 = (bf16[256,256]{1,0:T(8,128)(2,1)S(1)}, bf16[256,256]{1,0:T(8,128)(2,1)}, u32[]{:S(2)}) copy-start(bf16[256,256]{1,0:T(8,128)(2,1)} %param.14) | copy-start | bytes 393220
  9.3 31.7 %copy-start.2 = (bf16[256,256]{1,0:T(8,128)(2,1)S(1)}, bf16[256,256]{1,0:T(8,128)(2,1)}, u32[]{:S(2)}) copy-start(bf16[256,256]{1,0:T(8,128)(2,1)} %param.13) | copy-start | bytes 393220
  10.9 119.8 %all-gather.5.cloned.1.call-start = ((), (), s32[]{:S(2)}) async-start(), calls=%async_computation.4 | async-start | bytes 10813440 | tf_op jit(solution)/shard_map/all_gather | solution.py:94
  42.9 75.7 %all-to-all-start = ((bf16[8,256,768]{2,1,0:T(8,128)(2,1)}), bf16[8,256,768]{2,1,0:T(8,128)(2,1)S(1)}, u32[]{:S(2)}, u32[]{:S(2)}) async-start(bf16[8,256,768]{2,1,0:T(8,128)(2,1)} %broadcast_in_dim.12), calls=%async_computation | async-start | bytes 6291456 | tf_op jit(solution)/shard_map/all_to_all | solution.py:50
  47.9 175.8 %reduce-scatter.2.cloned.1.call-start = ((), (), s32[]{:S(2)}) async-start(), calls=%async_computation.5 | async-start | bytes 4325376 | tf_op jit(solution)/shard_map/reduce_scatter | solution.py:96
  118.6 3.2 %copy-start.3 = (bf16[512,4224]{1,0:T(8,128)(2,1)S(1)}, bf16[512,4224]{1,0:T(8,128)(2,1)}, u32[]{:S(2)}) copy-start(bf16[512,4224]{1,0:T(8,128)(2,1)} %all-gather.3.cloned.1.call-done) | copy-start | bytes 12976132
  130.8 5.5 %copy-start.4 = (bf16[1280,4096]{1,0:T(8,128)(2,1)S(1)}, bf16[1280,4096]{1,0:T(8,128)(2,1)}, u32[]{:S(2)}) copy-start(bf16[1280,4096]{1,0:T(8,128)(2,1)} %all-gather.5.cloned.1.call-done) | copy-start | bytes 31457284
Sparse Core Ops, SparseCore 0:
  11.2 53.9 all-gather.2
  68.2 62.2 all-gather.4
  134.5 89.1 reduce-scatter.1

commit v5 on v4

--- a/solution.py
+++ b/solution.py
@@ -92,14 +92,16 @@
     send = jnp.concatenate([send_x, send_s], axis=1)
     got = lax.all_to_all(send, "expert", split_axis=0, concat_axis=0, tiled=True)
     rows = lax.all_gather(got, GROUP, axis=0, tiled=True)
-    terms, rows = lax.optimization_barrier((terms, rows))
-    summed = lax.psum_scatter(terms, GROUP, scatter_dimension=0, tiled=True)
-    expert_out = summed[:, :model_width].astype(jnp.float32)
+    n_group = terms.shape[0] // count_tok
+    pieces = terms.reshape(n_group, count_tok, 2 * model_width)
+    pieces = lax.all_to_all(pieces, GROUP, split_axis=0, concat_axis=0, tiled=True)
+    summed = jnp.sum(pieces.astype(jnp.float32), axis=0)
+    expert_out = summed[:, :model_width].astype(jnp.bfloat16).astype(jnp.float32)
     code_scale = weight_codes.astype(jnp.float32) / 256.0
     mixed = (code_scale[:, 0:1] * expert_out + code_scale[:, 1:2] * expert_out).astype(
         jnp.bfloat16
     )
-    input_grad = summed[:, model_width:]
+    input_grad = summed[:, model_width:].astype(jnp.bfloat16)
     rows_x = rows[:, :model_width]
     rows_s = rows[:, model_width:]
     r_up, r_act, r_slope, r_hidden = forward_parts(rows_x, gate_cols, up_cols)

time: 234 us -> 220 us (0.940)
  waiting for transfers between devices: 145 us -> 123 us
  starting transfers between devices: 5.09 us -> 12.7 us
    reduce_scatter x1 -> x0, waiting for transfers between devices: 75.5 us -> none  [shards(): summed = lax.psum_scatter(terms, GROUP, scatter_dimension=0, tiled=True)]
    all_to_all x0 -> x1, waiting for transfers between devices: none -> 53.3 us  [shards(): lax.all_to_all(pieces, GROUP, split_axis=0, concat_axis=0, tiled=True)]
    all_to_all x0 -> x1, starting transfers between devices: none -> 7.62 us  [shards(): lax.all_to_all(pieces, GROUP, split_axis=0, concat_axis=0, tiled=True)]
    reduce_sum x0 -> x1, other arithmetic: none -> 2.83 us  [shards(): summed = jnp.sum(pieces.astype(jnp.float32), axis=0)]
  transfers between devices with their start and end apart: 4 -> 4, of which waited for: 3 -> 3; matrix products, arithmetic and copies ran while one was open for 15% -> 11% of each run, Pallas kernels for 0% -> 0%
where the time goes in v5:
time: 220 us
  waiting for transfers between devices  123 us (56%)
  matrix products  25.4 us (12%)
  blocking collectives  24.4 us (11%)
  between operations  14.2 us (6%)
  starting transfers between devices  12.7 us (6%)
  other arithmetic  11.6 us (5%)
  local copies, waits for them, and re-layouts  8.85 us (4%)
    all_to_all x1, waiting for transfers between devices, shards(): lax.all_to_all(pieces, GROUP, split_axis=0, concat_axis=0, tiled=True)  53.3 us
    all_to_all x1, waiting for transfers between devices, shards(): lax.all_to_all(copies, 'expert', split_axis=0, concat_axis=0, tiled=True)  52.3 us
    all_to_all x1, blocking collectives, shards(): lax.all_to_all(send, 'expert', split_axis=0, concat_axis=0, tiled=True)  24.4 us
    all_gather x1, waiting for transfers between devices, shards(): plane = lax.all_gather(home, GROUP, axis=0, tiled=True)  17.2 us
    dot_general x3, matrix products, contract_rows(): lax.dot_general(left_side, right_side, (((0,), (0,)), ((), ())), preferre...  8.68 us
    all_to_all x1, starting transfers between devices, shards(): lax.all_to_all(pieces, GROUP, split_axis=0, concat_axis=0, tiled=True)  7.62 us
    all_to_all x1, starting transfers between devices, shards(): lax.all_to_all(copies, 'expert', split_axis=0, concat_axis=0, tiled=True)  5.01 us
    dot_general x2, matrix products, forward_parts(): gate_pre = jnp.dot(rows_x, gate_cols, preferred_element_type=jnp.float32)  4.97 us
  transfers between devices with their start and end apart: 4, of which 3 were waited for; matrix products, arithmetic and copies ran while one was open for 11% of the time, Pallas kernels for 0%

profile of v5, /device:TPU:32, one launch (start us, length us, event | category | flops | bytes accessed | tf_op | source)
XLA Modules:
  0.0 219.9 jit_solution(16622830076091332177)
XLA Ops:
  7.2 0.6 compare_reduce_fusion
  7.9 1.3 broadcast_select_fusion
  9.2 0.1 copy.18
  9.3 1.6 fusion.67
  10.9 0.9 broadcast_in_dim.28
  11.9 0.2 convert_element_type.113
  12.1 0.7 convert_multiply_fusion.3
  12.8 0.1 copy.17
  12.9 0.1 div.27
  12.9 0.8 copy.16
  13.7 0.1 reshape.74
  13.8 0.9 broadcast_in_dim.13
  14.7 0.1 reshape.75
  14.8 0.1 fusion.69
  14.8 0.1 reduce_window_sum.11
  14.9 0.2 select_reduce_fusion
  15.1 0.2 convolution_convert_fusion.2
  15.3 0.2 convolution_convert_fusion.1
  15.6 0.1 all_to_all.16
  15.7 24.4 %all_to_all.22 = bf16[8,5,4096]{2,1,0:T(8,128)(2,1)S(1)} all-to-all(bf16[8,5,4096]{2,1,0:T(8,128)(2,1)S(1)} %all_to_all.16), channel_id=1, replica_groups=mesh['dp'=8,'expert'=8,'tensor'=4] {'expert'}, dimensions={0} | all-to-all | bytes 655360 | tf_op jit(solution)/shard_map/all_to_all | solution.py:93
  40.1 0.9 all_to_all.18
  41.1 1.8 broadcast_in_dim.12
  42.9 5.0 %all-to-all-start = ((bf16[8,256,768]{2,1,0:T(8,128)(2,1)}), bf16[8,256,768]{2,1,0:T(8,128)(2,1)S(1)}, u32[]{:S(2)}, u32[]{:S(2)}) async-start(bf16[8,256,768]{2,1,0:T(8,128)(2,1)} %broadcast_in_dim.12), calls=%async_computation | async-start | bytes 6291456 | tf_op jit(solution)/shard_map/all_to_all | solution.py:50
  47.9 17.2 %all-gather.3.cloned.1.call-done = bf16[512,4224]{1,0:T(8,128)(2,1)} async-done(((bf16[16,4224]{1,0:T(8,128)(2,1)}), bf16[512,4224]{1,0:T(8,128)(2,1)}) %all-gather.3.cloned.1.call-update) | async-done | bytes 4325392 | tf_op jit(solution)/shard_map/all_gather | solution.py:60
  65.1 0.9 convert_multiply_fusion.2
  66.1 0.3 slice_reduce_fusion
  66.4 52.3 %all-to-all-done = bf16[8,256,768]{2,1,0:T(8,128)(2,1)S(1)} async-done(((bf16[8,256,768]{2,1,0:T(8,128)(2,1)}), bf16[8,256,768]{2,1,0:T(8,128)(2,1)S(1)}, u32[]{:S(2)}, u32[]{:S(2)}) %all-to-all-start) | async-done | bytes 3145760 | tf_op jit(solution)/shard_map/all_to_all | solution.py:50
  118.6 2.7 %fusion.43 = f32[512,256]{0,1:T(8,128)S(1)} fusion(bf16[512,4224]{1,0:T(8,128)(2,1)} %all-gather.3.cloned.1.call-done, bf16[2048,768]{1,0:T(8,128)(2,1)S(1)} %bitcast.12), kind=kOutput, calls=%fused_computation.36 | convolution fusion | flops 536870912 | bytes 3670016 | tf_op jit(solution)/shard_map/dot_general | solution.py:28
  121.3 0.5 copy-done.3
  121.9 0.8 fusion.45
  122.7 0.8 convolution_convert_fusion
  123.4 0.9 fusion.34
  124.4 1.2 multiply_convert_fusion.7
  125.6 1.3 fusion.39
  126.9 1.3 add_convert_fusion
  128.2 2.5 %pad_maximum_fusion = bf16[512,4096]{1,0:T(8,128)(2,1)} fusion(bf16[512,2048]{1,0:T(8,128)(2,1)S(1)} %add_convert_fusion, bf16[512,2048]{1,0:T(8,128)(2,1)S(1)} %convolution_convert_fusion), kind=kLoop, calls=%fused_computation.8 | loop fusion | flops 8388608 | bytes 8388608 | tf_op jit(solution)/shard_map/concatenate | solution.py:74
  130.6 7.6 %all-to-all-start.1 = ((bf16[32,16,4096]{2,1,0:T(8,128)(2,1)}), bf16[32,16,4096]{2,1,0:T(8,128)(2,1)}, u32[]{:S(2)}, u32[]{:S(2)}) async-start(bf16[32,16,4096]{2,1,0:T(8,128)(2,1)} %bitcast.11), calls=%async_computation.1 | async-start | bytes 8388608 | tf_op jit(solution)/shard_map/all_to_all | solution.py:97
  138.3 53.3 %all-to-all-done.1 = bf16[32,16,4096]{2,1,0:T(8,128)(2,1)} async-done(((bf16[32,16,4096]{2,1,0:T(8,128)(2,1)}), bf16[32,16,4096]{2,1,0:T(8,128)(2,1)}, u32[]{:S(2)}, u32[]{:S(2)}) %all-to-all-start.1) | async-done | bytes 4194336 | tf_op jit(solution)/shard_map/all_to_all | solution.py:97
  191.6 2.8 %reduce.7 = bf16[16,4096]{1,0:T(8,128)(2,1)S(1)} reduce(bf16[32,16,4096]{2,1,0:T(8,128)(2,1)} %all-to-all-done.1, bf16[]{:T(256)} %constant.46.clone.1), dimensions={0}, to_apply=%region_1.0.clone | reduce | flops 2031616 | bytes 4325378 | tf_op jit(solution)/shard_map/reduce_sum | solution.py:98
  194.4 0.6 slice.88
  195.0 0.7 multiply_convert_fusion.14
  195.7 4.2 %fusion.10 = f32[1280,256]{1,0:T(8,128)S(1)} fusion(bf16[1280,4096]{1,0:T(8,128)(2,1)} %all-gather.5.cloned.1.call-done, bf16[2048,768]{1,0:T(8,128)(2,1)S(1)} %bitcast.19), kind=kOutput, calls=%fused_computation.14 | convolution fusion | flops 1342177280 | bytes 7602176 | tf_op jit(solution)/shard_map/dot_general | solution.py:27
  200.0 1.3 copy-done.4
  201.3 1.5 fusion.2
  202.8 1.6 fusion.12
  204.4 2.9 %fusion.26 = bf16[1,2048,256]{2,1,0:T(8,128)(2,1)} fusion(bf16[1280,4096]{1,0:T(8,128)(2,1)S(1)} %copy-done.4, f32[1280,256]{1,0:T(8,128)S(1)} %fusion.2, f32[1280,256]{1,0:T(8,128)S(1)} %fusion.10), kind=kOutput, calls=%fused_computation.23 | convolution fusion | flops 1344667648 | bytes 8912896 | tf_op jit(solution)/shard_map/dot_general | solution.py:15
  207.2 3.0 %fusion.29 = bf16[1,2048,256]{2,1,0:T(8,128)(2,1)} fusion(bf16[1280,4096]{1,0:T(8,128)(2,1)S(1)} %copy-done.4, f32[1280,256]{1,0:T(8,128)S(1)} %fusion.10, f32[1280,256]{1,0:T(8,128)S(1)} %fusion.2, f32[1280,256]{1,0:T(8,128)S(1)} %fusion.12), kind=kOutput, calls=%fused_computation.24 | convolution fusion | flops 1345978368 | bytes 10223616 | tf_op jit(solution)/shard_map/dot_general | solution.py:15
  210.2 2.9 %fusion.23 = bf16[1,2048,256]{2,1,0:T(8,128)(2,1)} fusion(bf16[1280,4096]{1,0:T(8,128)(2,1)S(1)} %copy-done.4, f32[1280,256]{1,0:T(8,128)S(1)} %fusion.12, f32[1280,256]{1,0:T(8,128)S(1)} %fusion.10), kind=kOutput, calls=%fused_computation.22 | convolution fusion | flops 1344667648 | bytes 8912896 | tf_op jit(solution)/shard_map/dot_general | solution.py:15
  (17 shorter events, 0.2 us)
Async XLA Ops:
  7.2 58.0 %all-gather.3.cloned.1.call-start = ((), (), s32[]{:S(2)}) async-start(), calls=%async_computation.3 | async-start | bytes 4460544 | tf_op jit(solution)/shard_map/all_gather | solution.py:60
  9.3 31.7 %copy-start = (bf16[256,256]{1,0:T(8,128)(2,1)S(1)}, bf16[256,256]{1,0:T(8,128)(2,1)}, u32[]{:S(2)}) copy-start(bf16[256,256]{1,0:T(8,128)(2,1)} %param.15) | copy-start | bytes 393220
  9.3 31.7 %copy-start.1 = (bf16[256,256]{1,0:T(8,128)(2,1)S(1)}, bf16[256,256]{1,0:T(8,128)(2,1)}, u32[]{:S(2)}) copy-start(bf16[256,256]{1,0:T(8,128)(2,1)} %param.14) | copy-start | bytes 393220
  9.3 31.7 %copy-start.2 = (bf16[256,256]{1,0:T(8,128)(2,1)S(1)}, bf16[256,256]{1,0:T(8,128)(2,1)}, u32[]{:S(2)}) copy-start(bf16[256,256]{1,0:T(8,128)(2,1)} %param.13) | copy-start | bytes 393220
  10.9 184.8 %all-gather.5.cloned.1.call-start = ((), (), s32[]{:S(2)}) async-start(), calls=%async_computation.4 | async-start | bytes 10813440 | tf_op jit(solution)/shard_map/all_gather | solution.py:94
  42.9 75.7 %all-to-all-start = ((bf16[8,256,768]{2,1,0:T(8,128)(2,1)}), bf16[8,256,768]{2,1,0:T(8,128)(2,1)S(1)}, u32[]{:S(2)}, u32[]{:S(2)}) async-start(bf16[8,256,768]{2,1,0:T(8,128)(2,1)} %broadcast_in_dim.12), calls=%async_computation | async-start | bytes 6291456 | tf_op jit(solution)/shard_map/all_to_all | solution.py:50
  118.6 3.2 %copy-start.3 = (bf16[512,4224]{1,0:T(8,128)(2,1)S(1)}, bf16[512,4224]{1,0:T(8,128)(2,1)}, u32[]{:S(2)}) copy-start(bf16[512,4224]{1,0:T(8,128)(2,1)} %all-gather.3.cloned.1.call-done) | copy-start | bytes 12976132
  130.6 60.9 %all-to-all-start.1 = ((bf16[32,16,4096]{2,1,0:T(8,128)(2,1)}), bf16[32,16,4096]{2,1,0:T(8,128)(2,1)}, u32[]{:S(2)}, u32[]{:S(2)}) async-start(bf16[32,16,4096]{2,1,0:T(8,128)(2,1)} %bitcast.11), calls=%async_computation.1 | async-start | bytes 8388608 | tf_op jit(solution)/shard_map/all_to_all | solution.py:97
  195.7 5.5 %copy-start.4 = (bf16[1280,4096]{1,0:T(8,128)(2,1)S(1)}, bf16[1280,4096]{1,0:T(8,128)(2,1)}, u32[]{:S(2)}) copy-start(bf16[1280,4096]{1,0:T(8,128)(2,1)} %all-gather.5.cloned.1.call-done) | copy-start | bytes 31457284
Sparse Core Ops, SparseCore 0:
  11.2 53.8 all-gather.2
  68.2 62.2 all-gather.4

commit v6 on v3

--- a/solution.py
+++ b/solution.py
@@ -45,13 +45,6 @@
     capacity = 5 * count_tok // (2 * experts)
     slots_here = experts * capacity
 
-    stacked = jnp.concatenate([dense_gate, dense_up, dense_down_t], axis=1)
-    full_cols = lax.all_gather(stacked, "expert", axis=0, tiled=True)
-    gate_cols = full_cols[:, :hid]
-    up_cols = full_cols[:, hid : 2 * hid]
-    down_cols = full_cols[:, 2 * hid :]
-    gate_up_cols = full_cols[:, : 2 * hid]
-
     flat_route = routes.reshape(-1)
     flat_scale = weight_codes.reshape(-1).astype(jnp.float32) / 256.0
     onehot = (flat_route[:, None] == jnp.arange(experts, dtype=jnp.int32)[None, :]).astype(
@@ -69,27 +62,27 @@
     send_x = jnp.dot(placed, flat_x, preferred_element_type=jnp.float32).astype(jnp.bfloat16)
     send_s = jnp.dot(placed, flat_scaled, preferred_element_type=jnp.float32).astype(jnp.bfloat16)
     send = jnp.concatenate([send_x, send_s], axis=1)
-    got = lax.all_to_all(send, "expert", split_axis=0, concat_axis=0, tiled=True)
 
-    code_rows = jnp.zeros((8, 2 * model_width), jnp.bfloat16)
-    code_rows = code_rows.at[0, : 2 * count_tok].set(weight_codes.reshape(-1).astype(jnp.bfloat16))
-    parcel = jnp.concatenate(
-        [got, jnp.concatenate([tokens, cotangent], axis=1), code_rows], axis=0
-    )
-    per_dev = parcel.shape[0]
-    full_cols, parcel = lax.optimization_barrier((full_cols, parcel))
+    lane = 1024
+    stacked = jnp.concatenate([dense_gate, dense_up, dense_down_t], axis=1)
+    w_rows = stacked.size // lane
+    copies = jnp.broadcast_to(stacked.reshape(1, w_rows, lane), (experts, w_rows, lane))
+    routed = send.reshape(experts, -1, lane)
+    parcel = jnp.concatenate([copies, routed], axis=1)
+    parcel = lax.all_to_all(parcel, "expert", split_axis=0, concat_axis=0, tiled=True)
+    full_cols = parcel[:, :w_rows].reshape(-1, stacked.shape[1])
+    got = parcel[:, w_rows:].reshape(slots_here, 2 * model_width)
     gate_cols = full_cols[:, :hid]
     up_cols = full_cols[:, hid : 2 * hid]
     down_cols = full_cols[:, 2 * hid :]
     gate_up_cols = full_cols[:, : 2 * hid]
-    gathered = lax.all_gather(parcel, ("tensor", "dp"), axis=0, tiled=True)
-    gathered = gathered.reshape(-1, per_dev, 2 * model_width)
-    rows = gathered[:, :slots_here].reshape(-1, 2 * model_width)
-    plane = gathered[:, slots_here : slots_here + count_tok].reshape(-1, 2 * model_width)
-    plane_codes = gathered[:, slots_here + count_tok, : 2 * count_tok].reshape(-1, 2)
+    code_cols = jnp.zeros((count_tok, 128), jnp.bfloat16)
+    code_cols = code_cols.at[:, 0:2].set(weight_codes.astype(jnp.bfloat16))
+    home = jnp.concatenate([tokens, cotangent, code_cols], axis=1)
+    plane = lax.all_gather(home, GROUP, axis=0, tiled=True)
     plane_x = plane[:, :model_width]
-    plane_dy = plane[:, model_width:].astype(jnp.float32)
-    plane_scale = plane_codes.astype(jnp.float32) / 256.0
+    plane_dy = plane[:, model_width : 2 * model_width].astype(jnp.float32)
+    plane_scale = plane[:, 2 * model_width : 2 * model_width + 2].astype(jnp.float32) / 256.0
 
     up_pre, activation, act_slope, hidden = forward_parts(plane_x, gate_cols, up_cols)
     out_term = contract_cols(hidden, down_cols).astype(jnp.bfloat16)
@@ -101,14 +94,11 @@
             jnp.concatenate([gate_grad, up_grad], axis=1), gate_up_cols
         )
     terms = jnp.concatenate([out_term, grad_term.astype(jnp.bfloat16)], axis=1)
-    part = lax.psum_scatter(terms, "tensor", scatter_dimension=0, tiled=True)
-    summed = lax.psum_scatter(part, "dp", scatter_dimension=0, tiled=True)
-    expert_out = summed[:, :model_width].astype(jnp.float32)
-    code_scale = weight_codes.astype(jnp.float32) / 256.0
-    mixed = (code_scale[:, 0:1] * expert_out + code_scale[:, 1:2] * expert_out).astype(
-        jnp.bfloat16
-    )
-    input_grad = summed[:, model_width:]
+
+    rows = lax.all_gather(got, GROUP, axis=0, tiled=True)
+    n_group = terms.shape[0] // count_tok
+    pieces = terms.reshape(n_group, count_tok, 2 * model_width)
+    pieces = lax.all_to_all(pieces, GROUP, split_axis=0, concat_axis=0, tiled=True)
     rows_x = rows[:, :model_width]
     rows_s = rows[:, model_width:]
     r_up, r_act, r_slope, r_hidden = forward_parts(rows_x, gate_cols, up_cols)
@@ -116,6 +106,16 @@
     grad_gate = contract_rows(rows_x, r_gate).astype(jnp.bfloat16)[None]
     grad_up = contract_rows(rows_x, r_upg).astype(jnp.bfloat16)[None]
     grad_down_t = contract_rows(rows_s, r_hidden).astype(jnp.bfloat16)[None]
+    pieces, grad_gate, grad_up, grad_down_t = lax.optimization_barrier(
+        (pieces, grad_gate, grad_up, grad_down_t)
+    )
+    summed = jnp.sum(pieces.astype(jnp.float32), axis=0)
+    expert_out = summed[:, :model_width].astype(jnp.bfloat16).astype(jnp.float32)
+    code_scale = weight_codes.astype(jnp.float32) / 256.0
+    mixed = (code_scale[:, 0:1] * expert_out + code_scale[:, 1:2] * expert_out).astype(
+        jnp.bfloat16
+    )
+    input_grad = summed[:, model_width:].astype(jnp.bfloat16)
     return (mixed, input_grad, grad_gate, grad_up, grad_down_t)
 
 

time: 335 us -> 239 us (0.71)
  waiting for transfers between devices: 248 us -> 71.6 us
  blocking collectives: 0 us -> 89 us
  local copies, waits for them, and re-layouts: 24.6 us -> 16.2 us
  matrix products: 31.4 us -> 24.5 us
  other arithmetic: 7.78 us -> 12.3 us
    reduce_scatter x2 -> x0, waiting for transfers between devices: 96.9 us -> none  [the longest x1 69.4 us: shards(): summed = lax.psum_scatter(part, 'dp', scatter_dimension=0, tiled=True)]
    all_to_all x0 -> x1, blocking collectives: none -> 89 us  [shards(): lax.all_to_all(parcel, 'expert', split_axis=0, concat_axis=0, tiled=True)]
    all_gather x2, waiting for transfers between devices: 129 us -> 71.6 us  [the longest x1 71.5 us: shards(): rows = lax.all_gather(got, GROUP, axis=0, tiled=True)]
    all_to_all x1, waiting for transfers between devices: 21.4 us -> 0.01 us  [shards(): lax.all_to_all(pieces, GROUP, split_axis=0, concat_axis=0, tiled=True)]
    slice x4 -> x3, local copies, waits for them, and re-layouts: 14.6 us -> 3.45 us  [the longest x1 2.04 us: shards(): full_cols = parcel[:, :w_rows].reshape(-1, stacked.shape[1])]
    reshape x0 -> x3, local copies, waits for them, and re-layouts: none -> 7.2 us  [the longest x1 4.89 us: shards(): full_cols = parcel[:, :w_rows].reshape(-1, stacked.shape[1])]
    unnamed x33 -> x12, local copies, waits for them, and re-layouts: 5.93 us -> 2.23 us
  transfers between devices with their start and end apart: 5 -> 3, of which waited for: 5 -> 1; matrix products, arithmetic and copies ran while one was open for 11% -> 19% of each run, Pallas kernels for 0% -> 0%
where the time goes in v6:
time: 239 us; the launch traced here: 236 us
  blocking collectives  89 us (37%)
  waiting for transfers between devices  71.6 us (30%)
  matrix products  24.5 us (10%)
  local copies, waits for them, and re-layouts  16.2 us (7%)
  between operations  14.3 us (6%)
  other arithmetic  12.3 us (5%)
  starting transfers between devices  7.7 us (3%)
    all_to_all x1, blocking collectives, shards(): lax.all_to_all(parcel, 'expert', split_axis=0, concat_axis=0, tiled=True)  89 us
    all_gather x1, waiting for transfers between devices, shards(): rows = lax.all_gather(got, GROUP, axis=0, tiled=True)  71.5 us
    dot_general x3, matrix products, contract_rows(): lax.dot_general(left_side, right_side, (((0,), (0,)), ((), ())), preferre...  8.31 us
    all_to_all x1, starting transfers between devices, shards(): lax.all_to_all(pieces, GROUP, split_axis=0, concat_axis=0, tiled=True)  7.62 us
    dot_general x2, matrix products, forward_parts(): gate_pre = jnp.dot(rows_x, gate_cols, preferred_element_type=jnp.float32)  4.91 us
    reshape x1, local copies, waits for them, and re-layouts, shards(): full_cols = parcel[:, :w_rows].reshape(-1, stacked.shape[1])  4.89 us
  transfers between devices with their start and end apart: 3, of which 1 were waited for; matrix products, arithmetic and copies ran while one was open for 19% of the time, Pallas kernels for 0%

profile of v6, /device:TPU:32, one launch (start us, length us, event | category | flops | bytes accessed | tf_op | source)
XLA Modules:
  0.0 235.6 jit_solution(2537076619078845735)
XLA Ops:
  7.2 0.6 compare_reduce_fusion
  7.9 1.3 broadcast_select_fusion
  9.2 0.1 copy.18
  9.3 1.5 fusion.67
  10.9 0.8 copy.16
  11.7 0.1 reshape.77
  11.8 0.7 convert_multiply_fusion.3
  12.5 0.1 copy.17
  12.5 0.1 div.24
  12.6 0.9 broadcast_in_dim.30
  13.6 0.2 convert_element_type.99
  13.8 0.9 broadcast_in_dim.29
  14.7 0.1 fusion.69
  14.8 0.1 reduce_window_sum.11
  14.9 0.2 select_reduce_fusion
  15.1 0.2 convolution_convert_fusion.2
  15.3 0.2 convolution_convert_fusion.1
  15.5 0.3 reshape.79
  15.9 0.3 broadcast_in_dim.27
  16.2 0.4 broadcast_in_dim.28
  16.6 0.6 pad_maximum_fusion.1
  17.2 89.0 %all_to_all.10 = bf16[8,212,1024]{2,1,0:T(8,128)(2,1)S(1)} all-to-all(bf16[8,212,1024]{2,1,0:T(8,128)(2,1)S(1)} %pad_maximum_fusion.1), channel_id=1, replica_groups=mesh['dp'=8,'expert'=8,'tensor'=4] {'expert'}, dimensions={0} | all-to-all | bytes 6946816 | tf_op jit(solution)/shard_map/all_to_all | solution.py:72
  106.3 0.8 slice.96
  107.0 2.0 reshape.82
  109.1 2.0 slice.87
  111.1 4.9 %reshape.80 = bf16[2048,768]{1,0:T(8,128)(2,1)S(1)} reshape(bf16[8,192,1024]{2,1,0:T(8,128)(2,1)} %slice.87) | data formatting | bytes 6291456 | tf_op jit(solution)/shard_map/reshape | solution.py:73
  116.1 1.1 convert_multiply_fusion.2
  117.1 0.3 slice_reduce_fusion
  117.4 2.4 %fusion.43 = f32[512,256]{0,1:T(8,128)S(1)} fusion(bf16[512,4224]{1,0:T(8,128)(2,1)} %all-gather.3.cloned.1.call-done, bf16[2048,768]{1,0:T(8,128)(2,1)S(1)} %reshape.80), kind=kOutput, calls=%fused_computation.37 | convolution fusion | flops 536870912 | bytes 3670016 | tf_op jit(solution)/shard_map/dot_general | solution.py:28
  119.9 0.8 fusion.45
  120.6 0.8 convolution_convert_fusion
  121.4 0.9 fusion.34
  122.3 1.1 multiply_convert_fusion.7
  123.4 1.3 fusion.39
  124.7 1.3 add_convert_fusion
  126.0 2.5 %pad_maximum_fusion = bf16[512,4096]{1,0:T(8,128)(2,1)} fusion(bf16[512,2048]{1,0:T(8,128)(2,1)S(1)} %add_convert_fusion, bf16[512,2048]{1,0:T(8,128)(2,1)S(1)} %convolution_convert_fusion), kind=kLoop, calls=%fused_computation.8 | loop fusion | flops 8388608 | bytes 8388608 | tf_op jit(solution)/shard_map/concatenate | solution.py:96
  128.5 7.6 %all-to-all-start.1 = ((bf16[32,16,4096]{2,1,0:T(8,128)(2,1)}), bf16[32,16,4096]{2,1,0:T(8,128)(2,1)}, u32[]{:S(2)}, u32[]{:S(2)}) async-start(bf16[32,16,4096]{2,1,0:T(8,128)(2,1)} %bitcast.10), calls=%async_computation.1 | async-start | bytes 8388608 | tf_op jit(solution)/shard_map/all_to_all | solution.py:101
  136.1 71.5 %all-gather.5.cloned.1.call-done = bf16[1280,4096]{1,0:T(8,128)(2,1)} async-done(((bf16[40,4096]{1,0:T(8,128)(2,1)}), bf16[1280,4096]{1,0:T(8,128)(2,1)}) %all-gather.5.cloned.1.call-update) | async-done | bytes 10485776 | tf_op jit(solution)/shard_map/all_gather | solution.py:98
  207.6 4.2 %fusion.10 = f32[1280,256]{1,0:T(8,128)S(1)} fusion(bf16[1280,4096]{1,0:T(8,128)(2,1)} %all-gather.5.cloned.1.call-done, bf16[2048,768]{1,0:T(8,128)(2,1)S(1)} %reshape.80), kind=kOutput, calls=%fused_computation.15 | convolution fusion | flops 1342177280 | bytes 7602176 | tf_op jit(solution)/shard_map/dot_general | solution.py:27
  211.8 1.4 copy-done.4
  213.2 1.5 fusion.12
  214.7 1.5 fusion.2
  216.2 2.7 %fusion.23 = bf16[1,2048,256]{2,1,0:T(8,128)(2,1)} fusion(bf16[1280,4096]{1,0:T(8,128)(2,1)S(1)} %copy-done.4, f32[1280,256]{1,0:T(8,128)S(1)} %fusion.12, f32[1280,256]{1,0:T(8,128)S(1)} %fusion.10), kind=kOutput, calls=%fused_computation.23 | convolution fusion | flops 1344667648 | bytes 8912896 | tf_op jit(solution)/shard_map/dot_general | solution.py:15
  219.0 2.7 %fusion.26 = bf16[1,2048,256]{2,1,0:T(8,128)(2,1)} fusion(bf16[1280,4096]{1,0:T(8,128)(2,1)S(1)} %copy-done.4, f32[1280,256]{1,0:T(8,128)S(1)} %fusion.2, f32[1280,256]{1,0:T(8,128)S(1)} %fusion.10), kind=kOutput, calls=%fused_computation.24 | convolution fusion | flops 1344667648 | bytes 8912896 | tf_op jit(solution)/shard_map/dot_general | solution.py:15
  221.7 2.8 %fusion.29 = bf16[1,2048,256]{2,1,0:T(8,128)(2,1)} fusion(bf16[1280,4096]{1,0:T(8,128)(2,1)S(1)} %copy-done.4, f32[1280,256]{1,0:T(8,128)S(1)} %fusion.10, f32[1280,256]{1,0:T(8,128)S(1)} %fusion.2, f32[1280,256]{1,0:T(8,128)S(1)} %fusion.12), kind=kOutput, calls=%fused_computation.25 | convolution fusion | flops 1345978368 | bytes 10223616 | tf_op jit(solution)/shard_map/dot_general | solution.py:15
  224.6 2.8 %reduce.7 = bf16[16,4096]{1,0:T(8,128)(2,1)S(1)} reduce(bf16[32,16,4096]{2,1,0:T(8,128)(2,1)} %all-to-all-done.1, bf16[]{:T(256)} %constant.46.clone.1), dimensions={0}, to_apply=%region_3.4.clone | reduce | flops 2031616 | bytes 4325378 | tf_op jit(solution)/shard_map/reduce_sum | solution.py:112
  227.4 0.6 slice.100
  228.0 0.7 multiply_convert_fusion.14
  (20 shorter events, 0.3 us)
Async XLA Ops:
  7.2 8.7 %copy-start.2 = (bf16[256,256]{1,0:T(8,128)(2,1)S(1)}, bf16[256,256]{1,0:T(8,128)(2,1)}, u32[]{:S(2)}) copy-start(bf16[256,256]{1,0:T(8,128)(2,1)} %param.13) | copy-start | bytes 393220
  7.2 8.7 %copy-start.1 = (bf16[256,256]{1,0:T(8,128)(2,1)S(1)}, bf16[256,256]{1,0:T(8,128)(2,1)}, u32[]{:S(2)}) copy-start(bf16[256,256]{1,0:T(8,128)(2,1)} %param.14) | copy-start | bytes 393220
  7.2 8.7 %copy-start = (bf16[256,256]{1,0:T(8,128)(2,1)S(1)}, bf16[256,256]{1,0:T(8,128)(2,1)}, u32[]{:S(2)}) copy-start(bf16[256,256]{1,0:T(8,128)(2,1)} %param.15) | copy-start | bytes 393220
  7.2 108.8 %all-gather.3.cloned.1.call-start = ((), (), s32[]{:S(2)}) async-start(), calls=%async_computation.2 | async-start | bytes 4460544 | tf_op jit(solution)/shard_map/all_gather | solution.py:82
  10.9 196.8 %all-gather.5.cloned.1.call-start = ((), (), s32[]{:S(2)}) async-start(), calls=%async_computation.3 | async-start | bytes 10813440 | tf_op jit(solution)/shard_map/all_gather | solution.py:98
  116.0 3.8 %copy-start.3 = (bf16[512,4224]{1,0:T(8,128)(2,1)S(1)}, bf16[512,4224]{1,0:T(8,128)(2,1)}, u32[]{:S(2)}) copy-start(bf16[512,4224]{1,0:T(8,128)(2,1)} %all-gather.3.cloned.1.call-done) | copy-start | bytes 12976132
  128.5 96.1 %all-to-all-start.1 = ((bf16[32,16,4096]{2,1,0:T(8,128)(2,1)}), bf16[32,16,4096]{2,1,0:T(8,128)(2,1)}, u32[]{:S(2)}, u32[]{:S(2)}) async-start(bf16[32,16,4096]{2,1,0:T(8,128)(2,1)} %bitcast.10), calls=%async_computation.1 | async-start | bytes 8388608 | tf_op jit(solution)/shard_map/all_to_all | solution.py:101
  207.6 5.5 %copy-start.4 = (bf16[1280,4096]{1,0:T(8,128)(2,1)S(1)}, bf16[1280,4096]{1,0:T(8,128)(2,1)}, u32[]{:S(2)}) copy-start(bf16[1280,4096]{1,0:T(8,128)(2,1)} %all-gather.5.cloned.1.call-done) | copy-start | bytes 31457284
Sparse Core Ops, SparseCore 0:
  11.2 53.9 all-gather.2
  109.2 98.3 all-gather.4

commit v7 on v5

--- a/solution.py
+++ b/solution.py
@@ -95,6 +95,16 @@
     n_group = terms.shape[0] // count_tok
     pieces = terms.reshape(n_group, count_tok, 2 * model_width)
     pieces = lax.all_to_all(pieces, GROUP, split_axis=0, concat_axis=0, tiled=True)
+    rows_x = rows[:, :model_width]
+    rows_s = rows[:, model_width:]
+    r_up, r_act, r_slope, r_hidden = forward_parts(rows_x, gate_cols, up_cols)
+    r_gate, r_upg = grad_parts(rows_s, down_cols, r_up, r_act, r_slope)
+    grad_gate = contract_rows(rows_x, r_gate).astype(jnp.bfloat16)[None]
+    grad_up = contract_rows(rows_x, r_upg).astype(jnp.bfloat16)[None]
+    grad_down_t = contract_rows(rows_s, r_hidden).astype(jnp.bfloat16)[None]
+    pieces, grad_gate, grad_up, grad_down_t = lax.optimization_barrier(
+        (pieces, grad_gate, grad_up, grad_down_t)
+    )
     summed = jnp.sum(pieces.astype(jnp.float32), axis=0)
     expert_out = summed[:, :model_width].astype(jnp.bfloat16).astype(jnp.float32)
     code_scale = weight_codes.astype(jnp.float32) / 256.0
@@ -102,13 +112,6 @@
         jnp.bfloat16
     )
     input_grad = summed[:, model_width:].astype(jnp.bfloat16)
-    rows_x = rows[:, :model_width]
-    rows_s = rows[:, model_width:]
-    r_up, r_act, r_slope, r_hidden = forward_parts(rows_x, gate_cols, up_cols)
-    r_gate, r_upg = grad_parts(rows_s, down_cols, r_up, r_act, r_slope)
-    grad_gate = contract_rows(rows_x, r_gate).astype(jnp.bfloat16)[None]
-    grad_up = contract_rows(rows_x, r_upg).astype(jnp.bfloat16)[None]
-    grad_down_t = contract_rows(rows_s, r_hidden).astype(jnp.bfloat16)[None]
     return (mixed, input_grad, grad_gate, grad_up, grad_down_t)
 
 

time: 220 us -> 203 us (0.923)
  waiting for transfers between devices: 123 us -> 106 us
    all_to_all x1, waiting for transfers between devices: 53.3 us -> 36.3 us  [shards(): lax.all_to_all(pieces, GROUP, split_axis=0, concat_axis=0, tiled=True)]
  transfers between devices with their start and end apart: 4 -> 4, of which waited for: 3 -> 3; matrix products, arithmetic and copies ran while one was open for 11% -> 17% of each run, Pallas kernels for 0% -> 0%
where the time goes in v7:
time: 203 us
  waiting for transfers between devices  106 us (52%)
  matrix products  24.9 us (12%)
  blocking collectives  24.4 us (12%)
  between operations  14.2 us (7%)
  starting transfers between devices  12.7 us (6%)
  other arithmetic  11.6 us (6%)
  local copies, waits for them, and re-layouts  8.88 us (4%)
    all_to_all x1, waiting for transfers between devices, shards(): lax.all_to_all(copies, 'expert', split_axis=0, concat_axis=0, tiled=True)  52.3 us
    all_to_all x1, waiting for transfers between devices, shards(): lax.all_to_all(pieces, GROUP, split_axis=0, concat_axis=0, tiled=True)  36.3 us
    all_to_all x1, blocking collectives, shards(): lax.all_to_all(send, 'expert', split_axis=0, concat_axis=0, tiled=True)  24.4 us
    all_gather x1, waiting for transfers between devices, shards(): plane = lax.all_gather(home, GROUP, axis=0, tiled=True)  17.2 us
    dot_general x3, matrix products, contract_rows(): lax.dot_general(left_side, right_side, (((0,), (0,)), ((), ())), preferre...  8.31 us
    all_to_all x1, starting transfers between devices, shards(): lax.all_to_all(pieces, GROUP, split_axis=0, concat_axis=0, tiled=True)  7.62 us
    all_to_all x1, starting transfers between devices, shards(): lax.all_to_all(copies, 'expert', split_axis=0, concat_axis=0, tiled=True)  5.01 us
    dot_general x2, matrix products, forward_parts(): gate_pre = jnp.dot(rows_x, gate_cols, preferred_element_type=jnp.float32)  4.92 us
  transfers between devices with their start and end apart: 4, of which 3 were waited for; matrix products, arithmetic and copies ran while one was open for 17% of the time, Pallas kernels for 0%

profile of v7, /device:TPU:32, one launch (start us, length us, event | category | flops | bytes accessed | tf_op | source)
XLA Modules:
  0.0 202.5 jit_solution(9798106059664174780)
XLA Ops:
  7.2 0.6 compare_reduce_fusion
  7.9 1.3 broadcast_select_fusion
  9.2 0.1 copy.18
  9.3 1.6 fusion.67
  10.9 0.9 broadcast_in_dim.28
  11.9 0.2 convert_element_type.110
  12.1 0.7 convert_multiply_fusion.3
  12.8 0.1 copy.17
  12.9 0.1 div.27
  12.9 0.8 copy.16
  13.7 0.1 reshape.74
  13.8 0.9 broadcast_in_dim.13
  14.7 0.1 reshape.75
  14.8 0.1 fusion.69
  14.8 0.1 reduce_window_sum.11
  14.9 0.2 select_reduce_fusion
  15.1 0.2 convolution_convert_fusion.2
  15.3 0.2 convolution_convert_fusion.1
  15.6 0.1 all_to_all.16
  15.7 24.4 %all_to_all.22 = bf16[8,5,4096]{2,1,0:T(8,128)(2,1)S(1)} all-to-all(bf16[8,5,4096]{2,1,0:T(8,128)(2,1)S(1)} %all_to_all.16), channel_id=1, replica_groups=mesh['dp'=8,'expert'=8,'tensor'=4] {'expert'}, dimensions={0} | all-to-all | bytes 655360 | tf_op jit(solution)/shard_map/all_to_all | solution.py:93
  40.1 0.9 all_to_all.18
  41.1 1.8 broadcast_in_dim.12
  42.9 5.0 %all-to-all-start = ((bf16[8,256,768]{2,1,0:T(8,128)(2,1)}), bf16[8,256,768]{2,1,0:T(8,128)(2,1)S(1)}, u32[]{:S(2)}, u32[]{:S(2)}) async-start(bf16[8,256,768]{2,1,0:T(8,128)(2,1)} %broadcast_in_dim.12), calls=%async_computation | async-start | bytes 6291456 | tf_op jit(solution)/shard_map/all_to_all | solution.py:50
  47.9 17.2 %all-gather.3.cloned.1.call-done = bf16[512,4224]{1,0:T(8,128)(2,1)} async-done(((bf16[16,4224]{1,0:T(8,128)(2,1)}), bf16[512,4224]{1,0:T(8,128)(2,1)}) %all-gather.3.cloned.1.call-update) | async-done | bytes 4325392 | tf_op jit(solution)/shard_map/all_gather | solution.py:60
  65.1 0.9 convert_multiply_fusion.2
  66.1 0.3 slice_reduce_fusion
  66.4 52.3 %all-to-all-done = bf16[8,256,768]{2,1,0:T(8,128)(2,1)S(1)} async-done(((bf16[8,256,768]{2,1,0:T(8,128)(2,1)}), bf16[8,256,768]{2,1,0:T(8,128)(2,1)S(1)}, u32[]{:S(2)}, u32[]{:S(2)}) %all-to-all-start) | async-done | bytes 3145760 | tf_op jit(solution)/shard_map/all_to_all | solution.py:50
  118.6 2.7 %fusion.43 = f32[512,256]{0,1:T(8,128)S(1)} fusion(bf16[512,4224]{1,0:T(8,128)(2,1)} %all-gather.3.cloned.1.call-done, bf16[2048,768]{1,0:T(8,128)(2,1)S(1)} %bitcast.12), kind=kOutput, calls=%fused_computation.36 | convolution fusion | flops 536870912 | bytes 3670016 | tf_op jit(solution)/shard_map/dot_general | solution.py:28
  121.4 0.5 copy-done.3
  121.9 0.7 fusion.45
  122.6 0.8 convolution_convert_fusion
  123.4 0.9 fusion.34
  124.4 1.1 multiply_convert_fusion.7
  125.5 1.3 fusion.39
  126.8 1.3 add_convert_fusion
  128.1 2.5 %pad_maximum_fusion = bf16[512,4096]{1,0:T(8,128)(2,1)} fusion(bf16[512,2048]{1,0:T(8,128)(2,1)S(1)} %add_convert_fusion, bf16[512,2048]{1,0:T(8,128)(2,1)S(1)} %convolution_convert_fusion), kind=kLoop, calls=%fused_computation.8 | loop fusion | flops 8388608 | bytes 8388608 | tf_op jit(solution)/shard_map/concatenate | solution.py:74
  130.6 7.6 %all-to-all-start.1 = ((bf16[32,16,4096]{2,1,0:T(8,128)(2,1)}), bf16[32,16,4096]{2,1,0:T(8,128)(2,1)}, u32[]{:S(2)}, u32[]{:S(2)}) async-start(bf16[32,16,4096]{2,1,0:T(8,128)(2,1)} %bitcast.11), calls=%async_computation.1 | async-start | bytes 8388608 | tf_op jit(solution)/shard_map/all_to_all | solution.py:97
  138.3 4.2 %fusion.10 = f32[1280,256]{1,0:T(8,128)S(1)} fusion(bf16[1280,4096]{1,0:T(8,128)(2,1)} %all-gather.5.cloned.1.call-done, bf16[2048,768]{1,0:T(8,128)(2,1)S(1)} %bitcast.19), kind=kOutput, calls=%fused_computation.14 | convolution fusion | flops 1342177280 | bytes 7602176 | tf_op jit(solution)/shard_map/dot_general | solution.py:27
  142.4 1.3 copy-done.4
  143.8 1.5 fusion.2
  145.3 1.5 fusion.12
  146.9 2.7 %fusion.26 = bf16[1,2048,256]{2,1,0:T(8,128)(2,1)} fusion(bf16[1280,4096]{1,0:T(8,128)(2,1)S(1)} %copy-done.4, f32[1280,256]{1,0:T(8,128)S(1)} %fusion.2, f32[1280,256]{1,0:T(8,128)S(1)} %fusion.10), kind=kOutput, calls=%fused_computation.23 | convolution fusion | flops 1344667648 | bytes 8912896 | tf_op jit(solution)/shard_map/dot_general | solution.py:15
  149.6 2.7 %fusion.23 = bf16[1,2048,256]{2,1,0:T(8,128)(2,1)} fusion(bf16[1280,4096]{1,0:T(8,128)(2,1)S(1)} %copy-done.4, f32[1280,256]{1,0:T(8,128)S(1)} %fusion.12, f32[1280,256]{1,0:T(8,128)S(1)} %fusion.10), kind=kOutput, calls=%fused_computation.22 | convolution fusion | flops 1344667648 | bytes 8912896 | tf_op jit(solution)/shard_map/dot_general | solution.py:15
  152.3 2.8 %fusion.29 = bf16[1,2048,256]{2,1,0:T(8,128)(2,1)} fusion(bf16[1280,4096]{1,0:T(8,128)(2,1)S(1)} %copy-done.4, f32[1280,256]{1,0:T(8,128)S(1)} %fusion.10, f32[1280,256]{1,0:T(8,128)S(1)} %fusion.2, f32[1280,256]{1,0:T(8,128)S(1)} %fusion.12), kind=kOutput, calls=%fused_computation.24 | convolution fusion | flops 1345978368 | bytes 10223616 | tf_op jit(solution)/shard_map/dot_general | solution.py:15
  155.2 36.3 %all-to-all-done.1 = bf16[32,16,4096]{2,1,0:T(8,128)(2,1)} async-done(((bf16[32,16,4096]{2,1,0:T(8,128)(2,1)}), bf16[32,16,4096]{2,1,0:T(8,128)(2,1)}, u32[]{:S(2)}, u32[]{:S(2)}) %all-to-all-start.1) | async-done | bytes 4194336 | tf_op jit(solution)/shard_map/all_to_all | solution.py:97
  191.5 2.8 %reduce.7 = bf16[16,4096]{1,0:T(8,128)(2,1)S(1)} reduce(bf16[32,16,4096]{2,1,0:T(8,128)(2,1)} %all-to-all-done.1, bf16[]{:T(256)} %constant.46.clone.1), dimensions={0}, to_apply=%region_3.4.clone | reduce | flops 2031616 | bytes 4325378 | tf_op jit(solution)/shard_map/reduce_sum | solution.py:108
  194.4 0.6 slice.90
  195.0 0.7 multiply_convert_fusion.14
  (17 shorter events, 0.2 us)
Async XLA Ops:
  7.2 58.0 %all-gather.3.cloned.1.call-start = ((), (), s32[]{:S(2)}) async-start(), calls=%async_computation.3 | async-start | bytes 4460544 | tf_op jit(solution)/shard_map/all_gather | solution.py:60
  9.3 31.7 %copy-start = (bf16[256,256]{1,0:T(8,128)(2,1)S(1)}, bf16[256,256]{1,0:T(8,128)(2,1)}, u32[]{:S(2)}) copy-start(bf16[256,256]{1,0:T(8,128)(2,1)} %param.15) | copy-start | bytes 393220
  9.3 31.7 %copy-start.1 = (bf16[256,256]{1,0:T(8,128)(2,1)S(1)}, bf16[256,256]{1,0:T(8,128)(2,1)}, u32[]{:S(2)}) copy-start(bf16[256,256]{1,0:T(8,128)(2,1)} %param.14) | copy-start | bytes 393220
  9.3 31.7 %copy-start.2 = (bf16[256,256]{1,0:T(8,128)(2,1)S(1)}, bf16[256,256]{1,0:T(8,128)(2,1)}, u32[]{:S(2)}) copy-start(bf16[256,256]{1,0:T(8,128)(2,1)} %param.13) | copy-start | bytes 393220
  10.9 127.3 %all-gather.5.cloned.1.call-start = ((), (), s32[]{:S(2)}) async-start(), calls=%async_computation.4 | async-start | bytes 10813440 | tf_op jit(solution)/shard_map/all_gather | solution.py:94
  42.9 75.7 %all-to-all-start = ((bf16[8,256,768]{2,1,0:T(8,128)(2,1)}), bf16[8,256,768]{2,1,0:T(8,128)(2,1)S(1)}, u32[]{:S(2)}, u32[]{:S(2)}) async-start(bf16[8,256,768]{2,1,0:T(8,128)(2,1)} %broadcast_in_dim.12), calls=%async_computation | async-start | bytes 6291456 | tf_op jit(solution)/shard_map/all_to_all | solution.py:50
  118.6 3.2 %copy-start.3 = (bf16[512,4224]{1,0:T(8,128)(2,1)S(1)}, bf16[512,4224]{1,0:T(8,128)(2,1)}, u32[]{:S(2)}) copy-start(bf16[512,4224]{1,0:T(8,128)(2,1)} %all-gather.3.cloned.1.call-done) | copy-start | bytes 12976132
  130.6 60.9 %all-to-all-start.1 = ((bf16[32,16,4096]{2,1,0:T(8,128)(2,1)}), bf16[32,16,4096]{2,1,0:T(8,128)(2,1)}, u32[]{:S(2)}, u32[]{:S(2)}) async-start(bf16[32,16,4096]{2,1,0:T(8,128)(2,1)} %bitcast.11), calls=%async_computation.1 | async-start | bytes 8388608 | tf_op jit(solution)/shard_map/all_to_all | solution.py:97
  138.2 5.5 %copy-start.4 = (bf16[1280,4096]{1,0:T(8,128)(2,1)S(1)}, bf16[1280,4096]{1,0:T(8,128)(2,1)}, u32[]{:S(2)}) copy-start(bf16[1280,4096]{1,0:T(8,128)(2,1)} %all-gather.5.cloned.1.call-done) | copy-start | bytes 31457284
Sparse Core Ops, SparseCore 0:
  11.2 53.8 all-gather.2
  68.2 62.2 all-gather.4

commit v8 on v7

--- a/solution.py
+++ b/solution.py
@@ -92,9 +92,12 @@
     send = jnp.concatenate([send_x, send_s], axis=1)
     got = lax.all_to_all(send, "expert", split_axis=0, concat_axis=0, tiled=True)
     rows = lax.all_gather(got, GROUP, axis=0, tiled=True)
-    n_group = terms.shape[0] // count_tok
-    pieces = terms.reshape(n_group, count_tok, 2 * model_width)
-    pieces = lax.all_to_all(pieces, GROUP, split_axis=0, concat_axis=0, tiled=True)
+    n_dp = lax.axis_size("dp")
+    n_tensor = lax.axis_size("tensor")
+    pieces = terms.reshape(n_dp, n_tensor, count_tok, 2 * model_width)
+    pieces = lax.all_to_all(pieces, "tensor", split_axis=1, concat_axis=1, tiled=True)
+    pieces = jnp.sum(pieces.astype(jnp.float32), axis=1).astype(jnp.bfloat16)
+    pieces = lax.all_to_all(pieces, "dp", split_axis=0, concat_axis=0, tiled=True)
     rows_x = rows[:, :model_width]
     rows_s = rows[:, model_width:]
     r_up, r_act, r_slope, r_hidden = forward_parts(rows_x, gate_cols, up_cols)

time: 203 us -> 225 us (1.11)
  waiting for transfers between devices: 106 us -> 118 us
  starting transfers between devices: 12.7 us -> 16.9 us
  local copies, waits for them, and re-layouts: 8.88 us -> 11.3 us
    all_to_all x1 -> x2, waiting for transfers between devices: 36.3 us -> 48.2 us  [the longest x1 48.2 us: shards(): lax.all_to_all(pieces, 'tensor', split_axis=1, concat_axis=1, tiled=True)]
    reduce_sum x0 -> x1, other arithmetic: none -> 4.23 us  [shards(): pieces = jnp.sum(pieces.astype(jnp.float32), axis=1).astype(jnp.bfloat16)]
    all_to_all x1 -> x2, starting transfers between devices: 7.62 us -> 11.8 us  [the longest x1 6.92 us: shards(): lax.all_to_all(pieces, 'dp', split_axis=0, concat_axis=0, tiled=True)]
    reshape x0 -> x1, local copies, waits for them, and re-layouts: none -> 2.48 us  [shards(): pieces = terms.reshape(n_dp, n_tensor, count_tok, 2 * model_width)]
  transfers between devices with their start and end apart: 4 -> 5, of which waited for: 3 -> 3; matrix products, arithmetic and copies ran while one was open for 17% -> 18% of each run, Pallas kernels for 0% -> 0%
where the time goes in v8:
time: 225 us; the launch traced here: 222 us
  waiting for transfers between devices  118 us (52%)
  matrix products  25.4 us (11%)
  blocking collectives  24.4 us (11%)
  starting transfers between devices  16.9 us (8%)
  between operations  14.3 us (6%)
  other arithmetic  12.3 us (5%)
  local copies, waits for them, and re-layouts  11.3 us (5%)
    all_to_all x1, waiting for transfers between devices, shards(): lax.all_to_all(copies, 'expert', split_axis=0, concat_axis=0, tiled=True)  52.3 us
    all_to_all x1, waiting for transfers between devices, shards(): lax.all_to_all(pieces, 'tensor', split_axis=1, concat_axis=1, tiled=True)  48.2 us
    all_to_all x1, blocking collectives, shards(): lax.all_to_all(send, 'expert', split_axis=0, concat_axis=0, tiled=True)  24.4 us
    all_gather x1, waiting for transfers between devices, shards(): plane = lax.all_gather(home, GROUP, axis=0, tiled=True)  17.2 us
    dot_general x3, matrix products, contract_rows(): lax.dot_general(left_side, right_side, (((0,), (0,)), ((), ())), preferre...  8.68 us
    all_to_all x1, starting transfers between devices, shards(): lax.all_to_all(pieces, 'dp', split_axis=0, concat_axis=0, tiled=True)  6.92 us
    all_to_all x1, starting transfers between devices, shards(): lax.all_to_all(copies, 'expert', split_axis=0, concat_axis=0, tiled=True)  5.01 us
    dot_general x2, matrix products, forward_parts(): gate_pre = jnp.dot(rows_x, gate_cols, preferred_element_type=jnp.float32)  4.97 us
  transfers between devices with their start and end apart: 5, of which 3 were waited for; matrix products, arithmetic and copies ran while one was open for 18% of the time, Pallas kernels for 0%

profile of v8, /device:TPU:32, one launch (start us, length us, event | category | flops | bytes accessed | tf_op | source)
XLA Modules:
  0.0 222.3 jit_solution(7417964083327292620)
XLA Ops:
  7.2 0.6 compare_reduce_fusion
  7.9 1.3 broadcast_select_fusion
  9.2 0.1 copy.22
  9.3 1.6 fusion.67
  10.9 0.9 broadcast_in_dim.28
  11.9 0.2 convert_element_type.112
  12.1 0.7 convert_multiply_fusion.3
  12.8 0.1 copy.21
  12.9 0.1 div.27
  12.9 0.8 copy.20
  13.7 0.1 reshape.74
  13.8 0.9 broadcast_in_dim.13
  14.9 0.2 select_reduce_fusion
  15.1 0.2 convolution_convert_fusion.2
  15.3 0.2 convolution_convert_fusion.1
  15.6 0.1 all_to_all.20
  15.7 24.4 %all_to_all.27 = bf16[8,5,4096]{2,1,0:T(8,128)(2,1)S(1)} all-to-all(bf16[8,5,4096]{2,1,0:T(8,128)(2,1)S(1)} %all_to_all.20), channel_id=1, replica_groups=mesh['dp'=8,'expert'=8,'tensor'=4] {'expert'}, dimensions={0} | all-to-all | bytes 655360 | tf_op jit(solution)/shard_map/all_to_all | solution.py:93
  40.1 0.9 all_to_all.22
  41.1 1.8 broadcast_in_dim.12
  42.9 5.0 %all-to-all-start = ((bf16[8,256,768]{2,1,0:T(8,128)(2,1)}), bf16[8,256,768]{2,1,0:T(8,128)(2,1)S(1)}, u32[]{:S(2)}, u32[]{:S(2)}) async-start(bf16[8,256,768]{2,1,0:T(8,128)(2,1)} %broadcast_in_dim.12), calls=%async_computation | async-start | bytes 6291456 | tf_op jit(solution)/shard_map/all_to_all | solution.py:50
  47.9 17.2 %all-gather.3.cloned.1.call-done = bf16[512,4224]{1,0:T(8,128)(2,1)} async-done(((bf16[16,4224]{1,0:T(8,128)(2,1)}), bf16[512,4224]{1,0:T(8,128)(2,1)}) %all-gather.3.cloned.1.call-update) | async-done | bytes 4325392 | tf_op jit(solution)/shard_map/all_gather | solution.py:60
  65.1 0.9 convert_multiply_fusion.2
  66.1 0.3 slice_reduce_fusion
  66.4 52.3 %all-to-all-done = bf16[8,256,768]{2,1,0:T(8,128)(2,1)S(1)} async-done(((bf16[8,256,768]{2,1,0:T(8,128)(2,1)}), bf16[8,256,768]{2,1,0:T(8,128)(2,1)S(1)}, u32[]{:S(2)}, u32[]{:S(2)}) %all-to-all-start) | async-done | bytes 3145760 | tf_op jit(solution)/shard_map/all_to_all | solution.py:50
  118.6 2.7 %fusion.43 = f32[512,256]{0,1:T(8,128)S(1)} fusion(bf16[512,4224]{1,0:T(8,128)(2,1)} %all-gather.3.cloned.1.call-done, bf16[2048,768]{1,0:T(8,128)(2,1)S(1)} %bitcast.12), kind=kOutput, calls=%fused_computation.36 | convolution fusion | flops 536870912 | bytes 3670016 | tf_op jit(solution)/shard_map/dot_general | solution.py:28
  121.3 0.5 copy-done.3
  121.9 0.8 fusion.45
  122.7 0.8 convolution_convert_fusion
  123.4 0.9 fusion.34
  124.4 1.2 multiply_convert_fusion.7
  125.6 1.3 fusion.39
  126.9 1.3 add_convert_fusion
  128.2 0.5 pad_maximum_fusion
  128.7 2.5 %copy.19 = bf16[8,4,16,4096]{3,2,0,1:T(8,128)(2,1)} copy(bf16[8,4,16,4096]{3,2,1,0:T(8,128)(2,1)S(1)} %bitcast.11) | data formatting | bytes 8388608 | tf_op jit(solution)/shard_map/reshape | solution.py:97
  131.1 4.8 %all-to-all-start.1 = ((bf16[8,4,16,4096]{3,2,0,1:T(8,128)(2,1)}), bf16[8,4,16,4096]{3,2,0,1:T(8,128)(2,1)}, u32[]{:S(2)}, u32[]{:S(2)}) async-start(bf16[8,4,16,4096]{3,2,0,1:T(8,128)(2,1)} %copy.19), calls=%async_computation.1 | async-start | bytes 8388608 | tf_op jit(solution)/shard_map/all_to_all | solution.py:98
  136.0 48.2 %all-to-all-done.1 = bf16[8,4,16,4096]{3,2,0,1:T(8,128)(2,1)} async-done(((bf16[8,4,16,4096]{3,2,0,1:T(8,128)(2,1)}), bf16[8,4,16,4096]{3,2,0,1:T(8,128)(2,1)}, u32[]{:S(2)}, u32[]{:S(2)}) %all-to-all-start.1) | async-done | bytes 4194336 | tf_op jit(solution)/shard_map/all_to_all | solution.py:98
  184.2 4.2 %reduce_sum.30 = bf16[8,16,4096]{2,1,0:T(8,128)(2,1)} reduce(bf16[8,4,16,4096]{3,2,0,1:T(8,128)(2,1)} %all-to-all-done.1, bf16[]{:T(256)} %constant.47.clone.1), dimensions={1}, to_apply=%region_1.0 | reduce | flops 1572864 | bytes 5242882 | tf_op jit(solution)/shard_map/reduce_sum | solution.py:99
  188.4 6.9 %all-to-all-start.2 = ((bf16[8,16,4096]{2,1,0:T(8,128)(2,1)}), bf16[8,16,4096]{2,1,0:T(8,128)(2,1)}, u32[]{:S(2)}, u32[]{:S(2)}) async-start(bf16[8,16,4096]{2,1,0:T(8,128)(2,1)} %reduce_sum.30), calls=%async_computation.2 | async-start | bytes 2097152 | tf_op jit(solution)/shard_map/all_to_all | solution.py:100
  195.4 4.2 %fusion.10 = f32[1280,256]{1,0:T(8,128)S(1)} fusion(bf16[1280,4096]{1,0:T(8,128)(2,1)} %all-gather.5.cloned.1.call-done, bf16[2048,768]{1,0:T(8,128)(2,1)S(1)} %bitcast.19), kind=kOutput, calls=%fused_computation.14 | convolution fusion | flops 1342177280 | bytes 7602176 | tf_op jit(solution)/shard_map/dot_general | solution.py:27
  199.6 1.3 copy-done.4
  200.9 1.5 fusion.2
  202.5 1.6 fusion.12
  204.0 2.9 %fusion.26 = bf16[1,2048,256]{2,1,0:T(8,128)(2,1)} fusion(bf16[1280,4096]{1,0:T(8,128)(2,1)S(1)} %copy-done.4, f32[1280,256]{1,0:T(8,128)S(1)} %fusion.2, f32[1280,256]{1,0:T(8,128)S(1)} %fusion.10), kind=kOutput, calls=%fused_computation.23 | convolution fusion | flops 1344667648 | bytes 8912896 | tf_op jit(solution)/shard_map/dot_general | solution.py:15
  206.9 2.9 %fusion.23 = bf16[1,2048,256]{2,1,0:T(8,128)(2,1)} fusion(bf16[1280,4096]{1,0:T(8,128)(2,1)S(1)} %copy-done.4, f32[1280,256]{1,0:T(8,128)S(1)} %fusion.12, f32[1280,256]{1,0:T(8,128)S(1)} %fusion.10), kind=kOutput, calls=%fused_computation.22 | convolution fusion | flops 1344667648 | bytes 8912896 | tf_op jit(solution)/shard_map/dot_general | solution.py:15
  209.8 3.0 %fusion.29 = bf16[1,2048,256]{2,1,0:T(8,128)(2,1)} fusion(bf16[1280,4096]{1,0:T(8,128)(2,1)S(1)} %copy-done.4, f32[1280,256]{1,0:T(8,128)S(1)} %fusion.10, f32[1280,256]{1,0:T(8,128)S(1)} %fusion.2, f32[1280,256]{1,0:T(8,128)S(1)} %fusion.12), kind=kOutput, calls=%fused_computation.24 | convolution fusion | flops 1345978368 | bytes 10223616 | tf_op jit(solution)/shard_map/dot_general | solution.py:15
  212.7 1.4 reduce.8
  214.1 0.6 slice.90
  214.7 0.7 multiply_convert_fusion.14
  (21 shorter events, 0.4 us)
Async XLA Ops:
  7.2 58.0 %all-gather.3.cloned.1.call-start = ((), (), s32[]{:S(2)}) async-start(), calls=%async_computation.4 | async-start | bytes 4460544 | tf_op jit(solution)/shard_map/all_gather | solution.py:60
  9.3 31.7 %copy-start = (bf16[256,256]{1,0:T(8,128)(2,1)S(1)}, bf16[256,256]{1,0:T(8,128)(2,1)}, u32[]{:S(2)}) copy-start(bf16[256,256]{1,0:T(8,128)(2,1)} %param.15) | copy-start | bytes 393220
  9.3 31.7 %copy-start.1 = (bf16[256,256]{1,0:T(8,128)(2,1)S(1)}, bf16[256,256]{1,0:T(8,128)(2,1)}, u32[]{:S(2)}) copy-start(bf16[256,256]{1,0:T(8,128)(2,1)} %param.14) | copy-start | bytes 393220
  9.3 31.7 %copy-start.2 = (bf16[256,256]{1,0:T(8,128)(2,1)S(1)}, bf16[256,256]{1,0:T(8,128)(2,1)}, u32[]{:S(2)}) copy-start(bf16[256,256]{1,0:T(8,128)(2,1)} %param.13) | copy-start | bytes 393220
  10.9 184.5 %all-gather.5.cloned.1.call-start = ((), (), s32[]{:S(2)}) async-start(), calls=%async_computation.5 | async-start | bytes 10813440 | tf_op jit(solution)/shard_map/all_gather | solution.py:94
  42.9 75.7 %all-to-all-start = ((bf16[8,256,768]{2,1,0:T(8,128)(2,1)}), bf16[8,256,768]{2,1,0:T(8,128)(2,1)S(1)}, u32[]{:S(2)}, u32[]{:S(2)}) async-start(bf16[8,256,768]{2,1,0:T(8,128)(2,1)} %broadcast_in_dim.12), calls=%async_computation | async-start | bytes 6291456 | tf_op jit(solution)/shard_map/all_to_all | solution.py:50
  118.6 3.2 %copy-start.3 = (bf16[512,4224]{1,0:T(8,128)(2,1)S(1)}, bf16[512,4224]{1,0:T(8,128)(2,1)}, u32[]{:S(2)}) copy-start(bf16[512,4224]{1,0:T(8,128)(2,1)} %all-gather.3.cloned.1.call-done) | copy-start | bytes 12976132
  131.1 53.1 %all-to-all-start.1 = ((bf16[8,4,16,4096]{3,2,0,1:T(8,128)(2,1)}), bf16[8,4,16,4096]{3,2,0,1:T(8,128)(2,1)}, u32[]{:S(2)}, u32[]{:S(2)}) async-start(bf16[8,4,16,4096]{3,2,0,1:T(8,128)(2,1)} %copy.19), calls=%async_computation.1 | async-start | bytes 8388608 | tf_op jit(solution)/shard_map/all_to_all | solution.py:98
  188.4 24.3 %all-to-all-start.2 = ((bf16[8,16,4096]{2,1,0:T(8,128)(2,1)}), bf16[8,16,4096]{2,1,0:T(8,128)(2,1)}, u32[]{:S(2)}, u32[]{:S(2)}) async-start(bf16[8,16,4096]{2,1,0:T(8,128)(2,1)} %reduce_sum.30), calls=%async_computation.2 | async-start | bytes 2097152 | tf_op jit(solution)/shard_map/all_to_all | solution.py:100
  195.4 5.5 %copy-start.4 = (bf16[1280,4096]{1,0:T(8,128)(2,1)S(1)}, bf16[1280,4096]{1,0:T(8,128)(2,1)}, u32[]{:S(2)}) copy-start(bf16[1280,4096]{1,0:T(8,128)(2,1)} %all-gather.5.cloned.1.call-done) | copy-start | bytes 31457284
Sparse Core Ops, SparseCore 0:
  11.2 53.8 all-gather.2
  68.2 62.2 all-gather.4

commit v9 on v7

--- a/solution.py
+++ b/solution.py
@@ -57,7 +57,8 @@
     code_cols = jnp.zeros((count_tok, 128), jnp.bfloat16)
     code_cols = code_cols.at[:, 0:2].set(weight_codes.astype(jnp.bfloat16))
     home = jnp.concatenate([tokens, cotangent, code_cols], axis=1)
-    plane = lax.all_gather(home, GROUP, axis=0, tiled=True)
+    plane = lax.all_gather(home, "tensor", axis=0, tiled=True)
+    plane = lax.all_gather(plane, "dp", axis=0, tiled=True)
     plane_x = plane[:, :model_width]
     plane_dy = plane[:, model_width : 2 * model_width].astype(jnp.float32)
     plane_scale = plane[:, 2 * model_width : 2 * model_width + 2].astype(jnp.float32) / 256.0

time: 203 us -> 235 us (1.16)
  the two profiles are of different devices: /device:TPU:32 before, /device:TPU:101 now
where the time goes in v9:
time: 235 us; the launch traced here: 234 us
  waiting for transfers between devices  130 us (55%)
  blocking collectives  28.5 us (12%)
  matrix products  24.7 us (11%)
  starting transfers between devices  17.2 us (7%)
  between operations  14.2 us (6%)
  other arithmetic  10.8 us (5%)
  local copies, waits for them, and re-layouts  8.81 us (4%)
    all_gather x1, waiting for transfers between devices, shards(): rows = lax.all_gather(got, GROUP, axis=0, tiled=True)  64.7 us
    all_gather x1, waiting for transfers between devices, shards(): plane = lax.all_gather(plane, 'dp', axis=0, tiled=True)  40.2 us
    all_to_all x1, waiting for transfers between devices, shards(): lax.all_to_all(copies, 'expert', split_axis=0, concat_axis=0, tiled=True)  25.2 us
    all_to_all x1, blocking collectives, shards(): lax.all_to_all(send, 'expert', split_axis=0, concat_axis=0, tiled=True)  20.6 us
    all_to_all x1, starting transfers between devices, shards(): lax.all_to_all(pieces, GROUP, split_axis=0, concat_axis=0, tiled=True)  9.39 us
    dot_general x3, matrix products, contract_rows(): lax.dot_general(left_side, right_side, (((0,), (0,)), ((), ())), preferre...  8.31 us
    all_gather x1, blocking collectives, shards(): plane = lax.all_gather(home, 'tensor', axis=0, tiled=True)  7.93 us
    all_to_all x1, starting transfers between devices, shards(): lax.all_to_all(copies, 'expert', split_axis=0, concat_axis=0, tiled=True)  7.78 us
  transfers between devices with their start and end apart: 4, of which 3 were waited for; matrix products, arithmetic and copies ran while one was open for 15% of the time, Pallas kernels for 0%

profile of v9, /device:TPU:101, one launch (start us, length us, event | category | flops | bytes accessed | tf_op | source)
XLA Modules:
  0.0 234.4 jit_solution(17076146826277948566)
XLA Ops:
  7.2 0.6 compare_reduce_fusion
  7.9 1.3 broadcast_select_fusion
  9.2 0.1 copy.18
  9.3 0.9 fusion.67
  10.2 7.9 %all_gather.9 = bf16[64,4224]{1,0:T(8,128)(2,1)} all-gather(bf16[16,4224]{1,0:T(8,128)(2,1)S(1)} %fusion.67), channel_id=1, replica_groups=mesh['dp'=8,'expert'=8,'tensor'=4] {'tensor'}, dimensions={0}, use_global_device_ids=true | all-gather | bytes 675840 | tf_op jit(solution)/shard_map/all_gather | solution.py:60
  18.2 1.0 broadcast_in_dim.28
  19.2 0.2 convert_element_type.110
  19.4 0.7 convert_multiply_fusion.3
  20.1 0.1 copy.17
  20.2 0.1 div.27
  20.3 0.8 copy.16
  21.0 0.1 reshape.74
  21.1 0.9 broadcast_in_dim.13
  22.1 0.1 fusion.69
  22.2 0.1 reduce_window_sum.11
  22.2 0.2 select_reduce_fusion
  22.4 0.2 convolution_convert_fusion.2
  22.6 0.2 convolution_convert_fusion.1
  22.9 0.1 all_to_all.16
  23.0 20.6 %all_to_all.22 = bf16[8,5,4096]{2,1,0:T(8,128)(2,1)S(1)} all-to-all(bf16[8,5,4096]{2,1,0:T(8,128)(2,1)S(1)} %all_to_all.16), channel_id=1, replica_groups=mesh['dp'=8,'expert'=8,'tensor'=4] {'expert'}, dimensions={0} | all-to-all | bytes 655360 | tf_op jit(solution)/shard_map/all_to_all | solution.py:94
  43.6 0.9 all_to_all.18
  44.6 1.8 broadcast_in_dim.12
  46.4 7.8 %all-to-all-start = ((bf16[8,256,768]{2,1,0:T(8,128)(2,1)}), bf16[8,256,768]{2,1,0:T(8,128)(2,1)S(1)}, u32[]{:S(2)}, u32[]{:S(2)}) async-start(bf16[8,256,768]{2,1,0:T(8,128)(2,1)} %broadcast_in_dim.12), calls=%async_computation | async-start | bytes 6291456 | tf_op jit(solution)/shard_map/all_to_all | solution.py:50
  54.2 40.2 %all-gather.3.cloned.1.call-done = bf16[512,4224]{1,0:T(8,128)(2,1)} async-done(((bf16[64,4224]{1,0:T(8,128)(2,1)}), bf16[512,4224]{1,0:T(8,128)(2,1)}) %all-gather.3.cloned.1.call-update) | async-done | bytes 4325392 | tf_op jit(solution)/shard_map/all_gather | solution.py:61
  94.3 0.9 convert_multiply_fusion.2
  95.3 0.3 slice_reduce_fusion
  95.6 25.2 %all-to-all-done = bf16[8,256,768]{2,1,0:T(8,128)(2,1)S(1)} async-done(((bf16[8,256,768]{2,1,0:T(8,128)(2,1)}), bf16[8,256,768]{2,1,0:T(8,128)(2,1)S(1)}, u32[]{:S(2)}, u32[]{:S(2)}) %all-to-all-start) | async-done | bytes 3145760 | tf_op jit(solution)/shard_map/all_to_all | solution.py:50
  120.7 2.5 %fusion.43 = f32[512,256]{0,1:T(8,128)S(1)} fusion(bf16[512,4224]{1,0:T(8,128)(2,1)} %all-gather.3.cloned.1.call-done, bf16[2048,768]{1,0:T(8,128)(2,1)S(1)} %bitcast.12), kind=kOutput, calls=%fused_computation.36 | convolution fusion | flops 536870912 | bytes 3670016 | tf_op jit(solution)/shard_map/dot_general | solution.py:28
  123.3 0.3 copy-done.3
  123.6 0.7 fusion.45
  124.4 0.8 convolution_convert_fusion
  125.2 0.9 fusion.34
  126.1 1.1 multiply_convert_fusion.7
  127.2 1.3 fusion.39
  128.5 1.3 add_convert_fusion
  129.8 2.5 %pad_maximum_fusion = bf16[512,4096]{1,0:T(8,128)(2,1)} fusion(bf16[512,2048]{1,0:T(8,128)(2,1)S(1)} %add_convert_fusion, bf16[512,2048]{1,0:T(8,128)(2,1)S(1)} %convolution_convert_fusion), kind=kLoop, calls=%fused_computation.8 | loop fusion | flops 8388608 | bytes 8388608 | tf_op jit(solution)/shard_map/concatenate | solution.py:75
  132.3 9.4 %all-to-all-start.1 = ((bf16[32,16,4096]{2,1,0:T(8,128)(2,1)}), bf16[32,16,4096]{2,1,0:T(8,128)(2,1)}, u32[]{:S(2)}, u32[]{:S(2)}) async-start(bf16[32,16,4096]{2,1,0:T(8,128)(2,1)} %bitcast.11), calls=%async_computation.1 | async-start | bytes 8388608 | tf_op jit(solution)/shard_map/all_to_all | solution.py:98
  141.7 64.7 %all-gather.5.cloned.1.call-done = bf16[1280,4096]{1,0:T(8,128)(2,1)} async-done(((bf16[40,4096]{1,0:T(8,128)(2,1)}), bf16[1280,4096]{1,0:T(8,128)(2,1)}) %all-gather.5.cloned.1.call-update) | async-done | bytes 10485776 | tf_op jit(solution)/shard_map/all_gather | solution.py:95
  206.4 4.2 %fusion.10 = f32[1280,256]{1,0:T(8,128)S(1)} fusion(bf16[1280,4096]{1,0:T(8,128)(2,1)} %all-gather.5.cloned.1.call-done, bf16[2048,768]{1,0:T(8,128)(2,1)S(1)} %bitcast.19), kind=kOutput, calls=%fused_computation.14 | convolution fusion | flops 1342177280 | bytes 7602176 | tf_op jit(solution)/shard_map/dot_general | solution.py:27
  210.6 1.4 copy-done.4
  212.0 1.5 fusion.2
  213.5 1.5 fusion.12
  215.1 2.7 %fusion.26 = bf16[1,2048,256]{2,1,0:T(8,128)(2,1)} fusion(bf16[1280,4096]{1,0:T(8,128)(2,1)S(1)} %copy-done.4, f32[1280,256]{1,0:T(8,128)S(1)} %fusion.2, f32[1280,256]{1,0:T(8,128)S(1)} %fusion.10), kind=kOutput, calls=%fused_computation.23 | convolution fusion | flops 1344667648 | bytes 8912896 | tf_op jit(solution)/shard_map/dot_general | solution.py:15
  217.8 2.7 %fusion.23 = bf16[1,2048,256]{2,1,0:T(8,128)(2,1)} fusion(bf16[1280,4096]{1,0:T(8,128)(2,1)S(1)} %copy-done.4, f32[1280,256]{1,0:T(8,128)S(1)} %fusion.12, f32[1280,256]{1,0:T(8,128)S(1)} %fusion.10), kind=kOutput, calls=%fused_computation.22 | convolution fusion | flops 1344667648 | bytes 8912896 | tf_op jit(solution)/shard_map/dot_general | solution.py:15
  220.5 2.8 %fusion.29 = bf16[1,2048,256]{2,1,0:T(8,128)(2,1)} fusion(bf16[1280,4096]{1,0:T(8,128)(2,1)S(1)} %copy-done.4, f32[1280,256]{1,0:T(8,128)S(1)} %fusion.10, f32[1280,256]{1,0:T(8,128)S(1)} %fusion.2, f32[1280,256]{1,0:T(8,128)S(1)} %fusion.12), kind=kOutput, calls=%fused_computation.24 | convolution fusion | flops 1345978368 | bytes 10223616 | tf_op jit(solution)/shard_map/dot_general | solution.py:15
  223.4 2.8 %reduce.7 = bf16[16,4096]{1,0:T(8,128)(2,1)S(1)} reduce(bf16[32,16,4096]{2,1,0:T(8,128)(2,1)} %all-to-all-done.1, bf16[]{:T(256)} %constant.46.clone.1), dimensions={0}, to_apply=%region_3.4.clone | reduce | flops 2031616 | bytes 4325378 | tf_op jit(solution)/shard_map/reduce_sum | solution.py:109
  226.2 0.6 slice.90
  226.9 0.7 multiply_convert_fusion.14
  (18 shorter events, 0.2 us)
Async XLA Ops:
  7.2 87.2 %all-gather.3.cloned.1.call-start = ((), (), s32[]{:S(2)}) async-start(), calls=%async_computation.3 | async-start | bytes 4866048 | tf_op jit(solution)/shard_map/all_gather | solution.py:61
  18.1 26.4 %copy-start = (bf16[256,256]{1,0:T(8,128)(2,1)S(1)}, bf16[256,256]{1,0:T(8,128)(2,1)}, u32[]{:S(2)}) copy-start(bf16[256,256]{1,0:T(8,128)(2,1)} %param.15) | copy-start | bytes 393220
  18.1 26.4 %copy-start.1 = (bf16[256,256]{1,0:T(8,128)(2,1)S(1)}, bf16[256,256]{1,0:T(8,128)(2,1)}, u32[]{:S(2)}) copy-start(bf16[256,256]{1,0:T(8,128)(2,1)} %param.14) | copy-start | bytes 393220
  18.1 26.4 %copy-start.2 = (bf16[256,256]{1,0:T(8,128)(2,1)S(1)}, bf16[256,256]{1,0:T(8,128)(2,1)}, u32[]{:S(2)}) copy-start(bf16[256,256]{1,0:T(8,128)(2,1)} %param.13) | copy-start | bytes 393220
  18.1 188.3 %all-gather.5.cloned.1.call-start = ((), (), s32[]{:S(2)}) async-start(), calls=%async_computation.4 | async-start | bytes 10813440 | tf_op jit(solution)/shard_map/all_gather | solution.py:95
  46.4 74.3 %all-to-all-start = ((bf16[8,256,768]{2,1,0:T(8,128)(2,1)}), bf16[8,256,768]{2,1,0:T(8,128)(2,1)S(1)}, u32[]{:S(2)}, u32[]{:S(2)}) async-start(bf16[8,256,768]{2,1,0:T(8,128)(2,1)} %broadcast_in_dim.12), calls=%async_computation | async-start | bytes 6291456 | tf_op jit(solution)/shard_map/all_to_all | solution.py:50
  120.7 2.9 %copy-start.3 = (bf16[512,4224]{1,0:T(8,128)(2,1)S(1)}, bf16[512,4224]{1,0:T(8,128)(2,1)}, u32[]{:S(2)}) copy-start(bf16[512,4224]{1,0:T(8,128)(2,1)} %all-gather.3.cloned.1.call-done) | copy-start | bytes 12976132
  132.3 91.1 %all-to-all-start.1 = ((bf16[32,16,4096]{2,1,0:T(8,128)(2,1)}), bf16[32,16,4096]{2,1,0:T(8,128)(2,1)}, u32[]{:S(2)}, u32[]{:S(2)}) async-start(bf16[32,16,4096]{2,1,0:T(8,128)(2,1)} %bitcast.11), calls=%async_computation.1 | async-start | bytes 8388608 | tf_op jit(solution)/shard_map/all_to_all | solution.py:98
  206.4 5.5 %copy-start.4 = (bf16[1280,4096]{1,0:T(8,128)(2,1)S(1)}, bf16[1280,4096]{1,0:T(8,128)(2,1)}, u32[]{:S(2)}) copy-start(bf16[1280,4096]{1,0:T(8,128)(2,1)} %all-gather.5.cloned.1.call-done) | copy-start | bytes 31457284
Sparse Core Ops, SparseCore 0:
  18.2 76.0 all-gather.2
  97.5 108.9 all-gather.4

commit v10 on v7

--- a/solution.py
+++ b/solution.py
@@ -71,7 +71,6 @@
         grad_term = grad_term + contract_cols(
             jnp.concatenate([gate_grad, up_grad], axis=1), gate_up_cols
         )
-    terms = jnp.concatenate([out_term, grad_term.astype(jnp.bfloat16)], axis=1)
 
     flat_route = routes.reshape(-1)
     flat_scale = weight_codes.reshape(-1).astype(jnp.float32) / 256.0
@@ -92,9 +91,12 @@
     send = jnp.concatenate([send_x, send_s], axis=1)
     got = lax.all_to_all(send, "expert", split_axis=0, concat_axis=0, tiled=True)
     rows = lax.all_gather(got, GROUP, axis=0, tiled=True)
-    n_group = terms.shape[0] // count_tok
-    pieces = terms.reshape(n_group, count_tok, 2 * model_width)
-    pieces = lax.all_to_all(pieces, GROUP, split_axis=0, concat_axis=0, tiled=True)
+    n_group = out_term.shape[0] // count_tok
+    out_pieces = out_term.reshape(n_group, count_tok, model_width)
+    out_pieces = lax.all_to_all(out_pieces, GROUP, split_axis=0, concat_axis=0, tiled=True)
+    out_pieces, grad_term = lax.optimization_barrier((out_pieces, grad_term))
+    grad_pieces = grad_term.astype(jnp.bfloat16).reshape(n_group, count_tok, model_width)
+    grad_pieces = lax.all_to_all(grad_pieces, GROUP, split_axis=0, concat_axis=0, tiled=True)
     rows_x = rows[:, :model_width]
     rows_s = rows[:, model_width:]
     r_up, r_act, r_slope, r_hidden = forward_parts(rows_x, gate_cols, up_cols)
@@ -102,16 +104,16 @@
     grad_gate = contract_rows(rows_x, r_gate).astype(jnp.bfloat16)[None]
     grad_up = contract_rows(rows_x, r_upg).astype(jnp.bfloat16)[None]
     grad_down_t = contract_rows(rows_s, r_hidden).astype(jnp.bfloat16)[None]
-    pieces, grad_gate, grad_up, grad_down_t = lax.optimization_barrier(
-        (pieces, grad_gate, grad_up, grad_down_t)
+    out_pieces, grad_pieces, grad_gate, grad_up, grad_down_t = lax.optimization_barrier(
+        (out_pieces, grad_pieces, grad_gate, grad_up, grad_down_t)
     )
-    summed = jnp.sum(pieces.astype(jnp.float32), axis=0)
-    expert_out = summed[:, :model_width].astype(jnp.bfloat16).astype(jnp.float32)
+    expert_out = jnp.sum(out_pieces.astype(jnp.float32), axis=0)
+    expert_out = expert_out.astype(jnp.bfloat16).astype(jnp.float32)
     code_scale = weight_codes.astype(jnp.float32) / 256.0
     mixed = (code_scale[:, 0:1] * expert_out + code_scale[:, 1:2] * expert_out).astype(
         jnp.bfloat16
     )
-    input_grad = summed[:, model_width:].astype(jnp.bfloat16)
+    input_grad = jnp.sum(grad_pieces.astype(jnp.float32), axis=0).astype(jnp.bfloat16)
     return (mixed, input_grad, grad_gate, grad_up, grad_down_t)
 
 

time: 203 us -> 209 us (1.030)
  blocking collectives: 24.4 us -> 99 us
  waiting for transfers between devices: 106 us -> 32.3 us
  matrix products: 24.9 us -> 32.4 us
    all_to_all x0 -> x1, blocking collectives: none -> 74.6 us  [shards(): lax.all_to_all(copies, 'expert', split_axis=0, concat_axis=0, tiled=True)]
    all_to_all x2, waiting for transfers between devices: 88.6 us -> 32.3 us  [the longest x1 19.5 us: shards(): lax.all_to_all(out_pieces, GROUP, split_axis=0, concat_axis=0, tiled=True)]
    all_gather x1, waiting for transfers between devices: 17.2 us -> 0.01 us  [shards(): plane = lax.all_gather(home, GROUP, axis=0, tiled=True)]
    dot_general x3, matrix products: 3.56 us -> 6.69 us  [grad_parts(): hidden_grad = jnp.dot(scaled, down_cols, preferred_element_type=jnp.float32)]
    dot_general x3, matrix products: 3.41 us -> 6.17 us  [contract_cols(): lax.dot_general(left_side, right_side, (((1,), (1,)), ((), ())), preferre...]
    concatenate x1 -> x0, other arithmetic: 2.48 us -> none  [shards(): terms = jnp.concatenate([out_term, grad_term.astype(jnp.bfloat16)], axis=1)]
    reduce_sum x1 -> x2, other arithmetic: 2.83 us -> 4.47 us  [the longest x1 2.56 us: shards(): jnp.sum(grad_pieces.astype(jnp.float32), axis=0).astype(jnp.bfloat16)]
  transfers between devices with their start and end apart: 4 -> 4, of which waited for: 3 -> 2; matrix products, arithmetic and copies ran while one was open for 17% -> 18% of each run, Pallas kernels for 0% -> 0%
where the time goes in v10:
time: 209 us; the launch traced here: 208 us
  blocking collectives  99 us (47%)
  matrix products  32.4 us (16%)
  waiting for transfers between devices  32.3 us (15%)
  between operations  14.3 us (7%)
  starting transfers between devices  12.5 us (6%)
  other arithmetic  10.7 us (5%)
  local copies, waits for them, and re-layouts  6.89 us (3%)
    all_to_all x1, blocking collectives, shards(): lax.all_to_all(copies, 'expert', split_axis=0, concat_axis=0, tiled=True)  74.6 us
    all_to_all x1, blocking collectives, shards(): lax.all_to_all(send, 'expert', split_axis=0, concat_axis=0, tiled=True)  24.4 us
    all_to_all x1, waiting for transfers between devices, shards(): lax.all_to_all(out_pieces, GROUP, split_axis=0, concat_axis=0, tiled=True)  19.5 us
    all_to_all x1, waiting for transfers between devices, shards(): lax.all_to_all(grad_pieces, GROUP, split_axis=0, concat_axis=0, tiled=True)  12.8 us
    dot_general x3, matrix products, contract_rows(): lax.dot_general(left_side, right_side, (((0,), (0,)), ((), ())), preferre...  8.31 us
    all_to_all x1, starting transfers between devices, shards(): lax.all_to_all(out_pieces, GROUP, split_axis=0, concat_axis=0, tiled=True)  7.45 us
    dot_general x2, matrix products, forward_parts(): gate_pre = jnp.dot(rows_x, gate_cols, preferred_element_type=jnp.float32)  6.89 us
    dot_general x3, matrix products, grad_parts(): hidden_grad = jnp.dot(scaled, down_cols, preferred_element_type=jnp.float32)  6.69 us
  transfers between devices with their start and end apart: 4, of which 2 were waited for; matrix products, arithmetic and copies ran while one was open for 18% of the time, Pallas kernels for 0%

profile of v10, /device:TPU:32, one launch (start us, length us, event | category | flops | bytes accessed | tf_op | source)
XLA Modules:
  0.0 208.2 jit_solution(6839514295071946212)
XLA Ops:
  7.2 0.6 compare_reduce_fusion
  7.9 1.3 broadcast_select_fusion
  9.2 0.1 copy.18
  9.3 1.6 fusion.67
  10.9 0.0 all-gather.5.cloned.1.call-start
  10.9 0.9 broadcast_in_dim.28
  11.9 0.2 convert_element_type.109
  12.1 0.7 convert_multiply_fusion.3
  12.8 0.1 copy.17
  12.9 0.1 div.27
  13.0 0.8 copy.16
  13.7 0.1 reshape.78
  13.8 0.9 broadcast_in_dim.13
  14.7 0.1 reshape.79
  14.8 0.1 fusion.69
  14.8 0.1 reduce_window_sum.11
  14.9 0.2 select_reduce_fusion
  15.1 0.2 convolution_convert_fusion.2
  15.3 0.2 convolution_convert_fusion.1
  15.6 0.1 all_to_all.20
  15.7 24.4 %all_to_all.27 = bf16[8,5,4096]{2,1,0:T(8,128)(2,1)S(1)} all-to-all(bf16[8,5,4096]{2,1,0:T(8,128)(2,1)S(1)} %all_to_all.20), channel_id=1, replica_groups=mesh['dp'=8,'expert'=8,'tensor'=4] {'expert'}, dimensions={0} | all-to-all | bytes 655360 | tf_op jit(solution)/shard_map/all_to_all | solution.py:92
  40.1 0.9 all_to_all.22
  41.1 0.2 broadcast_in_dim.12
  41.3 74.6 %all_to_all.28 = bf16[8,256,768]{2,1,0:T(8,128)(2,1)S(1)} all-to-all(bf16[8,256,768]{2,1,0:T(8,128)(2,1)S(1)} %broadcast_in_dim.12), channel_id=1, replica_groups=mesh['dp'=8,'expert'=8,'tensor'=4] {'expert'}, dimensions={0} | all-to-all | bytes 6291456 | tf_op jit(solution)/shard_map/all_to_all | solution.py:50
  115.9 2.4 %fusion.43 = f32[512,256]{0,1:T(8,128)S(1)} fusion(bf16[512,4224]{1,0:T(8,128)(2,1)} %all-gather.3.cloned.1.call-done, bf16[2048,768]{1,0:T(8,128)(2,1)S(1)} %bitcast.12), kind=kOutput, calls=%fused_computation.35 | convolution fusion | flops 536870912 | bytes 3670016 | tf_op jit(solution)/shard_map/dot_general | solution.py:28
  118.3 2.7 %fusion.45 = f32[512,256]{0,1:T(8,128)S(1)} fusion(bf16[512,4224]{1,0:T(8,128)(2,1)} %all-gather.3.cloned.1.call-done, bf16[2048,768]{1,0:T(8,128)(2,1)S(1)} %bitcast.13), kind=kOutput, calls=%fused_computation.37 | convolution fusion | flops 536870912 | bytes 3670016 | tf_op jit(solution)/shard_map/dot_general | solution.py:27
  121.1 0.8 copy-done.6
  121.8 2.1 %convolution_convert_fusion = bf16[512,2048]{1,0:T(8,128)(2,1)} fusion(bf16[2048,768]{1,0:T(8,128)(2,1)S(1)} %bitcast.14, f32[512,256]{0,1:T(8,128)S(1)} %fusion.43, f32[512,256]{0,1:T(8,128)S(1)} %fusion.45), kind=kOutput, calls=%fused_computation.17 | convolution fusion | flops 538705920 | bytes 4194304 | tf_op jit(solution)/shard_map/dot_general | solution.py:21
  124.0 7.4 %all-to-all-start.1 = ((bf16[32,16,2048]{2,1,0:T(8,128)(2,1)}), bf16[32,16,2048]{2,1,0:T(8,128)(2,1)}, u32[]{:S(2)}, u32[]{:S(2)}) async-start(bf16[32,16,2048]{2,1,0:T(8,128)(2,1)} %bitcast.23), calls=%async_computation.1 | async-start | bytes 4194304 | tf_op jit(solution)/shard_map/all_to_all | solution.py:96
  131.5 0.9 convert_multiply_fusion.2
  132.4 0.3 slice_reduce_fusion
  132.7 2.5 %fusion.34 = f32[512,256]{0,1:T(8,128)S(1)} fusion(f32[512]{0:T(512)S(1)} %get-tuple-element.32, bf16[512,4224]{1,0:T(8,128)(2,1)} %all-gather.3.cloned.1.call-done, bf16[2048,768]{1,0:T(8,128)(2,1)S(1)} %bitcast.15), kind=kOutput, calls=%fused_computation.27 | convolution fusion | flops 540016640 | bytes 3672064 | tf_op jit(solution)/shard_map/dot_general | solution.py:35
  135.2 2.7 %multiply_convert_fusion.7 = (bf16[512,256]{0,1:T(8,128)(2,1)S(1)}, bf16[512,256]{0,1:T(8,128)(2,1)S(1)}, bf16[512,256]{0,1:T(8,128)(2,1)S(1)}, bf16[512,256]{0,1:T(8,128)(2,1)S(1)}) fusion(f32[512,256]{0,1:T(8,128)S(1)} %copy-done.5, f32[512,256]{0,1:T(8,128)S(1)} %copy-done.7, f32[512,256]{0,1:T(8,128)S(1)} %fusion.34, ...), kind=kOutput, calls=%fused_computation.60 | convolution fusion | flops 542375936 | bytes 5769216 | tf_op jit(solution)/shard_map/dot_general | solution.py:35
  137.9 1.3 fusion.39
  139.2 2.7 %convolution_add_fusion = bf16[512,2048]{1,0:T(8,128)(2,1)} fusion(f32[512,2048]{1,0:T(8,128)S(1)} %fusion.39, bf16[2048,768]{1,0:T(8,128)(2,1)S(1)} %bitcast.18, bf16[512,256]{0,1:T(8,128)(2,1)S(1)} %get-tuple-element.36, bf16[512,256]{0,1:T(8,128)(2,1)S(1)} %get-tuple-element.33), kind=kOutput, calls=%fused_computation.16 | convolution fusion | flops 1076887552 | bytes 8912896 | tf_op jit(solution)/shard_map/dot_general | solution.py:21
  141.9 19.5 %all-to-all-done.1 = bf16[32,16,2048]{2,1,0:T(8,128)(2,1)} async-done(((bf16[32,16,2048]{2,1,0:T(8,128)(2,1)}), bf16[32,16,2048]{2,1,0:T(8,128)(2,1)}, u32[]{:S(2)}, u32[]{:S(2)}) %all-to-all-start.1) | async-done | bytes 2097184 | tf_op jit(solution)/shard_map/all_to_all | solution.py:96
  161.4 4.9 %all-to-all-start.2 = ((bf16[32,16,2048]{2,1,0:T(8,128)(2,1)}), bf16[32,16,2048]{2,1,0:T(8,128)(2,1)}, u32[]{:S(2)}, u32[]{:S(2)}) async-start(bf16[32,16,2048]{2,1,0:T(8,128)(2,1)} %bitcast.22), calls=%async_computation.2 | async-start | bytes 4194304 | tf_op jit(solution)/shard_map/all_to_all | solution.py:99
  166.4 4.2 %fusion.10 = f32[1280,256]{1,0:T(8,128)S(1)} fusion(bf16[1280,4096]{1,0:T(8,128)(2,1)} %all-gather.5.cloned.1.call-done, bf16[2048,768]{1,0:T(8,128)(2,1)S(1)} %bitcast.19), kind=kOutput, calls=%fused_computation.12 | convolution fusion | flops 1342177280 | bytes 7602176 | tf_op jit(solution)/shard_map/dot_general | solution.py:27
  170.6 1.3 copy-done.3
  171.9 1.5 fusion.2
  173.5 2.7 %fusion.26 = bf16[1,2048,256]{2,1,0:T(8,128)(2,1)} fusion(bf16[1280,4096]{1,0:T(8,128)(2,1)S(1)} %copy-done.3, f32[1280,256]{1,0:T(8,128)S(1)} %fusion.2, f32[1280,256]{1,0:T(8,128)S(1)} %fusion.10), kind=kOutput, calls=%fused_computation.22 | convolution fusion | flops 1344667648 | bytes 8912896 | tf_op jit(solution)/shard_map/dot_general | solution.py:15
  176.2 1.5 fusion.12
  177.8 2.7 %fusion.23 = bf16[1,2048,256]{2,1,0:T(8,128)(2,1)} fusion(bf16[1280,4096]{1,0:T(8,128)(2,1)S(1)} %copy-done.3, f32[1280,256]{1,0:T(8,128)S(1)} %fusion.12, f32[1280,256]{1,0:T(8,128)S(1)} %fusion.10), kind=kOutput, calls=%fused_computation.21 | convolution fusion | flops 1344667648 | bytes 8912896 | tf_op jit(solution)/shard_map/dot_general | solution.py:15
  180.5 2.8 %fusion.29 = bf16[1,2048,256]{2,1,0:T(8,128)(2,1)} fusion(bf16[1280,4096]{1,0:T(8,128)(2,1)S(1)} %copy-done.3, f32[1280,256]{1,0:T(8,128)S(1)} %fusion.10, f32[1280,256]{1,0:T(8,128)S(1)} %fusion.2, f32[1280,256]{1,0:T(8,128)S(1)} %fusion.12), kind=kOutput, calls=%fused_computation.23 | convolution fusion | flops 1345978368 | bytes 10223616 | tf_op jit(solution)/shard_map/dot_general | solution.py:15
  183.3 12.8 %all-to-all-done.2 = bf16[32,16,2048]{2,1,0:T(8,128)(2,1)} async-done(((bf16[32,16,2048]{2,1,0:T(8,128)(2,1)}), bf16[32,16,2048]{2,1,0:T(8,128)(2,1)}, u32[]{:S(2)}, u32[]{:S(2)}) %all-to-all-start.2) | async-done | bytes 2097184 | tf_op jit(solution)/shard_map/all_to_all | solution.py:99
  196.1 1.9 reduce_sum.34
  198.1 2.6 %reduce_sum.35 = bf16[16,2048]{1,0:T(8,128)(2,1)} reduce(bf16[32,16,2048]{2,1,0:T(8,128)(2,1)} %all-to-all-done.2, bf16[]{:T(256)} %constant.48.clone.1), dimensions={0}, to_apply=%region_4.5 | reduce | flops 1015808 | bytes 2162690 | tf_op jit(solution)/shard_map/reduce_sum | solution.py:116
  200.6 0.7 multiply_convert_fusion.14
  (23 shorter events, 0.2 us)
Async XLA Ops:
  7.2 108.8 %all-gather.3.cloned.1.call-start = ((), (), s32[]{:S(2)}) async-start(), calls=%async_computation.4 | async-start | bytes 4460544 | tf_op jit(solution)/shard_map/all_gather | solution.py:60
  9.3 31.7 %copy-start = (bf16[256,256]{1,0:T(8,128)(2,1)S(1)}, bf16[256,256]{1,0:T(8,128)(2,1)}, u32[]{:S(2)}) copy-start(bf16[256,256]{1,0:T(8,128)(2,1)} %param.15) | copy-start | bytes 393220
  9.3 31.7 %copy-start.1 = (bf16[256,256]{1,0:T(8,128)(2,1)S(1)}, bf16[256,256]{1,0:T(8,128)(2,1)}, u32[]{:S(2)}) copy-start(bf16[256,256]{1,0:T(8,128)(2,1)} %param.14) | copy-start | bytes 393220
  9.3 31.7 %copy-start.2 = (bf16[256,256]{1,0:T(8,128)(2,1)S(1)}, bf16[256,256]{1,0:T(8,128)(2,1)}, u32[]{:S(2)}) copy-start(bf16[256,256]{1,0:T(8,128)(2,1)} %param.13) | copy-start | bytes 393220
  10.9 155.5 %all-gather.5.cloned.1.call-start = ((), (), s32[]{:S(2)}) async-start(), calls=%async_computation.5 | async-start | bytes 10813440 | tf_op jit(solution)/shard_map/all_gather | solution.py:93
  118.3 5.7 %copy-start.4 = (f32[512,256]{0,1:T(8,128)}, f32[512,256]{0,1:T(8,128)S(1)}, u32[]{:S(2)}) copy-start(f32[512,256]{0,1:T(8,128)S(1)} %fusion.43) | copy-start | bytes 1572868
  121.0 0.8 copy-start.6
  124.0 37.4 %all-to-all-start.1 = ((bf16[32,16,2048]{2,1,0:T(8,128)(2,1)}), bf16[32,16,2048]{2,1,0:T(8,128)(2,1)}, u32[]{:S(2)}, u32[]{:S(2)}) async-start(bf16[32,16,2048]{2,1,0:T(8,128)(2,1)} %bitcast.23), calls=%async_computation.1 | async-start | bytes 4194304 | tf_op jit(solution)/shard_map/all_to_all | solution.py:96
  132.4 2.8 %copy-start.5 = (f32[512,256]{0,1:T(8,128)S(1)}, f32[512,256]{0,1:T(8,128)}, u32[]{:S(2)}) copy-start(f32[512,256]{0,1:T(8,128)} %copy-done.4) | copy-start | bytes 1572868
  132.4 2.8 %copy-start.7 = (f32[512,256]{0,1:T(8,128)S(1)}, f32[512,256]{0,1:T(8,128)}, u32[]{:S(2)}) copy-start(f32[512,256]{0,1:T(8,128)} %copy-done.6) | copy-start | bytes 1572868
  161.4 34.7 %all-to-all-start.2 = ((bf16[32,16,2048]{2,1,0:T(8,128)(2,1)}), bf16[32,16,2048]{2,1,0:T(8,128)(2,1)}, u32[]{:S(2)}, u32[]{:S(2)}) async-start(bf16[32,16,2048]{2,1,0:T(8,128)(2,1)} %bitcast.22), calls=%async_computation.2 | async-start | bytes 4194304 | tf_op jit(solution)/shard_map/all_to_all | solution.py:99
  166.4 5.5 %copy-start.3 = (bf16[1280,4096]{1,0:T(8,128)(2,1)S(1)}, bf16[1280,4096]{1,0:T(8,128)(2,1)}, u32[]{:S(2)}) copy-start(bf16[1280,4096]{1,0:T(8,128)(2,1)} %all-gather.5.cloned.1.call-done) | copy-start | bytes 31457284
Sparse Core Ops, SparseCore 0:
  11.2 53.8 all-gather.2
  68.2 62.2 all-gather.4

commit v11 on v7

--- a/solution.py
+++ b/solution.py
@@ -54,8 +54,7 @@
     down_cols = full_cols[:, 2 * hid :]
     gate_up_cols = full_cols[:, : 2 * hid]
 
-    code_cols = jnp.zeros((count_tok, 128), jnp.bfloat16)
-    code_cols = code_cols.at[:, 0:2].set(weight_codes.astype(jnp.bfloat16))
+    code_cols = jnp.pad(weight_codes.astype(jnp.bfloat16), ((0, 0), (0, 126)))
     home = jnp.concatenate([tokens, cotangent, code_cols], axis=1)
     plane = lax.all_gather(home, GROUP, axis=0, tiled=True)
     plane_x = plane[:, :model_width]

time: 203 us -> 202 us (level)
  no operation moved by 1% of the time
where the time goes in v11:
time: 202 us; the launch traced here: 201 us
  waiting for transfers between devices  106 us (52%)
  matrix products  24.7 us (12%)
  blocking collectives  24.4 us (12%)
  between operations  14.2 us (7%)
  starting transfers between devices  12.7 us (6%)
  other arithmetic  10.3 us (5%)
  local copies, waits for them, and re-layouts  8.91 us (4%)
    all_to_all x1, waiting for transfers between devices, shards(): lax.all_to_all(copies, 'expert', split_axis=0, concat_axis=0, tiled=True)  51 us
    all_to_all x1, waiting for transfers between devices, shards(): lax.all_to_all(pieces, GROUP, split_axis=0, concat_axis=0, tiled=True)  36.3 us
    all_to_all x1, blocking collectives, shards(): lax.all_to_all(send, 'expert', split_axis=0, concat_axis=0, tiled=True)  24.4 us
    all_gather x1, waiting for transfers between devices, shards(): plane = lax.all_gather(home, GROUP, axis=0, tiled=True)  18.5 us
    dot_general x3, matrix products, contract_rows(): lax.dot_general(left_side, right_side, (((0,), (0,)), ((), ())), preferre...  8.32 us
    all_to_all x1, starting transfers between devices, shards(): lax.all_to_all(pieces, GROUP, split_axis=0, concat_axis=0, tiled=True)  7.61 us
    all_to_all x1, starting transfers between devices, shards(): lax.all_to_all(copies, 'expert', split_axis=0, concat_axis=0, tiled=True)  5.01 us
    dot_general x2, matrix products, forward_parts(): gate_pre = jnp.dot(rows_x, gate_cols, preferred_element_type=jnp.float32)  4.91 us
  transfers between devices with their start and end apart: 4, of which 3 were waited for; matrix products, arithmetic and copies ran while one was open for 17% of the time, Pallas kernels for 0%

profile of v11, /device:TPU:32, one launch (start us, length us, event | category | flops | bytes accessed | tf_op | source)
XLA Modules:
  0.0 201.1 jit_solution(3990699922023904589)
XLA Ops:
  7.2 0.7 convert_element_type.97
  7.9 0.1 copy.18
  8.0 1.6 fusion.67
  9.6 0.0 all-gather.5.cloned.1.call-start
  9.7 0.9 broadcast_in_dim.27
  10.6 0.2 convert_element_type.112
  10.8 0.7 convert_multiply_fusion.3
  11.5 0.1 copy.17
  11.6 0.1 div.27
  11.7 0.8 copy.16
  12.4 0.1 reshape.48
  12.5 0.9 broadcast_in_dim.26
  13.4 0.1 reshape.49
  13.5 0.1 fusion.69
  13.6 0.1 reduce_window_sum.11
  13.6 0.2 select_reduce_fusion
  13.8 0.2 convolution_convert_fusion.2
  14.0 0.2 convolution_convert_fusion.1
  14.3 0.1 all_to_all.16
  14.4 24.4 %all_to_all.22 = bf16[8,5,4096]{2,1,0:T(8,128)(2,1)S(1)} all-to-all(bf16[8,5,4096]{2,1,0:T(8,128)(2,1)S(1)} %all_to_all.16), channel_id=1, replica_groups=mesh['dp'=8,'expert'=8,'tensor'=4] {'expert'}, dimensions={0} | all-to-all | bytes 655360 | tf_op jit(solution)/shard_map/all_to_all | solution.py:92
  38.8 0.9 all_to_all.18
  39.8 1.8 broadcast_in_dim.12
  41.6 5.0 %all-to-all-start = ((bf16[8,256,768]{2,1,0:T(8,128)(2,1)}), bf16[8,256,768]{2,1,0:T(8,128)(2,1)S(1)}, u32[]{:S(2)}, u32[]{:S(2)}) async-start(bf16[8,256,768]{2,1,0:T(8,128)(2,1)} %broadcast_in_dim.12), calls=%async_computation | async-start | bytes 6291456 | tf_op jit(solution)/shard_map/all_to_all | solution.py:50
  46.6 18.5 %all-gather.3.cloned.1.call-done = bf16[512,4224]{1,0:T(8,128)(2,1)} async-done(((bf16[16,4224]{1,0:T(8,128)(2,1)}), bf16[512,4224]{1,0:T(8,128)(2,1)}) %all-gather.3.cloned.1.call-update) | async-done | bytes 4325392 | tf_op jit(solution)/shard_map/all_gather | solution.py:59
  65.1 0.9 convert_multiply_fusion.2
  66.1 0.3 slice_reduce_fusion
  66.4 51.0 %all-to-all-done = bf16[8,256,768]{2,1,0:T(8,128)(2,1)S(1)} async-done(((bf16[8,256,768]{2,1,0:T(8,128)(2,1)}), bf16[8,256,768]{2,1,0:T(8,128)(2,1)S(1)}, u32[]{:S(2)}, u32[]{:S(2)}) %all-to-all-start) | async-done | bytes 3145760 | tf_op jit(solution)/shard_map/all_to_all | solution.py:50
  117.4 2.5 %fusion.43 = f32[512,256]{0,1:T(8,128)S(1)} fusion(bf16[512,4224]{1,0:T(8,128)(2,1)} %all-gather.3.cloned.1.call-done, bf16[2048,768]{1,0:T(8,128)(2,1)S(1)} %bitcast.12), kind=kOutput, calls=%fused_computation.36 | convolution fusion | flops 536870912 | bytes 3670016 | tf_op jit(solution)/shard_map/dot_general | solution.py:28
  119.9 0.6 copy-done.3
  120.5 0.7 fusion.45
  121.3 0.8 convolution_convert_fusion
  122.0 0.9 fusion.34
  123.0 1.1 multiply_convert_fusion.7
  124.1 1.3 fusion.39
  125.4 1.3 add_convert_fusion
  126.7 2.5 %pad_maximum_fusion = bf16[512,4096]{1,0:T(8,128)(2,1)} fusion(bf16[512,2048]{1,0:T(8,128)(2,1)S(1)} %add_convert_fusion, bf16[512,2048]{1,0:T(8,128)(2,1)S(1)} %convolution_convert_fusion), kind=kLoop, calls=%fused_computation.8 | loop fusion | flops 8388608 | bytes 8388608 | tf_op jit(solution)/shard_map/concatenate | solution.py:73
  129.2 7.6 %all-to-all-start.1 = ((bf16[32,16,4096]{2,1,0:T(8,128)(2,1)}), bf16[32,16,4096]{2,1,0:T(8,128)(2,1)}, u32[]{:S(2)}, u32[]{:S(2)}) async-start(bf16[32,16,4096]{2,1,0:T(8,128)(2,1)} %bitcast.11), calls=%async_computation.1 | async-start | bytes 8388608 | tf_op jit(solution)/shard_map/all_to_all | solution.py:96
  136.8 4.2 %fusion.10 = f32[1280,256]{1,0:T(8,128)S(1)} fusion(bf16[1280,4096]{1,0:T(8,128)(2,1)} %all-gather.5.cloned.1.call-done, bf16[2048,768]{1,0:T(8,128)(2,1)S(1)} %bitcast.19), kind=kOutput, calls=%fused_computation.14 | convolution fusion | flops 1342177280 | bytes 7602176 | tf_op jit(solution)/shard_map/dot_general | solution.py:27
  141.0 1.3 copy-done.4
  142.4 1.5 fusion.2
  143.9 1.5 fusion.12
  145.4 2.7 %fusion.26 = bf16[1,2048,256]{2,1,0:T(8,128)(2,1)} fusion(bf16[1280,4096]{1,0:T(8,128)(2,1)S(1)} %copy-done.4, f32[1280,256]{1,0:T(8,128)S(1)} %fusion.2, f32[1280,256]{1,0:T(8,128)S(1)} %fusion.10), kind=kOutput, calls=%fused_computation.23 | convolution fusion | flops 1344667648 | bytes 8912896 | tf_op jit(solution)/shard_map/dot_general | solution.py:15
  148.2 2.7 %fusion.23 = bf16[1,2048,256]{2,1,0:T(8,128)(2,1)} fusion(bf16[1280,4096]{1,0:T(8,128)(2,1)S(1)} %copy-done.4, f32[1280,256]{1,0:T(8,128)S(1)} %fusion.12, f32[1280,256]{1,0:T(8,128)S(1)} %fusion.10), kind=kOutput, calls=%fused_computation.22 | convolution fusion | flops 1344667648 | bytes 8912896 | tf_op jit(solution)/shard_map/dot_general | solution.py:15
  150.9 2.8 %fusion.29 = bf16[1,2048,256]{2,1,0:T(8,128)(2,1)} fusion(bf16[1280,4096]{1,0:T(8,128)(2,1)S(1)} %copy-done.4, f32[1280,256]{1,0:T(8,128)S(1)} %fusion.10, f32[1280,256]{1,0:T(8,128)S(1)} %fusion.2, f32[1280,256]{1,0:T(8,128)S(1)} %fusion.12), kind=kOutput, calls=%fused_computation.24 | convolution fusion | flops 1345978368 | bytes 10223616 | tf_op jit(solution)/shard_map/dot_general | solution.py:15
  153.8 36.3 %all-to-all-done.1 = bf16[32,16,4096]{2,1,0:T(8,128)(2,1)} async-done(((bf16[32,16,4096]{2,1,0:T(8,128)(2,1)}), bf16[32,16,4096]{2,1,0:T(8,128)(2,1)}, u32[]{:S(2)}, u32[]{:S(2)}) %all-to-all-start.1) | async-done | bytes 4194336 | tf_op jit(solution)/shard_map/all_to_all | solution.py:96
  190.1 2.8 %reduce = bf16[16,4096]{1,0:T(8,128)(2,1)S(1)} reduce(bf16[32,16,4096]{2,1,0:T(8,128)(2,1)} %all-to-all-done.1, bf16[]{:T(256)} %constant.8.clone.1), dimensions={0}, to_apply=%region_2.3.clone | reduce | flops 2031616 | bytes 4325378 | tf_op jit(solution)/shard_map/reduce_sum | solution.py:107
  192.9 0.6 slice.74
  193.6 0.7 multiply_convert_fusion.14
  (16 shorter events, 0.2 us)
Async XLA Ops:
  7.2 58.0 %all-gather.3.cloned.1.call-start = ((), (), s32[]{:S(2)}) async-start(), calls=%async_computation.3 | async-start | bytes 4460544 | tf_op jit(solution)/shard_map/all_gather | solution.py:59
  8.0 31.7 %copy-start = (bf16[256,256]{1,0:T(8,128)(2,1)S(1)}, bf16[256,256]{1,0:T(8,128)(2,1)}, u32[]{:S(2)}) copy-start(bf16[256,256]{1,0:T(8,128)(2,1)} %param.13) | copy-start | bytes 393220
  8.0 31.7 %copy-start.1 = (bf16[256,256]{1,0:T(8,128)(2,1)S(1)}, bf16[256,256]{1,0:T(8,128)(2,1)}, u32[]{:S(2)}) copy-start(bf16[256,256]{1,0:T(8,128)(2,1)} %param.12) | copy-start | bytes 393220
  8.0 31.7 %copy-start.2 = (bf16[256,256]{1,0:T(8,128)(2,1)S(1)}, bf16[256,256]{1,0:T(8,128)(2,1)}, u32[]{:S(2)}) copy-start(bf16[256,256]{1,0:T(8,128)(2,1)} %param.11) | copy-start | bytes 393220
  9.6 127.2 %all-gather.5.cloned.1.call-start = ((), (), s32[]{:S(2)}) async-start(), calls=%async_computation.4 | async-start | bytes 10813440 | tf_op jit(solution)/shard_map/all_gather | solution.py:93
  41.6 75.8 %all-to-all-start = ((bf16[8,256,768]{2,1,0:T(8,128)(2,1)}), bf16[8,256,768]{2,1,0:T(8,128)(2,1)S(1)}, u32[]{:S(2)}, u32[]{:S(2)}) async-start(bf16[8,256,768]{2,1,0:T(8,128)(2,1)} %broadcast_in_dim.12), calls=%async_computation | async-start | bytes 6291456 | tf_op jit(solution)/shard_map/all_to_all | solution.py:50
  117.4 3.1 %copy-start.3 = (bf16[512,4224]{1,0:T(8,128)(2,1)S(1)}, bf16[512,4224]{1,0:T(8,128)(2,1)}, u32[]{:S(2)}) copy-start(bf16[512,4224]{1,0:T(8,128)(2,1)} %all-gather.3.cloned.1.call-done) | copy-start | bytes 12976132
  129.2 60.9 %all-to-all-start.1 = ((bf16[32,16,4096]{2,1,0:T(8,128)(2,1)}), bf16[32,16,4096]{2,1,0:T(8,128)(2,1)}, u32[]{:S(2)}, u32[]{:S(2)}) async-start(bf16[32,16,4096]{2,1,0:T(8,128)(2,1)} %bitcast.11), calls=%async_computation.1 | async-start | bytes 8388608 | tf_op jit(solution)/shard_map/all_to_all | solution.py:96
  136.8 5.5 %copy-start.4 = (bf16[1280,4096]{1,0:T(8,128)(2,1)S(1)}, bf16[1280,4096]{1,0:T(8,128)(2,1)}, u32[]{:S(2)}) copy-start(bf16[1280,4096]{1,0:T(8,128)(2,1)} %all-gather.5.cloned.1.call-done) | copy-start | bytes 31457284
Sparse Core Ops, SparseCore 0:
  11.2 53.9 all-gather.2
  68.3 62.2 all-gather.4

commit v12 on v11

--- a/solution.py
+++ b/solution.py
@@ -54,22 +54,18 @@
     down_cols = full_cols[:, 2 * hid :]
     gate_up_cols = full_cols[:, : 2 * hid]
 
-    code_cols = jnp.pad(weight_codes.astype(jnp.bfloat16), ((0, 0), (0, 126)))
-    home = jnp.concatenate([tokens, cotangent, code_cols], axis=1)
+    code_scale = weight_codes.astype(jnp.float32) / 256.0
+    pair_scale = code_scale[:, 0:1] + code_scale[:, 1:2]
+    pair_scaled = (pair_scale * cotangent.astype(jnp.float32)).astype(jnp.bfloat16)
+    home = jnp.concatenate([tokens, pair_scaled], axis=1)
     plane = lax.all_gather(home, GROUP, axis=0, tiled=True)
     plane_x = plane[:, :model_width]
-    plane_dy = plane[:, model_width : 2 * model_width].astype(jnp.float32)
-    plane_scale = plane[:, 2 * model_width : 2 * model_width + 2].astype(jnp.float32) / 256.0
+    plane_s = plane[:, model_width:]
 
     up_pre, activation, act_slope, hidden = forward_parts(plane_x, gate_cols, up_cols)
     out_term = contract_cols(hidden, down_cols).astype(jnp.bfloat16)
-    grad_term = jnp.zeros(out_term.shape, jnp.float32)
-    for which in range(2):
-        scaled = (plane_scale[:, which : which + 1] * plane_dy).astype(jnp.bfloat16)
-        gate_grad, up_grad = grad_parts(scaled, down_cols, up_pre, activation, act_slope)
-        grad_term = grad_term + contract_cols(
-            jnp.concatenate([gate_grad, up_grad], axis=1), gate_up_cols
-        )
+    gate_grad, up_grad = grad_parts(plane_s, down_cols, up_pre, activation, act_slope)
+    grad_term = contract_cols(jnp.concatenate([gate_grad, up_grad], axis=1), gate_up_cols)
     terms = jnp.concatenate([out_term, grad_term.astype(jnp.bfloat16)], axis=1)
 
     flat_route = routes.reshape(-1)
@@ -106,7 +102,6 @@
     )
     summed = jnp.sum(pieces.astype(jnp.float32), axis=0)
     expert_out = summed[:, :model_width].astype(jnp.bfloat16).astype(jnp.float32)
-    code_scale = weight_codes.astype(jnp.float32) / 256.0
     mixed = (code_scale[:, 0:1] * expert_out + code_scale[:, 1:2] * expert_out).astype(
         jnp.bfloat16
     )

time: 202 us -> 197 us (0.975)
  blocking collectives: 24.4 us -> 99 us
  waiting for transfers between devices: 106 us -> 36 us
  starting transfers between devices: 12.7 us -> 7.71 us
  local copies, waits for them, and re-layouts: 8.91 us -> 6.74 us
    all_to_all x0 -> x1, blocking collectives: none -> 74.6 us  [shards(): lax.all_to_all(copies, 'expert', split_axis=0, concat_axis=0, tiled=True)]
    all_to_all x1 -> x0, waiting for transfers between devices: 51 us -> none  [shards(): lax.all_to_all(copies, 'expert', split_axis=0, concat_axis=0, tiled=True)]
    all_gather x1, waiting for transfers between devices: 18.5 us -> 0.01 us  [shards(): plane = lax.all_gather(home, GROUP, axis=0, tiled=True)]
    all_to_all x1 -> x0, starting transfers between devices: 5.01 us -> none  [shards(): lax.all_to_all(copies, 'expert', split_axis=0, concat_axis=0, tiled=True)]
  transfers between devices with their start and end apart: 4 -> 3, of which waited for: 3 -> 1; matrix products, arithmetic and copies ran while one was open for 17% -> 15% of each run, Pallas kernels for 0% -> 0%
where the time goes in v12:
time: 197 us; the launch traced here: 196 us
  blocking collectives  99 us (50%)
  waiting for transfers between devices  36 us (18%)
  matrix products  23 us (12%)
  between operations  14.3 us (7%)
  other arithmetic  9.48 us (5%)
  starting transfers between devices  7.71 us (4%)
  local copies, waits for them, and re-layouts  6.74 us (3%)
    all_to_all x1, blocking collectives, shards(): lax.all_to_all(copies, 'expert', split_axis=0, concat_axis=0, tiled=True)  74.6 us
    all_to_all x1, waiting for transfers between devices, shards(): lax.all_to_all(pieces, GROUP, split_axis=0, concat_axis=0, tiled=True)  35.9 us
    all_to_all x1, blocking collectives, shards(): lax.all_to_all(send, 'expert', split_axis=0, concat_axis=0, tiled=True)  24.4 us
    dot_general x3, matrix products, contract_rows(): lax.dot_general(left_side, right_side, (((0,), (0,)), ((), ())), preferre...  8.69 us
    all_to_all x1, starting transfers between devices, shards(): lax.all_to_all(pieces, GROUP, split_axis=0, concat_axis=0, tiled=True)  7.63 us
    dot_general x2, matrix products, forward_parts(): gate_pre = jnp.dot(rows_x, gate_cols, preferred_element_type=jnp.float32)  5.18 us
    dot_general x2, matrix products, forward_parts(): up_pre = jnp.dot(rows_x, up_cols, preferred_element_type=jnp.float32)  4.25 us
  transfers between devices with their start and end apart: 3, of which 1 were waited for; matrix products, arithmetic and copies ran while one was open for 15% of the time, Pallas kernels for 0%

profile of v12, /device:TPU:32, one launch (start us, length us, event | category | flops | bytes accessed | tf_op | source)
XLA Modules:
  0.0 196.2 jit_solution(14175856794953404686)
XLA Ops:
  7.2 0.0 all-gather.3.cloned.1.call-start
  7.2 0.7 convert_multiply_fusion
  7.9 0.9 multiply_convert_fusion.13
  8.8 1.5 pad_maximum_fusion.3
  10.3 0.0 all-gather.3.cloned.1.call-update
  10.3 0.0 all-gather.5.cloned.1.call-start
  10.4 0.1 copy.15
  10.5 0.8 copy.14
  11.2 0.1 reshape.48
  11.3 0.1 div.19
  11.4 0.9 broadcast_in_dim.27
  12.4 0.2 convert_element_type.87
  12.6 0.9 broadcast_in_dim.26
  13.5 0.1 reshape.49
  13.5 0.1 fusion.54
  13.6 0.1 reduce_window_sum.11
  13.7 0.2 select_reduce_fusion
  13.9 0.2 convolution_convert_fusion.3
  14.0 0.0 copy-start
  14.0 0.0 copy-start.1
  14.1 0.0 copy-start.2
  14.1 0.2 convolution_convert_fusion.2
  14.3 0.1 all_to_all.16
  14.5 24.4 %all_to_all.22 = bf16[8,5,4096]{2,1,0:T(8,128)(2,1)S(1)} all-to-all(bf16[8,5,4096]{2,1,0:T(8,128)(2,1)S(1)} %all_to_all.16), channel_id=1, replica_groups=mesh['dp'=8,'expert'=8,'tensor'=4] {'expert'}, dimensions={0} | all-to-all | bytes 655360 | tf_op jit(solution)/shard_map/all_to_all | solution.py:88
  38.9 0.9 all_to_all.18
  39.8 0.0 all-gather.5.cloned.1.call-update
  39.9 0.2 broadcast_in_dim.12
  40.1 74.6 %all_to_all.23 = bf16[8,256,768]{2,1,0:T(8,128)(2,1)S(1)} all-to-all(bf16[8,256,768]{2,1,0:T(8,128)(2,1)S(1)} %broadcast_in_dim.12), channel_id=1, replica_groups=mesh['dp'=8,'expert'=8,'tensor'=4] {'expert'}, dimensions={0} | all-to-all | bytes 6291456 | tf_op jit(solution)/shard_map/all_to_all | solution.py:50
  114.7 2.7 %fusion.33 = f32[512,256]{0,1:T(8,128)S(1)} fusion(bf16[512,4096]{1,0:T(8,128)(2,1)} %all-gather.3.cloned.1.call-done, bf16[2048,768]{1,0:T(8,128)(2,1)S(1)} %bitcast.12), kind=kOutput, calls=%fused_computation.26 | convolution fusion | flops 536870912 | bytes 3670016 | tf_op jit(solution)/shard_map/dot_general | solution.py:28
  117.4 0.5 copy-done.4
  117.9 0.8 fusion.31
  118.6 1.0 multiply_convert_fusion.7
  119.6 0.8 convolution_convert_fusion
  120.4 1.3 convolution_convert_fusion.1
  121.7 2.5 %pad_maximum_fusion = bf16[512,4096]{1,0:T(8,128)(2,1)} fusion(bf16[512,2048]{1,0:T(8,128)(2,1)S(1)} %convolution_convert_fusion.1, bf16[512,2048]{1,0:T(8,128)(2,1)S(1)} %convolution_convert_fusion), kind=kLoop, calls=%fused_computation.4 | loop fusion | flops 8388608 | bytes 8388608 | tf_op jit(solution)/shard_map/concatenate | solution.py:69
  124.2 7.6 %all-to-all-start.1 = ((bf16[32,16,4096]{2,1,0:T(8,128)(2,1)}), bf16[32,16,4096]{2,1,0:T(8,128)(2,1)}, u32[]{:S(2)}, u32[]{:S(2)}) async-start(bf16[32,16,4096]{2,1,0:T(8,128)(2,1)} %bitcast.11), calls=%async_computation.1 | async-start | bytes 8388608 | tf_op jit(solution)/shard_map/all_to_all | solution.py:92
  131.8 0.0 all-gather.5.cloned.1.call-done
  131.9 4.2 %fusion.8 = f32[1280,256]{1,0:T(8,128)S(1)} fusion(bf16[1280,4096]{1,0:T(8,128)(2,1)} %all-gather.5.cloned.1.call-done, bf16[2048,768]{1,0:T(8,128)(2,1)S(1)} %bitcast.17), kind=kOutput, calls=%fused_computation.9 | convolution fusion | flops 1342177280 | bytes 7602176 | tf_op jit(solution)/shard_map/dot_general | solution.py:27
  136.1 1.3 copy-done.3
  137.4 1.6 fusion.10
  139.0 1.6 fusion.2
  140.5 2.9 %fusion.21 = bf16[1,2048,256]{2,1,0:T(8,128)(2,1)} fusion(bf16[1280,4096]{1,0:T(8,128)(2,1)S(1)} %copy-done.3, f32[1280,256]{1,0:T(8,128)S(1)} %fusion.10, f32[1280,256]{1,0:T(8,128)S(1)} %fusion.8), kind=kOutput, calls=%fused_computation.18 | convolution fusion | flops 1344667648 | bytes 8912896 | tf_op jit(solution)/shard_map/dot_general | solution.py:15
  143.4 2.9 %fusion.24 = bf16[1,2048,256]{2,1,0:T(8,128)(2,1)} fusion(bf16[1280,4096]{1,0:T(8,128)(2,1)S(1)} %copy-done.3, f32[1280,256]{1,0:T(8,128)S(1)} %fusion.2, f32[1280,256]{1,0:T(8,128)S(1)} %fusion.8), kind=kOutput, calls=%fused_computation.19 | convolution fusion | flops 1344667648 | bytes 8912896 | tf_op jit(solution)/shard_map/dot_general | solution.py:15
  146.2 3.0 %fusion.27 = bf16[1,2048,256]{2,1,0:T(8,128)(2,1)} fusion(bf16[1280,4096]{1,0:T(8,128)(2,1)S(1)} %copy-done.3, f32[1280,256]{1,0:T(8,128)S(1)} %fusion.8, f32[1280,256]{1,0:T(8,128)S(1)} %fusion.2, f32[1280,256]{1,0:T(8,128)S(1)} %fusion.10), kind=kOutput, calls=%fused_computation.20 | convolution fusion | flops 1345978368 | bytes 10223616 | tf_op jit(solution)/shard_map/dot_general | solution.py:15
  149.2 35.9 %all-to-all-done.1 = bf16[32,16,4096]{2,1,0:T(8,128)(2,1)} async-done(((bf16[32,16,4096]{2,1,0:T(8,128)(2,1)}), bf16[32,16,4096]{2,1,0:T(8,128)(2,1)}, u32[]{:S(2)}, u32[]{:S(2)}) %all-to-all-start.1) | async-done | bytes 4194336 | tf_op jit(solution)/shard_map/all_to_all | solution.py:92
  185.1 2.8 %reduce = bf16[16,4096]{1,0:T(8,128)(2,1)S(1)} reduce(bf16[32,16,4096]{2,1,0:T(8,128)(2,1)} %all-to-all-done.1, bf16[]{:T(256)} %constant.22), dimensions={0}, to_apply=%region_2.3.clone | reduce | flops 2031616 | bytes 4325378 | tf_op jit(solution)/shard_map/reduce_sum | solution.py:103
  188.0 0.7 multiply_convert_fusion.12
  188.7 0.6 slice.61
  (10 shorter events, 0.1 us)
Async XLA Ops:
  7.2 107.5 %all-gather.3.cloned.1.call-start = ((), (), s32[]{:S(2)}) async-start(), calls=%async_computation.3 | async-start | bytes 4325376 | tf_op jit(solution)/shard_map/all_gather | solution.py:61
  10.3 121.5 %all-gather.5.cloned.1.call-start = ((), (), s32[]{:S(2)}) async-start(), calls=%async_computation.4 | async-start | bytes 10813440 | tf_op jit(solution)/shard_map/all_gather | solution.py:89
  14.0 25.8 %copy-start = (bf16[256,256]{1,0:T(8,128)(2,1)S(1)}, bf16[256,256]{1,0:T(8,128)(2,1)}, u32[]{:S(2)}) copy-start(bf16[256,256]{1,0:T(8,128)(2,1)} %param.13) | copy-start | bytes 393220
  14.0 25.8 %copy-start.1 = (bf16[256,256]{1,0:T(8,128)(2,1)S(1)}, bf16[256,256]{1,0:T(8,128)(2,1)}, u32[]{:S(2)}) copy-start(bf16[256,256]{1,0:T(8,128)(2,1)} %param.12) | copy-start | bytes 393220
  14.1 25.8 %copy-start.2 = (bf16[256,256]{1,0:T(8,128)(2,1)S(1)}, bf16[256,256]{1,0:T(8,128)(2,1)}, u32[]{:S(2)}) copy-start(bf16[256,256]{1,0:T(8,128)(2,1)} %param.11) | copy-start | bytes 393220
  114.7 3.2 %copy-start.4 = (bf16[512,4096]{1,0:T(8,128)(2,1)S(1)}, bf16[512,4096]{1,0:T(8,128)(2,1)}, u32[]{:S(2)}) copy-start(bf16[512,4096]{1,0:T(8,128)(2,1)} %all-gather.3.cloned.1.call-done) | copy-start | bytes 12582916
  124.2 60.9 %all-to-all-start.1 = ((bf16[32,16,4096]{2,1,0:T(8,128)(2,1)}), bf16[32,16,4096]{2,1,0:T(8,128)(2,1)}, u32[]{:S(2)}, u32[]{:S(2)}) async-start(bf16[32,16,4096]{2,1,0:T(8,128)(2,1)} %bitcast.11), calls=%async_computation.1 | async-start | bytes 8388608 | tf_op jit(solution)/shard_map/all_to_all | solution.py:92
  131.9 5.5 %copy-start.3 = (bf16[1280,4096]{1,0:T(8,128)(2,1)S(1)}, bf16[1280,4096]{1,0:T(8,128)(2,1)}, u32[]{:S(2)}) copy-start(bf16[1280,4096]{1,0:T(8,128)(2,1)} %all-gather.5.cloned.1.call-done) | copy-start | bytes 31457284
Sparse Core Ops, SparseCore 0:
  11.1 53.6 all-gather.2
  68.0 62.2 all-gather.4

commit v13 on v12

--- a/solution.py
+++ b/solution.py
@@ -4,6 +4,7 @@
 from jax.sharding import PartitionSpec as P
 
 GROUP = ("dp", "tensor")
+PLANE = ("tensor", "dp")
 
 
 def silu_parts(gate_pre):
@@ -58,7 +59,7 @@
     pair_scale = code_scale[:, 0:1] + code_scale[:, 1:2]
     pair_scaled = (pair_scale * cotangent.astype(jnp.float32)).astype(jnp.bfloat16)
     home = jnp.concatenate([tokens, pair_scaled], axis=1)
-    plane = lax.all_gather(home, GROUP, axis=0, tiled=True)
+    plane = lax.all_gather(home, PLANE, axis=0, tiled=True)
     plane_x = plane[:, :model_width]
     plane_s = plane[:, model_width:]
 
@@ -89,7 +90,7 @@
     rows = lax.all_gather(got, GROUP, axis=0, tiled=True)
     n_group = terms.shape[0] // count_tok
     pieces = terms.reshape(n_group, count_tok, 2 * model_width)
-    pieces = lax.all_to_all(pieces, GROUP, split_axis=0, concat_axis=0, tiled=True)
+    pieces = lax.all_to_all(pieces, PLANE, split_axis=0, concat_axis=0, tiled=True)
     rows_x = rows[:, :model_width]
     rows_s = rows[:, model_width:]
     r_up, r_act, r_slope, r_hidden = forward_parts(rows_x, gate_cols, up_cols)

time: 197 us -> 238 us (1.21); the launches traced: 196 us -> 234 us
  waiting for transfers between devices: 36 us -> 73.9 us
    all_gather x1, waiting for transfers between devices: 0.02 us -> 73.8 us  [shards(): rows = lax.all_gather(got, GROUP, axis=0, tiled=True)]
    all_to_all x1, waiting for transfers between devices: 35.9 us -> 0.01 us  [shards(): lax.all_to_all(pieces, PLANE, split_axis=0, concat_axis=0, tiled=True)]
  transfers between devices with their start and end apart: 3 -> 3, of which waited for: 1 -> 1; matrix products, arithmetic and copies ran while one was open for 15% -> 12% of each run, Pallas kernels for 0% -> 0%
where the time goes in v13:
time: 238 us; the launch traced here: 234 us
  blocking collectives  99 us (42%)
  waiting for transfers between devices  73.9 us (31%)
  matrix products  22.8 us (10%)
  between operations  14.2 us (6%)
  other arithmetic  9.48 us (4%)
  starting transfers between devices  7.72 us (3%)
  local copies, waits for them, and re-layouts  6.59 us (3%)
    all_to_all x1, blocking collectives, shards(): lax.all_to_all(copies, 'expert', split_axis=0, concat_axis=0, tiled=True)  74.6 us
    all_gather x1, waiting for transfers between devices, shards(): rows = lax.all_gather(got, GROUP, axis=0, tiled=True)  73.8 us
    all_to_all x1, blocking collectives, shards(): lax.all_to_all(send, 'expert', split_axis=0, concat_axis=0, tiled=True)  24.4 us
    dot_general x3, matrix products, contract_rows(): lax.dot_general(left_side, right_side, (((0,), (0,)), ((), ())), preferre...  8.68 us
    all_to_all x1, starting transfers between devices, shards(): lax.all_to_all(pieces, PLANE, split_axis=0, concat_axis=0, tiled=True)  7.64 us
    dot_general x2, matrix products, forward_parts(): gate_pre = jnp.dot(rows_x, gate_cols, preferred_element_type=jnp.float32)  5.18 us
  transfers between devices with their start and end apart: 3, of which 1 were waited for; matrix products, arithmetic and copies ran while one was open for 12% of the time, Pallas kernels for 0%

profile of v13, /device:TPU:32, one launch (start us, length us, event | category | flops | bytes accessed | tf_op | source)
XLA Modules:
  0.0 233.7 jit_solution(5448454466388891474)
XLA Ops:
  7.2 0.0 all-gather.3.cloned.1.call-start
  7.2 0.7 convert_multiply_fusion
  7.9 0.9 multiply_convert_fusion.13
  8.8 1.5 pad_maximum_fusion.3
  10.3 0.0 all-gather.3.cloned.1.call-update
  10.3 0.0 all-gather.5.cloned.1.call-start
  10.4 0.1 copy.15
  10.5 0.8 copy.14
  11.2 0.1 reshape.48
  11.3 0.1 div.19
  11.4 0.9 broadcast_in_dim.27
  12.4 0.2 convert_element_type.87
  12.6 0.9 broadcast_in_dim.26
  13.5 0.1 reshape.49
  13.5 0.1 fusion.54
  13.6 0.1 reduce_window_sum.11
  13.7 0.2 select_reduce_fusion
  13.9 0.2 convolution_convert_fusion.3
  14.0 0.0 copy-start
  14.0 0.0 copy-start.1
  14.1 0.0 copy-start.2
  14.1 0.2 convolution_convert_fusion.2
  14.3 0.1 all_to_all.16
  14.5 24.4 %all_to_all.22 = bf16[8,5,4096]{2,1,0:T(8,128)(2,1)S(1)} all-to-all(bf16[8,5,4096]{2,1,0:T(8,128)(2,1)S(1)} %all_to_all.16), channel_id=1, replica_groups=mesh['dp'=8,'expert'=8,'tensor'=4] {'expert'}, dimensions={0} | all-to-all | bytes 655360 | tf_op jit(solution)/shard_map/all_to_all | solution.py:89
  38.9 0.9 all_to_all.18
  39.8 0.0 all-gather.5.cloned.1.call-update
  39.9 0.2 broadcast_in_dim.12
  40.1 74.6 %all_to_all.23 = bf16[8,256,768]{2,1,0:T(8,128)(2,1)S(1)} all-to-all(bf16[8,256,768]{2,1,0:T(8,128)(2,1)S(1)} %broadcast_in_dim.12), channel_id=1, replica_groups=mesh['dp'=8,'expert'=8,'tensor'=4] {'expert'}, dimensions={0} | all-to-all | bytes 6291456 | tf_op jit(solution)/shard_map/all_to_all | solution.py:51
  114.7 2.5 %fusion.33 = f32[512,256]{0,1:T(8,128)S(1)} fusion(bf16[512,4096]{1,0:T(8,128)(2,1)} %all-gather.3.cloned.1.call-done, bf16[2048,768]{1,0:T(8,128)(2,1)S(1)} %bitcast.12), kind=kOutput, calls=%fused_computation.26 | convolution fusion | flops 536870912 | bytes 3670016 | tf_op jit(solution)/shard_map/dot_general | solution.py:29
  117.2 0.3 copy-done.4
  117.5 0.8 fusion.31
  118.3 1.0 multiply_convert_fusion.7
  119.3 0.8 convolution_convert_fusion
  120.1 1.3 convolution_convert_fusion.1
  121.4 2.5 %pad_maximum_fusion = bf16[512,4096]{1,0:T(8,128)(2,1)} fusion(bf16[512,2048]{1,0:T(8,128)(2,1)S(1)} %convolution_convert_fusion.1, bf16[512,2048]{1,0:T(8,128)(2,1)S(1)} %convolution_convert_fusion), kind=kLoop, calls=%fused_computation.4 | loop fusion | flops 8388608 | bytes 8388608 | tf_op jit(solution)/shard_map/concatenate | solution.py:70
  123.8 7.6 %all-to-all-start.1 = ((bf16[32,16,4096]{2,1,0:T(8,128)(2,1)}), bf16[32,16,4096]{2,1,0:T(8,128)(2,1)}, u32[]{:S(2)}, u32[]{:S(2)}) async-start(bf16[32,16,4096]{2,1,0:T(8,128)(2,1)} %bitcast.11), calls=%async_computation.1 | async-start | bytes 8388608 | tf_op jit(solution)/shard_map/all_to_all | solution.py:93
  131.5 73.8 %all-gather.5.cloned.1.call-done = bf16[1280,4096]{1,0:T(8,128)(2,1)} async-done(((bf16[40,4096]{1,0:T(8,128)(2,1)}), bf16[1280,4096]{1,0:T(8,128)(2,1)}) %all-gather.5.cloned.1.call-update) | async-done | bytes 10485776 | tf_op jit(solution)/shard_map/all_gather | solution.py:90
  205.3 4.2 %fusion.8 = f32[1280,256]{1,0:T(8,128)S(1)} fusion(bf16[1280,4096]{1,0:T(8,128)(2,1)} %all-gather.5.cloned.1.call-done, bf16[2048,768]{1,0:T(8,128)(2,1)S(1)} %bitcast.17), kind=kOutput, calls=%fused_computation.9 | convolution fusion | flops 1342177280 | bytes 7602176 | tf_op jit(solution)/shard_map/dot_general | solution.py:28
  209.5 1.3 copy-done.3
  210.9 1.6 fusion.10
  212.4 1.6 fusion.2
  214.0 2.9 %fusion.21 = bf16[1,2048,256]{2,1,0:T(8,128)(2,1)} fusion(bf16[1280,4096]{1,0:T(8,128)(2,1)S(1)} %copy-done.3, f32[1280,256]{1,0:T(8,128)S(1)} %fusion.10, f32[1280,256]{1,0:T(8,128)S(1)} %fusion.8), kind=kOutput, calls=%fused_computation.18 | convolution fusion | flops 1344667648 | bytes 8912896 | tf_op jit(solution)/shard_map/dot_general | solution.py:16
  216.8 2.9 %fusion.24 = bf16[1,2048,256]{2,1,0:T(8,128)(2,1)} fusion(bf16[1280,4096]{1,0:T(8,128)(2,1)S(1)} %copy-done.3, f32[1280,256]{1,0:T(8,128)S(1)} %fusion.2, f32[1280,256]{1,0:T(8,128)S(1)} %fusion.8), kind=kOutput, calls=%fused_computation.19 | convolution fusion | flops 1344667648 | bytes 8912896 | tf_op jit(solution)/shard_map/dot_general | solution.py:16
  219.7 3.0 %fusion.27 = bf16[1,2048,256]{2,1,0:T(8,128)(2,1)} fusion(bf16[1280,4096]{1,0:T(8,128)(2,1)S(1)} %copy-done.3, f32[1280,256]{1,0:T(8,128)S(1)} %fusion.8, f32[1280,256]{1,0:T(8,128)S(1)} %fusion.2, f32[1280,256]{1,0:T(8,128)S(1)} %fusion.10), kind=kOutput, calls=%fused_computation.20 | convolution fusion | flops 1345978368 | bytes 10223616 | tf_op jit(solution)/shard_map/dot_general | solution.py:16
  222.7 0.0 all-to-all-done.1
  222.7 2.8 %reduce = bf16[16,4096]{1,0:T(8,128)(2,1)S(1)} reduce(bf16[32,16,4096]{2,1,0:T(8,128)(2,1)} %all-to-all-done.1, bf16[]{:T(256)} %constant.22), dimensions={0}, to_apply=%region_2.3.clone | reduce | flops 2031616 | bytes 4325378 | tf_op jit(solution)/shard_map/reduce_sum | solution.py:104
  225.5 0.7 multiply_convert_fusion.12
  226.2 0.6 slice.61
  (10 shorter events, 0.1 us)
Async XLA Ops:
  7.2 107.5 %all-gather.3.cloned.1.call-start = ((), (), s32[]{:S(2)}) async-start(), calls=%async_computation.3 | async-start | bytes 4325376 | tf_op jit(solution)/shard_map/all_gather | solution.py:62
  10.3 195.0 %all-gather.5.cloned.1.call-start = ((), (), s32[]{:S(2)}) async-start(), calls=%async_computation.4 | async-start | bytes 10813440 | tf_op jit(solution)/shard_map/all_gather | solution.py:90
  14.0 25.8 %copy-start = (bf16[256,256]{1,0:T(8,128)(2,1)S(1)}, bf16[256,256]{1,0:T(8,128)(2,1)}, u32[]{:S(2)}) copy-start(bf16[256,256]{1,0:T(8,128)(2,1)} %param.13) | copy-start | bytes 393220
  14.0 25.8 %copy-start.1 = (bf16[256,256]{1,0:T(8,128)(2,1)S(1)}, bf16[256,256]{1,0:T(8,128)(2,1)}, u32[]{:S(2)}) copy-start(bf16[256,256]{1,0:T(8,128)(2,1)} %param.12) | copy-start | bytes 393220
  14.1 25.8 %copy-start.2 = (bf16[256,256]{1,0:T(8,128)(2,1)S(1)}, bf16[256,256]{1,0:T(8,128)(2,1)}, u32[]{:S(2)}) copy-start(bf16[256,256]{1,0:T(8,128)(2,1)} %param.11) | copy-start | bytes 393220
  114.7 2.8 %copy-start.4 = (bf16[512,4096]{1,0:T(8,128)(2,1)S(1)}, bf16[512,4096]{1,0:T(8,128)(2,1)}, u32[]{:S(2)}) copy-start(bf16[512,4096]{1,0:T(8,128)(2,1)} %all-gather.3.cloned.1.call-done) | copy-start | bytes 12582916
  123.8 98.8 %all-to-all-start.1 = ((bf16[32,16,4096]{2,1,0:T(8,128)(2,1)}), bf16[32,16,4096]{2,1,0:T(8,128)(2,1)}, u32[]{:S(2)}, u32[]{:S(2)}) async-start(bf16[32,16,4096]{2,1,0:T(8,128)(2,1)} %bitcast.11), calls=%async_computation.1 | async-start | bytes 8388608 | tf_op jit(solution)/shard_map/all_to_all | solution.py:93
  205.3 5.5 %copy-start.3 = (bf16[1280,4096]{1,0:T(8,128)(2,1)S(1)}, bf16[1280,4096]{1,0:T(8,128)(2,1)}, u32[]{:S(2)}) copy-start(bf16[1280,4096]{1,0:T(8,128)(2,1)} %all-gather.5.cloned.1.call-done) | copy-start | bytes 31457284
Sparse Core Ops, SparseCore 0:
  10.5 91.4 all-gather.2
  105.1 100.2 all-gather.4

commit v14 on v12

--- a/solution.py
+++ b/solution.py
@@ -23,9 +23,11 @@
     )
 
 
-def forward_parts(rows_x, gate_cols, up_cols):
-    gate_pre = jnp.dot(rows_x, gate_cols, preferred_element_type=jnp.float32)
-    up_pre = jnp.dot(rows_x, up_cols, preferred_element_type=jnp.float32)
+def forward_parts(rows_x, gate_up_cols):
+    both = jnp.dot(rows_x, gate_up_cols, preferred_element_type=jnp.float32)
+    hid = gate_up_cols.shape[1] // 2
+    gate_pre = both[:, :hid]
+    up_pre = both[:, hid:]
     activation, act_slope = silu_parts(gate_pre)
     hidden = (activation * up_pre).astype(jnp.bfloat16)
     return up_pre, activation, act_slope, hidden
@@ -62,7 +64,7 @@
     plane_x = plane[:, :model_width]
     plane_s = plane[:, model_width:]
 
-    up_pre, activation, act_slope, hidden = forward_parts(plane_x, gate_cols, up_cols)
+    up_pre, activation, act_slope, hidden = forward_parts(plane_x, gate_up_cols)
     out_term = contract_cols(hidden, down_cols).astype(jnp.bfloat16)
     gate_grad, up_grad = grad_parts(plane_s, down_cols, up_pre, activation, act_slope)
     grad_term = contract_cols(jnp.concatenate([gate_grad, up_grad], axis=1), gate_up_cols)
@@ -92,7 +94,7 @@
     pieces = lax.all_to_all(pieces, GROUP, split_axis=0, concat_axis=0, tiled=True)
     rows_x = rows[:, :model_width]
     rows_s = rows[:, model_width:]
-    r_up, r_act, r_slope, r_hidden = forward_parts(rows_x, gate_cols, up_cols)
+    r_up, r_act, r_slope, r_hidden = forward_parts(rows_x, gate_up_cols)
     r_gate, r_upg = grad_parts(rows_s, down_cols, r_up, r_act, r_slope)
     grad_gate = contract_rows(rows_x, r_gate).astype(jnp.bfloat16)[None]
     grad_up = contract_rows(rows_x, r_upg).astype(jnp.bfloat16)[None]

time: 197 us -> 197 us (level)
    dot_general x4 -> x2, matrix products: 9.43 us -> 5.95 us  [forward_parts(): both = jnp.dot(rows_x, gate_up_cols, preferred_element_type=jnp.float32)]
    dot_general x2, matrix products: 2.32 us -> 5.12 us  [grad_parts(): hidden_grad = jnp.dot(scaled, down_cols, preferred_element_type=jnp.float32)]
  transfers between devices with their start and end apart: 3 -> 3, of which waited for: 1 -> 1; matrix products, arithmetic and copies ran while one was open for 15% -> 14% of each run, Pallas kernels for 0% -> 0%
where the time goes in v14:
time: 197 us
  blocking collectives  99 us (50%)
  waiting for transfers between devices  36.2 us (18%)
  matrix products  22.3 us (11%)
  between operations  14.2 us (7%)
  other arithmetic  9.48 us (5%)
  local copies, waits for them, and re-layouts  7.91 us (4%)
  starting transfers between devices  7.69 us (4%)
    all_to_all x1, blocking collectives, shards(): lax.all_to_all(copies, 'expert', split_axis=0, concat_axis=0, tiled=True)  74.6 us
    all_to_all x1, waiting for transfers between devices, shards(): lax.all_to_all(pieces, GROUP, split_axis=0, concat_axis=0, tiled=True)  36.1 us
    all_to_all x1, blocking collectives, shards(): lax.all_to_all(send, 'expert', split_axis=0, concat_axis=0, tiled=True)  24.4 us
    dot_general x3, matrix products, contract_rows(): lax.dot_general(left_side, right_side, (((0,), (0,)), ((), ())), preferre...  8.71 us
    all_to_all x1, starting transfers between devices, shards(): lax.all_to_all(pieces, GROUP, split_axis=0, concat_axis=0, tiled=True)  7.61 us
    dot_general x2, matrix products, forward_parts(): both = jnp.dot(rows_x, gate_up_cols, preferred_element_type=jnp.float32)  5.95 us
    dot_general x2, matrix products, grad_parts(): hidden_grad = jnp.dot(scaled, down_cols, preferred_element_type=jnp.float32)  5.12 us
  transfers between devices with their start and end apart: 3, of which 1 were waited for; matrix products, arithmetic and copies ran while one was open for 14% of the time, Pallas kernels for 0%

profile of v14, /device:TPU:32, one launch (start us, length us, event | category | flops | bytes accessed | tf_op | source)
XLA Modules:
  0.0 196.9 jit_solution(15824161374165336555)
XLA Ops:
  7.2 0.0 all-gather.3.cloned.1.call-start
  7.2 0.7 convert_multiply_fusion
  7.9 0.9 multiply_convert_fusion.13
  8.8 1.5 pad_maximum_fusion.3
  10.3 0.0 all-gather.3.cloned.1.call-update
  10.3 0.0 all-gather.5.cloned.1.call-start
  10.4 0.1 copy.15
  10.5 0.9 broadcast_in_dim.27
  11.4 0.2 convert_element_type.87
  11.6 0.0 copy-start
  11.6 0.0 copy-start.1
  11.6 0.0 copy-start.2
  11.7 0.1 div.19
  11.7 0.8 copy.14
  12.6 0.1 reshape.48
  12.7 0.9 broadcast_in_dim.26
  13.6 0.1 reshape.49
  13.6 0.1 fusion.48
  13.7 0.1 reduce_window_sum.11
  13.8 0.2 select_reduce_fusion
  13.9 0.2 convolution_convert_fusion.3
  14.1 0.2 convolution_convert_fusion.2
  14.4 0.1 all_to_all.16
  14.6 24.4 %all_to_all.22 = bf16[8,5,4096]{2,1,0:T(8,128)(2,1)S(1)} all-to-all(bf16[8,5,4096]{2,1,0:T(8,128)(2,1)S(1)} %all_to_all.16), channel_id=1, replica_groups=mesh['dp'=8,'expert'=8,'tensor'=4] {'expert'}, dimensions={0} | all-to-all | bytes 655360 | tf_op jit(solution)/shard_map/all_to_all | solution.py:90
  39.0 0.9 all_to_all.18
  39.8 0.0 all-gather.5.cloned.1.call-update
  39.9 0.0 copy-done
  39.9 0.0 copy-done.1
  39.9 0.2 broadcast_in_dim.12
  40.1 74.6 %all_to_all.23 = bf16[8,256,768]{2,1,0:T(8,128)(2,1)S(1)} all-to-all(bf16[8,256,768]{2,1,0:T(8,128)(2,1)S(1)} %broadcast_in_dim.12), channel_id=1, replica_groups=mesh['dp'=8,'expert'=8,'tensor'=4] {'expert'}, dimensions={0} | all-to-all | bytes 6291456 | tf_op jit(solution)/shard_map/all_to_all | solution.py:52
  114.8 3.1 %fusion.30 = f32[512,512]{0,1:T(8,128)S(1)} fusion(bf16[512,4096]{1,0:T(8,128)(2,1)} %all-gather.3.cloned.1.call-done, bf16[2048,768]{1,0:T(8,128)(2,1)S(1)} %bitcast.12), kind=kOutput, calls=%fused_computation.23 | convolution fusion | flops 1073741824 | bytes 5242880 | tf_op jit(solution)/shard_map/dot_general | solution.py:27
  117.9 0.8 convolution_convert_fusion
  118.7 1.6 copy-done.4
  120.2 0.9 multiply_convert_fusion.7
  121.2 1.3 convolution_convert_fusion.1
  122.5 2.5 %pad_maximum_fusion = bf16[512,4096]{1,0:T(8,128)(2,1)} fusion(bf16[512,2048]{1,0:T(8,128)(2,1)S(1)} %convolution_convert_fusion.1, bf16[512,2048]{1,0:T(8,128)(2,1)S(1)} %convolution_convert_fusion), kind=kLoop, calls=%fused_computation.4 | loop fusion | flops 8388608 | bytes 8388608 | tf_op jit(solution)/shard_map/concatenate | solution.py:71
  124.9 7.6 %all-to-all-start.1 = ((bf16[32,16,4096]{2,1,0:T(8,128)(2,1)}), bf16[32,16,4096]{2,1,0:T(8,128)(2,1)}, u32[]{:S(2)}, u32[]{:S(2)}) async-start(bf16[32,16,4096]{2,1,0:T(8,128)(2,1)} %bitcast.11), calls=%async_computation.1 | async-start | bytes 8388608 | tf_op jit(solution)/shard_map/all_to_all | solution.py:94
  132.5 0.0 all-gather.5.cloned.1.call-done
  132.6 4.2 %fusion.2 = f32[1280,256]{1,0:T(8,128)S(1)} fusion(bf16[1280,4096]{1,0:T(8,128)(2,1)} %all-gather.5.cloned.1.call-done, bf16[2048,768]{1,0:T(8,128)(2,1)S(1)} %bitcast.16), kind=kOutput, calls=%fused_computation.2 | convolution fusion | flops 1342177280 | bytes 7602176 | tf_op jit(solution)/shard_map/dot_general | solution.py:37
  136.8 1.3 copy-done.3
  138.1 2.9 %fusion.8 = f32[1280,512]{1,0:T(8,128)S(1)} fusion(bf16[1280,4096]{1,0:T(8,128)(2,1)S(1)} %copy-done.3, bf16[2048,768]{1,0:T(8,128)(2,1)S(1)} %bitcast.17), kind=kOutput, calls=%fused_computation.9 | convolution fusion | flops 2684354560 | bytes 9961472 | tf_op jit(solution)/shard_map/dot_general | solution.py:27
  141.0 2.9 %fusion.19 = bf16[1,2048,256]{2,1,0:T(8,128)(2,1)} fusion(bf16[1280,4096]{1,0:T(8,128)(2,1)S(1)} %copy-done.3, f32[1280,512]{1,0:T(8,128)S(1)} %fusion.8), kind=kOutput, calls=%fused_computation.16 | convolution fusion | flops 1344667648 | bytes 8912896 | tf_op jit(solution)/shard_map/dot_general | solution.py:15
  143.8 2.9 %fusion.22 = bf16[1,2048,256]{2,1,0:T(8,128)(2,1)} fusion(bf16[1280,4096]{1,0:T(8,128)(2,1)S(1)} %copy-done.3, f32[1280,256]{1,0:T(8,128)S(1)} %fusion.2, f32[1280,512]{1,0:T(8,128)S(1)} %fusion.8), kind=kOutput, calls=%fused_computation.17 | convolution fusion | flops 1344667648 | bytes 8912896 | tf_op jit(solution)/shard_map/dot_general | solution.py:15
  146.7 3.0 %fusion.25 = bf16[1,2048,256]{2,1,0:T(8,128)(2,1)} fusion(bf16[1280,4096]{1,0:T(8,128)(2,1)S(1)} %copy-done.3, f32[1280,256]{1,0:T(8,128)S(1)} %fusion.2, f32[1280,512]{1,0:T(8,128)S(1)} %fusion.8), kind=kOutput, calls=%fused_computation.18 | convolution fusion | flops 1345978368 | bytes 10223616 | tf_op jit(solution)/shard_map/dot_general | solution.py:15
  149.7 36.1 %all-to-all-done.1 = bf16[32,16,4096]{2,1,0:T(8,128)(2,1)} async-done(((bf16[32,16,4096]{2,1,0:T(8,128)(2,1)}), bf16[32,16,4096]{2,1,0:T(8,128)(2,1)}, u32[]{:S(2)}, u32[]{:S(2)}) %all-to-all-start.1) | async-done | bytes 4194336 | tf_op jit(solution)/shard_map/all_to_all | solution.py:94
  185.8 2.8 %reduce = bf16[16,4096]{1,0:T(8,128)(2,1)S(1)} reduce(bf16[32,16,4096]{2,1,0:T(8,128)(2,1)} %all-to-all-done.1, bf16[]{:T(256)} %constant.22), dimensions={0}, to_apply=%region_2.3.clone | reduce | flops 2031616 | bytes 4325378 | tf_op jit(solution)/shard_map/reduce_sum | solution.py:105
  188.7 0.7 multiply_convert_fusion.12
  189.4 0.6 slice.71
  (8 shorter events, 0.1 us)
Async XLA Ops:
  7.2 107.6 %all-gather.3.cloned.1.call-start = ((), (), s32[]{:S(2)}) async-start(), calls=%async_computation.3 | async-start | bytes 4325376 | tf_op jit(solution)/shard_map/all_gather | solution.py:63
  10.3 122.2 %all-gather.5.cloned.1.call-start = ((), (), s32[]{:S(2)}) async-start(), calls=%async_computation.4 | async-start | bytes 10813440 | tf_op jit(solution)/shard_map/all_gather | solution.py:91
  11.6 28.2 %copy-start = (bf16[256,256]{1,0:T(8,128)(2,1)S(1)}, bf16[256,256]{1,0:T(8,128)(2,1)}, u32[]{:S(2)}) copy-start(bf16[256,256]{1,0:T(8,128)(2,1)} %param.13) | copy-start | bytes 393220
  11.6 28.2 %copy-start.1 = (bf16[256,256]{1,0:T(8,128)(2,1)S(1)}, bf16[256,256]{1,0:T(8,128)(2,1)}, u32[]{:S(2)}) copy-start(bf16[256,256]{1,0:T(8,128)(2,1)} %param.12) | copy-start | bytes 393220
  11.6 28.2 %copy-start.2 = (bf16[256,256]{1,0:T(8,128)(2,1)S(1)}, bf16[256,256]{1,0:T(8,128)(2,1)}, u32[]{:S(2)}) copy-start(bf16[256,256]{1,0:T(8,128)(2,1)} %param.11) | copy-start | bytes 393220
  117.8 2.4 %copy-start.4 = (bf16[512,4096]{1,0:T(8,128)(2,1)S(1)}, bf16[512,4096]{1,0:T(8,128)(2,1)}, u32[]{:S(2)}) copy-start(bf16[512,4096]{1,0:T(8,128)(2,1)} %all-gather.3.cloned.1.call-done) | copy-start | bytes 12582916
  124.9 60.9 %all-to-all-start.1 = ((bf16[32,16,4096]{2,1,0:T(8,128)(2,1)}), bf16[32,16,4096]{2,1,0:T(8,128)(2,1)}, u32[]{:S(2)}, u32[]{:S(2)}) async-start(bf16[32,16,4096]{2,1,0:T(8,128)(2,1)} %bitcast.11), calls=%async_computation.1 | async-start | bytes 8388608 | tf_op jit(solution)/shard_map/all_to_all | solution.py:94
  132.6 5.5 %copy-start.3 = (bf16[1280,4096]{1,0:T(8,128)(2,1)S(1)}, bf16[1280,4096]{1,0:T(8,128)(2,1)}, u32[]{:S(2)}) copy-start(bf16[1280,4096]{1,0:T(8,128)(2,1)} %all-gather.5.cloned.1.call-done) | copy-start | bytes 31457284
Sparse Core Ops, SparseCore 0:
  11.1 53.6 all-gather.2
  68.0 62.2 all-gather.4

commit v15 on v12

--- a/solution.py
+++ b/solution.py
@@ -100,12 +100,14 @@
     pieces, grad_gate, grad_up, grad_down_t = lax.optimization_barrier(
         (pieces, grad_gate, grad_up, grad_down_t)
     )
-    summed = jnp.sum(pieces.astype(jnp.float32), axis=0)
-    expert_out = summed[:, :model_width].astype(jnp.bfloat16).astype(jnp.float32)
+    expert_out = jnp.sum(pieces[:, :, :model_width].astype(jnp.float32), axis=0)
+    expert_out = expert_out.astype(jnp.bfloat16).astype(jnp.float32)
     mixed = (code_scale[:, 0:1] * expert_out + code_scale[:, 1:2] * expert_out).astype(
         jnp.bfloat16
     )
-    input_grad = summed[:, model_width:].astype(jnp.bfloat16)
+    input_grad = jnp.sum(pieces[:, :, model_width:].astype(jnp.float32), axis=0).astype(
+        jnp.bfloat16
+    )
     return (mixed, input_grad, grad_gate, grad_up, grad_down_t)
 
 

time: 197 us -> 197 us (level)
  no operation moved by 1% of the time
where the time goes in v15:
time: 197 us; the launch traced here: 196 us
  blocking collectives  99 us (50%)
  waiting for transfers between devices  36 us (18%)
  matrix products  23 us (12%)
  between operations  14.2 us (7%)
  other arithmetic  10.1 us (5%)
  starting transfers between devices  7.71 us (4%)
  local copies, waits for them, and re-layouts  6.11 us (3%)
    all_to_all x1, blocking collectives, shards(): lax.all_to_all(copies, 'expert', split_axis=0, concat_axis=0, tiled=True)  74.6 us
    all_to_all x1, waiting for transfers between devices, shards(): lax.all_to_all(pieces, GROUP, split_axis=0, concat_axis=0, tiled=True)  35.9 us
    all_to_all x1, blocking collectives, shards(): lax.all_to_all(send, 'expert', split_axis=0, concat_axis=0, tiled=True)  24.4 us
    dot_general x3, matrix products, contract_rows(): lax.dot_general(left_side, right_side, (((0,), (0,)), ((), ())), preferre...  8.69 us
    all_to_all x1, starting transfers between devices, shards(): lax.all_to_all(pieces, GROUP, split_axis=0, concat_axis=0, tiled=True)  7.63 us
    dot_general x2, matrix products, forward_parts(): gate_pre = jnp.dot(rows_x, gate_cols, preferred_element_type=jnp.float32)  5.18 us
    dot_general x2, matrix products, forward_parts(): up_pre = jnp.dot(rows_x, up_cols, preferred_element_type=jnp.float32)  4.25 us
  transfers between devices with their start and end apart: 3, of which 1 were waited for; matrix products, arithmetic and copies ran while one was open for 15% of the time, Pallas kernels for 0%

profile of v15, /device:TPU:32, one launch (start us, length us, event | category | flops | bytes accessed | tf_op | source)
XLA Modules:
  0.0 196.1 jit_solution(10611862574934424487)
XLA Ops:
  7.2 0.0 all-gather.3.cloned.1.call-start
  7.2 0.7 convert_multiply_fusion
  7.9 0.9 multiply_convert_fusion.13
  8.8 1.5 pad_maximum_fusion.3
  10.3 0.0 all-gather.3.cloned.1.call-update
  10.3 0.0 all-gather.5.cloned.1.call-start
  10.4 0.1 copy.15
  10.5 0.8 copy.14
  11.2 0.1 reshape.48
  11.3 0.1 div.19
  11.4 0.9 broadcast_in_dim.27
  12.4 0.2 convert_element_type.86
  12.6 0.9 broadcast_in_dim.26
  13.5 0.1 reshape.49
  13.5 0.1 fusion.54
  13.6 0.1 reduce_window_sum.11
  13.7 0.2 select_reduce_fusion
  13.9 0.2 convolution_convert_fusion.3
  14.0 0.0 copy-start
  14.0 0.0 copy-start.1
  14.1 0.0 copy-start.2
  14.1 0.2 convolution_convert_fusion.2
  14.3 0.1 all_to_all.16
  14.5 24.4 %all_to_all.22 = bf16[8,5,4096]{2,1,0:T(8,128)(2,1)S(1)} all-to-all(bf16[8,5,4096]{2,1,0:T(8,128)(2,1)S(1)} %all_to_all.16), channel_id=1, replica_groups=mesh['dp'=8,'expert'=8,'tensor'=4] {'expert'}, dimensions={0} | all-to-all | bytes 655360 | tf_op jit(solution)/shard_map/all_to_all | solution.py:88
  38.9 0.9 all_to_all.18
  39.8 0.0 all-gather.5.cloned.1.call-update
  39.8 0.0 copy-done
  39.9 0.2 broadcast_in_dim.12
  40.1 74.6 %all_to_all.23 = bf16[8,256,768]{2,1,0:T(8,128)(2,1)S(1)} all-to-all(bf16[8,256,768]{2,1,0:T(8,128)(2,1)S(1)} %broadcast_in_dim.12), channel_id=1, replica_groups=mesh['dp'=8,'expert'=8,'tensor'=4] {'expert'}, dimensions={0} | all-to-all | bytes 6291456 | tf_op jit(solution)/shard_map/all_to_all | solution.py:50
  114.7 2.7 %fusion.33 = f32[512,256]{0,1:T(8,128)S(1)} fusion(bf16[512,4096]{1,0:T(8,128)(2,1)} %all-gather.3.cloned.1.call-done, bf16[2048,768]{1,0:T(8,128)(2,1)S(1)} %bitcast.12), kind=kOutput, calls=%fused_computation.28 | convolution fusion | flops 536870912 | bytes 3670016 | tf_op jit(solution)/shard_map/dot_general | solution.py:28
  117.4 0.5 copy-done.4
  117.9 0.8 fusion.31
  118.6 1.0 multiply_convert_fusion.7
  119.6 0.8 convolution_convert_fusion
  120.4 1.3 convolution_convert_fusion.1
  121.7 2.5 %pad_maximum_fusion = bf16[512,4096]{1,0:T(8,128)(2,1)} fusion(bf16[512,2048]{1,0:T(8,128)(2,1)S(1)} %convolution_convert_fusion.1, bf16[512,2048]{1,0:T(8,128)(2,1)S(1)} %convolution_convert_fusion), kind=kLoop, calls=%fused_computation.4 | loop fusion | flops 8388608 | bytes 8388608 | tf_op jit(solution)/shard_map/concatenate | solution.py:69
  124.2 7.6 %all-to-all-start.1 = ((bf16[32,16,4096]{2,1,0:T(8,128)(2,1)}), bf16[32,16,4096]{2,1,0:T(8,128)(2,1)}, u32[]{:S(2)}, u32[]{:S(2)}) async-start(bf16[32,16,4096]{2,1,0:T(8,128)(2,1)} %bitcast.11), calls=%async_computation.1 | async-start | bytes 8388608 | tf_op jit(solution)/shard_map/all_to_all | solution.py:92
  131.8 0.0 all-gather.5.cloned.1.call-done
  131.9 4.2 %fusion.8 = f32[1280,256]{1,0:T(8,128)S(1)} fusion(bf16[1280,4096]{1,0:T(8,128)(2,1)} %all-gather.5.cloned.1.call-done, bf16[2048,768]{1,0:T(8,128)(2,1)S(1)} %bitcast.17), kind=kOutput, calls=%fused_computation.9 | convolution fusion | flops 1342177280 | bytes 7602176 | tf_op jit(solution)/shard_map/dot_general | solution.py:27
  136.1 1.3 copy-done.3
  137.4 1.6 fusion.10
  138.9 1.6 fusion.2
  140.5 2.9 %fusion.21 = bf16[1,2048,256]{2,1,0:T(8,128)(2,1)} fusion(bf16[1280,4096]{1,0:T(8,128)(2,1)S(1)} %copy-done.3, f32[1280,256]{1,0:T(8,128)S(1)} %fusion.10, f32[1280,256]{1,0:T(8,128)S(1)} %fusion.8), kind=kOutput, calls=%fused_computation.18 | convolution fusion | flops 1344667648 | bytes 8912896 | tf_op jit(solution)/shard_map/dot_general | solution.py:15
  143.4 2.9 %fusion.24 = bf16[1,2048,256]{2,1,0:T(8,128)(2,1)} fusion(bf16[1280,4096]{1,0:T(8,128)(2,1)S(1)} %copy-done.3, f32[1280,256]{1,0:T(8,128)S(1)} %fusion.2, f32[1280,256]{1,0:T(8,128)S(1)} %fusion.8), kind=kOutput, calls=%fused_computation.19 | convolution fusion | flops 1344667648 | bytes 8912896 | tf_op jit(solution)/shard_map/dot_general | solution.py:15
  146.2 3.0 %fusion.27 = bf16[1,2048,256]{2,1,0:T(8,128)(2,1)} fusion(bf16[1280,4096]{1,0:T(8,128)(2,1)S(1)} %copy-done.3, f32[1280,256]{1,0:T(8,128)S(1)} %fusion.8, f32[1280,256]{1,0:T(8,128)S(1)} %fusion.2, f32[1280,256]{1,0:T(8,128)S(1)} %fusion.10), kind=kOutput, calls=%fused_computation.20 | convolution fusion | flops 1345978368 | bytes 10223616 | tf_op jit(solution)/shard_map/dot_general | solution.py:15
  149.2 35.9 %all-to-all-done.1 = bf16[32,16,4096]{2,1,0:T(8,128)(2,1)} async-done(((bf16[32,16,4096]{2,1,0:T(8,128)(2,1)}), bf16[32,16,4096]{2,1,0:T(8,128)(2,1)}, u32[]{:S(2)}, u32[]{:S(2)}) %all-to-all-start.1) | async-done | bytes 4194336 | tf_op jit(solution)/shard_map/all_to_all | solution.py:92
  185.1 3.4 %slice_reduce_fusion = (bf16[16,2048]{1,0:T(8,128)(2,1)}, bf16[16,2048]{1,0:T(8,128)(2,1)S(1)}) fusion(bf16[32,16,4096]{2,1,0:T(8,128)(2,1)} %all-to-all-done.1), kind=kLoop, calls=%fused_computation.26 | loop fusion | flops 2031616 | bytes 4325376 | tf_op jit(solution)/shard_map/reduce_sum | solution.py:108
  188.5 0.7 multiply_convert_fusion.12
  (9 shorter events, 0.1 us)
Async XLA Ops:
  7.2 107.5 %all-gather.3.cloned.1.call-start = ((), (), s32[]{:S(2)}) async-start(), calls=%async_computation.3 | async-start | bytes 4325376 | tf_op jit(solution)/shard_map/all_gather | solution.py:61
  10.3 121.5 %all-gather.5.cloned.1.call-start = ((), (), s32[]{:S(2)}) async-start(), calls=%async_computation.4 | async-start | bytes 10813440 | tf_op jit(solution)/shard_map/all_gather | solution.py:89
  14.0 25.8 %copy-start = (bf16[256,256]{1,0:T(8,128)(2,1)S(1)}, bf16[256,256]{1,0:T(8,128)(2,1)}, u32[]{:S(2)}) copy-start(bf16[256,256]{1,0:T(8,128)(2,1)} %param.13) | copy-start | bytes 393220
  14.0 25.8 %copy-start.1 = (bf16[256,256]{1,0:T(8,128)(2,1)S(1)}, bf16[256,256]{1,0:T(8,128)(2,1)}, u32[]{:S(2)}) copy-start(bf16[256,256]{1,0:T(8,128)(2,1)} %param.12) | copy-start | bytes 393220
  14.1 25.8 %copy-start.2 = (bf16[256,256]{1,0:T(8,128)(2,1)S(1)}, bf16[256,256]{1,0:T(8,128)(2,1)}, u32[]{:S(2)}) copy-start(bf16[256,256]{1,0:T(8,128)(2,1)} %param.11) | copy-start | bytes 393220
  114.7 3.2 %copy-start.4 = (bf16[512,4096]{1,0:T(8,128)(2,1)S(1)}, bf16[512,4096]{1,0:T(8,128)(2,1)}, u32[]{:S(2)}) copy-start(bf16[512,4096]{1,0:T(8,128)(2,1)} %all-gather.3.cloned.1.call-done) | copy-start | bytes 12582916
  124.2 60.9 %all-to-all-start.1 = ((bf16[32,16,4096]{2,1,0:T(8,128)(2,1)}), bf16[32,16,4096]{2,1,0:T(8,128)(2,1)}, u32[]{:S(2)}, u32[]{:S(2)}) async-start(bf16[32,16,4096]{2,1,0:T(8,128)(2,1)} %bitcast.11), calls=%async_computation.1 | async-start | bytes 8388608 | tf_op jit(solution)/shard_map/all_to_all | solution.py:92
  131.9 5.5 %copy-start.3 = (bf16[1280,4096]{1,0:T(8,128)(2,1)S(1)}, bf16[1280,4096]{1,0:T(8,128)(2,1)}, u32[]{:S(2)}) copy-start(bf16[1280,4096]{1,0:T(8,128)(2,1)} %all-gather.5.cloned.1.call-done) | copy-start | bytes 31457284
Sparse Core Ops, SparseCore 0:
  11.1 53.6 all-gather.2
  68.0 62.2 all-gather.4
